TPU v7x, 512 devices: a whole 4x4x16 slice. The times are simulated.
512 devices in a mesh: seq: 128 (over y, z, core), tp: 4 (over x).
Axes of the slice: x: 4, y: 4, z: 16, core: 2. Of those that a mesh axis runs over, the one named last changes fastest.
Arguments:
- tokens: bfloat16 [32768, 1280], P('seq'), may hold values from -45 to 45
- ln_gain: float32 [1280], replicated, may hold values from 0.6 to 10, as said below
- ln_bias: float32 [1280], replicated, may hold values from -3 to 3
- w_qkv: bfloat16 [3, 1280, 1280], P(None, None, 'tp'), may hold values from -0.15625 to 0.15625
- b_qkv: float32 [3, 1280], P(None, 'tp'), may hold values from -3 to 3
- w_out: bfloat16 [1280, 1280], P('tp'), may hold values from -0.15625 to 0.15625
- b_out: float32 [1280], replicated, may hold values from -3 to 3
- merge_gain: float32 [1280], replicated, may hold values from 0.25 to 1.75
- merge_bias: float32 [1280], replicated, may hold values from -3 to 3
- segments: int32 [8192], replicated, may hold values from 0 to 63, never falling along the last dimension, each value on 1 to 256 neighbouring positions
- owners: int32 [8192, 1], P('seq'), may hold values from 0 to 127; in each aligned block of 64 rows (0 to 63, 64 to 127, ...) at most 2 rows name the same one
Outputs:
- routed: bfloat16 [32768, 5120], P('seq', 'tp')
Inputs may be any that keep to these rules, and one draw needn't show every extreme that they name: `segments`: Non-decreasing along the rows; one image holds at most 256 merged rows, and some image holds exactly that many. `owners`: among the 64 merged rows of one device no owner is named more than 2 times, a bound that some block reaches. `ln_gain`: gains are positive, within 0.6 to 10.
All inputs are finite; a program needn't handle non-finite values.
Results may differ from a plain program's by a relative error of at most 0.024.
The roundings to bfloat16 on the way count: a program that leaves them out, or rounds other values in their place, can miss the bound.
Values may be sent and summed in bfloat16 or wider, within the bound.
No kernel may reach another device: no remote copies, remote signals or barrier semaphores. Data moves between devices by JAX's collectives and lax.ppermute only.
A program may use at most 64 MiB of HBM per device.

v0:
```python
import jax
import jax.numpy as jnp
from jax import lax
from jax.sharding import PartitionSpec as P

HEAD_DIM = 80
SPAN = 4


epsilon = 1e-06
masked_score = -1e30


def from_behind(value, axis, steps):
    count = lax.axis_size(axis)
    leading, last = (max(0, -steps), min(count, count - steps))
    return lax.ppermute(value, axis, [(source, source + steps) for source in range(leading, last)])


def layer_norm(values, gain_row, shift_row):
    center = jnp.mean(values, axis=-1, keepdims=True)
    centered = values - center
    spread = jnp.mean(centered * centered, axis=-1, keepdims=True)
    return centered * lax.rsqrt(spread + epsilon) * gain_row + shift_row


def per_device(
    tokens, ln_gain, ln_bias, w_qkv, b_qkv, w_out, b_out, merge_gain, merge_bias, segments, owners
):
    tok_dev = tokens.shape[0]
    model_width = tokens.shape[1]
    local_width = w_qkv.shape[2]
    local_heads = local_width // HEAD_DIM
    seq_count = lax.axis_size("seq")
    seq_index = lax.axis_index("seq")
    row_start = seq_index * tok_dev
    reach_rows = SPAN * tok_dev
    scale_factor = HEAD_DIM ** (-0.5)
    normed = layer_norm(tokens.astype(jnp.float32), ln_gain, ln_bias).astype(jnp.bfloat16)
    query = (jnp.dot(normed, w_qkv[0], preferred_element_type=jnp.float32) + b_qkv[0]).astype(
        jnp.bfloat16
    )
    key_rows = (jnp.dot(normed, w_qkv[1], preferred_element_type=jnp.float32) + b_qkv[1]).astype(
        jnp.bfloat16
    )
    value_rows = (jnp.dot(normed, w_qkv[2], preferred_element_type=jnp.float32) + b_qkv[2]).astype(
        jnp.bfloat16
    )
    key_value = jnp.concatenate([key_rows, value_rows], axis=1)
    token_segment = jnp.repeat(segments, 4)
    padding = jnp.full((reach_rows,), -1, jnp.int32)
    padded_segment = jnp.concatenate([padding, token_segment, padding])
    query_segment = lax.dynamic_slice_in_dim(token_segment, row_start, tok_dev)
    query_heads = query.reshape(tok_dev, local_heads, HEAD_DIM)

    def segment_window(key_start, length):
        return lax.dynamic_slice_in_dim(padded_segment, key_start + reach_rows, length)

    def block_scores(block, key_segment):
        key_heads = block[:, :local_width].reshape(-1, local_heads, HEAD_DIM)
        value_heads = block[:, local_width:].reshape(-1, local_heads, HEAD_DIM)
        scores = (
            jnp.einsum("qhd,khd->hqk", query_heads, key_heads, preferred_element_type=jnp.float32)
            * scale_factor
        )
        allowed = query_segment[:, None] == key_segment[None, :]
        return (jnp.where(allowed[None], scores, masked_score), value_heads)

    def absorb(state, block, key_segment):
        row_top, totals, summed = state
        scores, value_heads = block_scores(block, key_segment)
        new_top = jnp.maximum(row_top, jnp.max(scores, axis=-1, keepdims=True))
        factor = jnp.exp(row_top - new_top)
        weights = jnp.exp(scores - new_top)
        totals = totals * factor + jnp.sum(weights, axis=-1, keepdims=True)
        summed = summed * factor + jnp.einsum(
            "hqk,khd->hqd",
            weights.astype(jnp.bfloat16),
            value_heads,
            preferred_element_type=jnp.float32,
        )
        return (new_top, totals, summed)

    def absorb_remote(state, block, key_start):
        key_segment = segment_window(key_start, tok_dev)
        return absorb(state, block, key_segment)

    start_state = (
        jnp.full((local_heads, tok_dev, 1), masked_score, jnp.float32),
        jnp.zeros((local_heads, tok_dev, 1), jnp.float32),
        jnp.zeros((local_heads, tok_dev, HEAD_DIM), jnp.float32),
    )
    state = absorb(start_state, key_value, query_segment)
    below = key_value
    above = key_value
    for distance in range(1, SPAN + 1):
        below = from_behind(below, "seq", 1)
        above = from_behind(above, "seq", -1)
        state = absorb_remote(state, below, row_start - distance * tok_dev)
        state = absorb_remote(state, above, row_start + distance * tok_dev)
    row_top, totals, summed = state
    attended = (
        jnp.transpose(summed / totals, (1, 0, 2)).reshape(tok_dev, local_width).astype(jnp.bfloat16)
    )
    tp_index = lax.axis_index("tp")
    quarter = tok_dev // 4
    partial_out = jnp.dot(attended, w_out, preferred_element_type=jnp.float32)
    full_out = lax.psum(partial_out.astype(jnp.bfloat16), "tp").astype(jnp.float32)
    residual = tokens.astype(jnp.float32) + full_out + b_out
    own_rows = lax.dynamic_index_in_dim(
        residual.reshape(quarter, 4, model_width), tp_index, 1, keepdims=False
    )
    merged_rows = layer_norm(own_rows, merge_gain, merge_bias).astype(jnp.bfloat16)
    owner_rows = owners[:, 0]
    capacity = max(2, 2 * quarter // seq_count)
    owner_table = (owner_rows[:, None] == jnp.arange(seq_count, dtype=jnp.int32)[None, :]).astype(
        jnp.int32
    )
    earlier = jnp.cumsum(owner_table, axis=0) - owner_table
    row_slot = jnp.sum(earlier * owner_table, axis=1)
    target_row = owner_rows * capacity + row_slot
    placing = (
        jnp.arange(seq_count * capacity, dtype=jnp.int32)[:, None] == target_row[None, :]
    ).astype(jnp.bfloat16)
    outgoing = jnp.dot(placing, merged_rows, preferred_element_type=jnp.float32).astype(
        jnp.bfloat16
    )
    return lax.all_to_all(outgoing, "seq", split_axis=0, concat_axis=0, tiled=True)


def solution(mesh):
    placed = (
        P("seq", None),
        P(),
        P(),
        P(None, None, "tp"),
        P(None, "tp"),
        P("tp", None),
        P(),
        P(),
        P(),
        P(),
        P("seq", None),
    )
    return jax.shard_map(
        per_device, mesh=mesh, in_specs=placed, out_specs=P("seq", "tp"), check_vma=False
    )
```

profile of v0, /device:TPU:32, one launch (start us, length us, event | category | flops | bytes accessed | tf_op | source)
XLA Modules:
  0.0 208.1 jit_solution(2838358114084987411)
XLA Ops:
  6.6 1.4 convert_reduce_fusion
  8.0 1.4 fusion.11
  9.4 1.7 fusion.36
  11.1 1.7 fusion.37
  12.8 1.9 collective-permute-start.1
  14.8 2.4 %collective-permute-start = (bf16[256,640]{0,1:T(8,128)(2,1)S(1)}, bf16[256,640]{0,1:T(8,128)(2,1)S(1)}, u32[]{:S(2)}, u32[]{:S(2)}) collective-permute-start(bf16[256,640]{0,1:T(8,128)(2,1)S(1)} %pad_maximum_fusion), channel_id=1, source_target_pairs={{0,4},{4,8},{8,12},{12,16},{16,20},{20,24},{24,28},{28,32},{32,36}... | collective-permute-start | bytes 983048 | tf_op jit(solution)/shard_map/ppermute | solution.py:17
  17.2 1.7 fusion.35
  18.9 5.0 %broadcast_in_dim.133 = s32[8192,4]{1,0:T(8,128)} broadcast(s32[8192]{0:T(1024)S(1)} %copy-done.2), dimensions={0} | broadcast | bytes 163840 | tf_op jit(solution)/shard_map/broadcast_in_dim | solution.py:50
  23.9 4.9 %reshape.637 = s32[32768]{0:T(1024)S(1)} reshape(s32[8192,4]{1,0:T(8,128)} %broadcast_in_dim.133) | data formatting | bytes 262144 | tf_op jit(solution)/shard_map/reshape | solution.py:50
  29.0 0.5 broadcast_compare_fusion.6
  29.5 0.4 fusion.123
  29.9 7.0 %collective-permute-start.3 = (bf16[256,640]{0,1:T(8,128)(2,1)S(1)}, bf16[256,640]{0,1:T(8,128)(2,1)S(1)}, u32[]{:S(2)}, u32[]{:S(2)}) collective-permute-start(bf16[256,640]{0,1:T(8,128)(2,1)S(1)} %collective-permute-done.1), channel_id=1, source_target_pairs={{4,0},{8,4},{12,8},{16,12},{20,16},{24,20},{28,24},{32,28},{36,32}... | collective-permute-start | bytes 983048 | tf_op jit(solution)/shard_map/ppermute | solution.py:17
  36.9 0.4 fusion.121
  37.3 1.9 collective-permute-start.2
  39.2 0.4 fusion.122
  39.6 6.1 %collective-permute-done.2 = bf16[256,640]{0,1:T(8,128)(2,1)S(1)} collective-permute-done((bf16[256,640]{0,1:T(8,128)(2,1)S(1)}, bf16[256,640]{0,1:T(8,128)(2,1)S(1)}, u32[]{:S(2)}, u32[]{:S(2)}) %collective-permute-start.2) | collective-permute-done | bytes 327712 | tf_op jit(solution)/shard_map/ppermute | solution.py:17
  45.7 1.9 collective-permute-start.4
  47.6 0.4 fusion.120
  48.1 0.4 fusion.119
  48.4 3.6 %collective-permute-start.5 = (bf16[256,640]{0,1:T(8,128)(2,1)S(1)}, bf16[256,640]{0,1:T(8,128)(2,1)S(1)}, u32[]{:S(2)}, u32[]{:S(2)}) collective-permute-start(bf16[256,640]{0,1:T(8,128)(2,1)S(1)} %collective-permute-done.3), channel_id=1, source_target_pairs={{4,0},{8,4},{12,8},{16,12},{20,16},{24,20},{28,24},{32,28},{36,32}... | collective-permute-start | bytes 983048 | tf_op jit(solution)/shard_map/ppermute | solution.py:17
  52.1 2.0 collective-permute-done.4
  54.1 1.9 collective-permute-start.6
  56.1 0.4 fusion.118
  56.7 4.0 %collective-permute-start.7 = (bf16[256,640]{0,1:T(8,128)(2,1)S(1)}, bf16[256,640]{0,1:T(8,128)(2,1)S(1)}, u32[]{:S(2)}, u32[]{:S(2)}) collective-permute-start(bf16[256,640]{0,1:T(8,128)(2,1)S(1)} %collective-permute-done.5), channel_id=1, source_target_pairs={{4,0},{8,4},{12,8},{16,12},{20,16},{24,20},{28,24},{32,28},{36,32}... | collective-permute-start | bytes 983048 | tf_op jit(solution)/shard_map/ppermute | solution.py:17
  60.7 0.4 fusion.117
  61.1 1.4 collective-permute-done.6
  62.5 0.4 fusion.116
  62.9 2.1 %collective-permute-done.7 = bf16[256,640]{0,1:T(8,128)(2,1)S(1)} collective-permute-done((bf16[256,640]{0,1:T(8,128)(2,1)S(1)}, bf16[256,640]{0,1:T(8,128)(2,1)S(1)}, u32[]{:S(2)}, u32[]{:S(2)}) %collective-permute-start.7) | collective-permute-done | bytes 327712 | tf_op jit(solution)/shard_map/ppermute | solution.py:17
  65.1 0.4 fusion.115
  65.7 0.3 fusion.50
  66.0 0.3 fusion.46
  66.6 0.3 fusion.38
  66.9 0.3 fusion.25
  67.2 0.3 fusion.26
  67.6 0.3 fusion.27
  67.9 0.3 fusion.28
  68.5 0.3 fusion.30
  68.8 0.3 fusion.31
  69.1 0.3 fusion.32
  69.4 0.3 fusion.34
  69.7 1.4 convolution_convert_fusion.1
  71.5 66.9 %all-reduce.2.cloned.1.call-done = bf16[256,1280]{1,0:T(8,128)(2,1)} async-done(((bf16[256,1280]{1,0:T(8,128)(2,1)}), bf16[256,1280]{1,0:T(8,128)(2,1)}) %all-reduce.2.cloned.1.call-update) | async-done | bytes 655376 | tf_op jit(solution)/shard_map/psum | solution.py:108
  138.5 1.3 fusion.15
  139.8 1.4 reshape.657
  141.2 1.9 fusion.102
  143.3 0.4 convolution_convert_fusion
  144.0 56.2 %all_to_all.12 = bf16[128,2,1280]{2,1,0:T(2,128)(2,1)S(1)} all-to-all(bf16[128,2,1280]{2,1,0:T(2,128)(2,1)S(1)} %all_to_all.8), channel_id=1, replica_groups=mesh['seq'=128,'tp'=4] {'seq'}, dimensions={0} | all-to-all | bytes 1310720 | tf_op jit(solution)/shard_map/all_to_all | solution.py:128
  200.2 1.1 all_to_all.10
  (56 shorter events, 2.4 us)
Async XLA Ops:
  6.5 63.2 %copy-start = (bf16[320,1280]{1,0:T(8,128)(2,1)S(1)}, bf16[320,1280]{1,0:T(8,128)(2,1)}, u32[]{:S(2)}) copy-start(bf16[320,1280]{1,0:T(8,128)(2,1)} %param.16) | copy-start | bytes 2457604
  6.5 2.9 %copy-start.1 = (bf16[256,1280]{1,0:T(8,128)(2,1)S(1)}, bf16[256,1280]{1,0:T(8,128)(2,1)}, u32[]{:S(2)}) copy-start(bf16[256,1280]{1,0:T(8,128)(2,1)} %param.11) | copy-start | bytes 1966084
  6.5 2.8 %copy-start.6 = (f32[3,320]{1,0:T(4,128)S(1)}, f32[3,320]{1,0:T(4,128)}, u32[]{:S(2)}) copy-start(f32[3,320]{1,0:T(4,128)} %param.15) | copy-start | bytes 11524
  6.5 2.9 %copy-start.8 = (f32[1280]{0:T(1024)S(1)}, f32[1280]{0:T(1024)}, u32[]{:S(2)}) copy-start(f32[1280]{0:T(1024)} %param.13) | copy-start | bytes 15364
  6.5 2.9 %copy-start.9 = (f32[1280]{0:T(1024)S(1)}, f32[1280]{0:T(1024)}, u32[]{:S(2)}) copy-start(f32[1280]{0:T(1024)} %param.12) | copy-start | bytes 15364
  6.5 131.9 %all-reduce.2.cloned.1.call-start = ((), (), s32[]{:S(2)}) async-start(), calls=%async_computation.1 | async-start | bytes 1310720 | tf_op jit(solution)/shard_map/psum | solution.py:108
  12.8 17.0 %collective-permute-start.1 = (bf16[256,640]{0,1:T(8,128)(2,1)S(1)}, bf16[256,640]{0,1:T(8,128)(2,1)S(1)}, u32[]{:S(2)}, u32[]{:S(2)}) collective-permute-start(bf16[256,640]{0,1:T(8,128)(2,1)S(1)} %pad_maximum_fusion), channel_id=1, source_target_pairs={{4,0},{8,4},{12,8},{16,12},{20,16},{24,20},{28,24},{32,28},{36,32}... | collective-permute-start | bytes 983048 | tf_op jit(solution)/shard_map/ppermute | solution.py:17
  14.8 22.5 %collective-permute-start = (bf16[256,640]{0,1:T(8,128)(2,1)S(1)}, bf16[256,640]{0,1:T(8,128)(2,1)S(1)}, u32[]{:S(2)}, u32[]{:S(2)}) collective-permute-start(bf16[256,640]{0,1:T(8,128)(2,1)S(1)} %pad_maximum_fusion), channel_id=1, source_target_pairs={{0,4},{4,8},{8,12},{12,16},{16,20},{20,24},{24,28},{28,32},{32,36}... | collective-permute-start | bytes 983048 | tf_op jit(solution)/shard_map/ppermute | solution.py:17
  17.2 1.7 copy-start.2
  29.9 18.1 %collective-permute-start.3 = (bf16[256,640]{0,1:T(8,128)(2,1)S(1)}, bf16[256,640]{0,1:T(8,128)(2,1)S(1)}, u32[]{:S(2)}, u32[]{:S(2)}) collective-permute-start(bf16[256,640]{0,1:T(8,128)(2,1)S(1)} %collective-permute-done.1), channel_id=1, source_target_pairs={{4,0},{8,4},{12,8},{16,12},{20,16},{24,20},{28,24},{32,28},{36,32}... | collective-permute-start | bytes 983048 | tf_op jit(solution)/shard_map/ppermute | solution.py:17
  37.3 8.4 %collective-permute-start.2 = (bf16[256,640]{0,1:T(8,128)(2,1)S(1)}, bf16[256,640]{0,1:T(8,128)(2,1)S(1)}, u32[]{:S(2)}, u32[]{:S(2)}) collective-permute-start(bf16[256,640]{0,1:T(8,128)(2,1)S(1)} %collective-permute-done), channel_id=1, source_target_pairs={{0,4},{4,8},{8,12},{12,16},{16,20},{20,24},{24,28},{28,32},{32,36}... | collective-permute-start | bytes 983048 | tf_op jit(solution)/shard_map/ppermute | solution.py:17
  45.7 8.4 %collective-permute-start.4 = (bf16[256,640]{0,1:T(8,128)(2,1)S(1)}, bf16[256,640]{0,1:T(8,128)(2,1)S(1)}, u32[]{:S(2)}, u32[]{:S(2)}) collective-permute-start(bf16[256,640]{0,1:T(8,128)(2,1)S(1)} %collective-permute-done.2), channel_id=1, source_target_pairs={{0,4},{4,8},{8,12},{12,16},{16,20},{20,24},{24,28},{28,32},{32,36}... | collective-permute-start | bytes 983048 | tf_op jit(solution)/shard_map/ppermute | solution.py:17
  48.4 8.2 %collective-permute-start.5 = (bf16[256,640]{0,1:T(8,128)(2,1)S(1)}, bf16[256,640]{0,1:T(8,128)(2,1)S(1)}, u32[]{:S(2)}, u32[]{:S(2)}) collective-permute-start(bf16[256,640]{0,1:T(8,128)(2,1)S(1)} %collective-permute-done.3), channel_id=1, source_target_pairs={{4,0},{8,4},{12,8},{16,12},{20,16},{24,20},{28,24},{32,28},{36,32}... | collective-permute-start | bytes 983048 | tf_op jit(solution)/shard_map/ppermute | solution.py:17
  54.1 8.4 %collective-permute-start.6 = (bf16[256,640]{0,1:T(8,128)(2,1)S(1)}, bf16[256,640]{0,1:T(8,128)(2,1)S(1)}, u32[]{:S(2)}, u32[]{:S(2)}) collective-permute-start(bf16[256,640]{0,1:T(8,128)(2,1)S(1)} %collective-permute-done.4), channel_id=1, source_target_pairs={{0,4},{4,8},{8,12},{12,16},{16,20},{20,24},{24,28},{28,32},{32,36}... | collective-permute-start | bytes 983048 | tf_op jit(solution)/shard_map/ppermute | solution.py:17
  56.7 8.4 %collective-permute-start.7 = (bf16[256,640]{0,1:T(8,128)(2,1)S(1)}, bf16[256,640]{0,1:T(8,128)(2,1)S(1)}, u32[]{:S(2)}, u32[]{:S(2)}) collective-permute-start(bf16[256,640]{0,1:T(8,128)(2,1)S(1)} %collective-permute-done.5), channel_id=1, source_target_pairs={{4,0},{8,4},{12,8},{16,12},{20,16},{24,20},{28,24},{32,28},{36,32}... | collective-permute-start | bytes 983048 | tf_op jit(solution)/shard_map/ppermute | solution.py:17
  69.7 1.4 copy-start.7
  69.7 68.7 %copy-start.3 = (f32[1280]{0:T(1024)S(1)}, f32[1280]{0:T(1024)}, u32[]{:S(2)}) copy-start(f32[1280]{0:T(1024)} %param.17) | copy-start | bytes 15364
  139.7 3.6 %copy-start.4 = (f32[1280]{0:T(1024)S(1)}, f32[1280]{0:T(1024)}, u32[]{:S(2)}) copy-start(f32[1280]{0:T(1024)} %param.19) | copy-start | bytes 15364
  139.7 3.6 %copy-start.5 = (f32[1280]{0:T(1024)S(1)}, f32[1280]{0:T(1024)}, u32[]{:S(2)}) copy-start(f32[1280]{0:T(1024)} %param.18) | copy-start | bytes 15364
Sparse Core Ops, SparseCore 0:
  71.3 67.1 all-reduce.1
where the time goes:
time: 209 us; the launch traced here: 208 us
  waiting for transfers between devices  78.8 us (38%)
  blocking collectives  56.2 us (27%)
  starting transfers between devices  24.8 us (12%)
  between operations  13.8 us (7%)
  local copies, waits for them, and re-layouts  13.1 us (6%)
  matrix products  13 us (6%)
  other arithmetic  8.5 us (4%)
    psum x1, waiting for transfers between devices, per_device(): lax.psum(partial_out.astype(jnp.bfloat16), 'tp').astype(jnp.float32)  66.9 us
    all_to_all x1, blocking collectives, per_device(): lax.all_to_all(outgoing, 'seq', split_axis=0, concat_axis=0, tiled=True)  56.2 us
    ppermute x8, starting transfers between devices, from_behind(): lax.ppermute(value, axis, [(source, source + steps) for source in range(l...  24.7 us
    ppermute x8, waiting for transfers between devices, from_behind(): lax.ppermute(value, axis, [(source, source + steps) for source in range(l...  11.9 us
    broadcast_in_dim x1, local copies, waits for them, and re-layouts, per_device(): token_segment = jnp.repeat(segments, 4)  5.02 us
    reshape x1, local copies, waits for them, and re-layouts, per_device(): token_segment = jnp.repeat(segments, 4)  4.85 us
  transfers between devices with their start and end apart: 9, of which 6 were waited for; matrix products, arithmetic and copies ran while one was open for 8% of the time, Pallas kernels for 0%

commit v1 on v0

--- a/solution.py
+++ b/solution.py
@@ -47,14 +47,17 @@
         jnp.bfloat16
     )
     key_value = jnp.concatenate([key_rows, value_rows], axis=1)
-    token_segment = jnp.repeat(segments, 4)
-    padding = jnp.full((reach_rows,), -1, jnp.int32)
-    padded_segment = jnp.concatenate([padding, token_segment, padding])
-    query_segment = lax.dynamic_slice_in_dim(token_segment, row_start, tok_dev)
-    query_heads = query.reshape(tok_dev, local_heads, HEAD_DIM)
+    group_rows = tok_dev // 4
+    reach_groups = SPAN * group_rows
+    padding = jnp.full((reach_groups,), -1, jnp.int32)
+    padded_segment = jnp.concatenate([padding, segments, padding])
 
     def segment_window(key_start, length):
-        return lax.dynamic_slice_in_dim(padded_segment, key_start + reach_rows, length)
+        groups = lax.dynamic_slice_in_dim(padded_segment, key_start // 4 + reach_groups, length // 4)
+        return jnp.repeat(groups, 4)
+
+    query_segment = segment_window(row_start, tok_dev)
+    query_heads = query.reshape(tok_dev, local_heads, HEAD_DIM)
 
     def block_scores(block, key_segment):
         key_heads = block[:, :local_width].reshape(-1, local_heads, HEAD_DIM)
@@ -99,17 +102,19 @@
         state = absorb_remote(state, below, row_start - distance * tok_dev)
         state = absorb_remote(state, above, row_start + distance * tok_dev)
     row_top, totals, summed = state
-    attended = (
-        jnp.transpose(summed / totals, (1, 0, 2)).reshape(tok_dev, local_width).astype(jnp.bfloat16)
-    )
     tp_index = lax.axis_index("tp")
     quarter = tok_dev // 4
-    partial_out = jnp.dot(attended, w_out, preferred_element_type=jnp.float32)
-    full_out = lax.psum(partial_out.astype(jnp.bfloat16), "tp").astype(jnp.float32)
-    residual = tokens.astype(jnp.float32) + full_out + b_out
-    own_rows = lax.dynamic_index_in_dim(
-        residual.reshape(quarter, 4, model_width), tp_index, 1, keepdims=False
+    by_token = (summed / totals).reshape(local_heads, quarter, 4, HEAD_DIM)
+    attended = jnp.transpose(by_token, (2, 1, 0, 3)).reshape(4, quarter, local_width).astype(jnp.bfloat16)
+    head_term = jnp.einsum(
+        "tgc,cd->tgd", attended, w_out, preferred_element_type=jnp.float32
+    ).astype(jnp.bfloat16)
+    head_terms = lax.all_to_all(head_term, "tp", split_axis=0, concat_axis=0, tiled=True)
+    head_total = jnp.sum(head_terms.astype(jnp.float32), axis=0)
+    own_tokens = lax.dynamic_index_in_dim(
+        tokens.reshape(quarter, 4, model_width), tp_index, 1, keepdims=False
     )
+    own_rows = own_tokens.astype(jnp.float32) + head_total + b_out
     merged_rows = layer_norm(own_rows, merge_gain, merge_bias).astype(jnp.bfloat16)
     owner_rows = owners[:, 0]
     capacity = max(2, 2 * quarter // seq_count)

time: 209 us -> 137 us (0.66)
  waiting for transfers between devices: 78.8 us -> 21.5 us
  between operations: 13.8 us -> 0.74 us
  local copies, waits for them, and re-layouts: 13.1 us -> 6.99 us
  blocking collectives: 56.2 us -> 59 us
  starting transfers between devices: 24.8 us -> 27.5 us
    psum x1 -> x0, waiting for transfers between devices: 66.9 us -> none  [per_device(): lax.psum(partial_out.astype(jnp.bfloat16), 'tp').astype(jnp.float32)]
    all_to_all x0 -> x1, waiting for transfers between devices: none -> 10.2 us  [per_device(): lax.all_to_all(head_term, 'tp', split_axis=0, concat_axis=0, tiled=True)]
    reshape x2 -> x1, local copies, waits for them, and re-layouts: 6.3 us -> 0.15 us  [per_device(): tokens.reshape(quarter, 4, model_width)]
    broadcast_in_dim x2 -> x10, local copies, waits for them, and re-layouts: 5.02 us -> 0.65 us  [the longest x9 0.64 us: segment_window(): return jnp.repeat(groups, 4)]
    eq x0 -> x9, local copies, waits for them, and re-layouts: none -> 3.88 us  [block_scores(): allowed = query_segment[:, None] == key_segment[None, :]]
    all_to_all x0 -> x1, starting transfers between devices: none -> 3.66 us  [per_device(): lax.all_to_all(head_term, 'tp', split_axis=0, concat_axis=0, tiled=True)]
    all_to_all x1, blocking collectives: 56.2 us -> 59 us  [per_device(): lax.all_to_all(outgoing, 'seq', split_axis=0, concat_axis=0, tiled=True)]
  transfers between devices with their start and end apart: 9 -> 9, of which waited for: 6 -> 6; matrix products, arithmetic and copies ran while one was open for 8% -> 9% of each run, Pallas kernels for 0% -> 0%
where the time goes in v1:
time: 137 us
  blocking collectives  59 us (43%)
  starting transfers between devices  27.5 us (20%)
  waiting for transfers between devices  21.5 us (16%)
  matrix products  12.9 us (9%)
  other arithmetic  7.84 us (6%)
  local copies, waits for them, and re-layouts  6.99 us (5%)
    all_to_all x1, blocking collectives, per_device(): lax.all_to_all(outgoing, 'seq', split_axis=0, concat_axis=0, tiled=True)  59 us
    ppermute x8, starting transfers between devices, from_behind(): lax.ppermute(value, axis, [(source, source + steps) for source in range(l...  23.9 us
    ppermute x8, waiting for transfers between devices, from_behind(): lax.ppermute(value, axis, [(source, source + steps) for source in range(l...  11.3 us
    all_to_all x1, waiting for transfers between devices, per_device(): lax.all_to_all(head_term, 'tp', split_axis=0, concat_axis=0, tiled=True)  10.2 us
    eq x9, local copies, waits for them, and re-layouts, block_scores(): allowed = query_segment[:, None] == key_segment[None, :]  3.88 us
    all_to_all x1, starting transfers between devices, per_device(): lax.all_to_all(head_term, 'tp', split_axis=0, concat_axis=0, tiled=True)  3.66 us
    dot_general x9, matrix products, block_scores(): jnp.einsum('qhd,khd->hqk', query_heads, key_heads, preferred_element_type...  3.4 us
  transfers between devices with their start and end apart: 9, of which 6 were waited for; matrix products, arithmetic and copies ran while one was open for 9% of the time, Pallas kernels for 0%

profile of v1, /device:TPU:32, one launch (start us, length us, event | category | flops | bytes accessed | tf_op | source)
XLA Modules:
  0.0 136.6 jit_solution(16122522062217633846)
XLA Ops:
  0.0 1.4 convert_reduce_fusion
  1.4 1.4 %fusion.11 = f32[256]{0:T(256)S(1)} fusion(bf16[256,1280]{1,0:T(8,128)(2,1)} %param.11, f32[256]{0:T(256)S(1)} %broadcast_multiply_fusion), kind=kLoop, calls=%fused_computation.24 | loop fusion | flops 1310464 | bytes 657408 | tf_op jit(solution)/shard_map/reduce_sum | solution.py:23
  2.9 1.7 %fusion.30 = bf16[256,320]{0,1:T(8,128)(2,1)S(1)} fusion(bf16[3,1280,320]{1,2,0:T(8,128)(2,1)} %param.14, f32[320]{0:T(512)S(1)} %get-tuple-element.7, bf16[256,1280]{1,0:T(8,128)(2,1)S(1)} %copy-done.1, f32[1280]{0:T(1024)S(1)} %copy-done.15, f32[1280]{0:T(1024)S(1)} %copy-done.16, f32[256]{0:T(256)S(1)} %add_rsqrt_fusion, f32[256]{0:T(256)S(1)} %broadcast_multiply_fusion), kind=kOutput, calls=%fused_computation.52 | convolution fusion | flops 211845120 | bytes 1651968 | tf_op jit(solution)/shard_map/dot_general | solution.py:43
  4.6 1.7 %fusion.31 = bf16[256,320]{0,1:T(8,128)(2,1)S(1)} fusion(bf16[3,1280,320]{1,2,0:T(8,128)(2,1)} %param.14, f32[320]{0:T(512)S(1)} %get-tuple-element.6, bf16[256,1280]{1,0:T(8,128)(2,1)S(1)} %copy-done.1, f32[1280]{0:T(1024)S(1)} %copy-done.15, f32[1280]{0:T(1024)S(1)} %copy-done.16, f32[256]{0:T(256)S(1)} %add_rsqrt_fusion, f32[256]{0:T(256)S(1)} %broadcast_multiply_fusion), kind=kOutput, calls=%fused_computation.53 | convolution fusion | flops 211845120 | bytes 1651968 | tf_op jit(solution)/shard_map/dot_general | solution.py:46
  6.3 1.9 %collective-permute-start = (bf16[256,640]{0,1:T(8,128)(2,1)S(1)}, bf16[256,640]{0,1:T(8,128)(2,1)S(1)}, u32[]{:S(2)}, u32[]{:S(2)}) collective-permute-start(bf16[256,640]{0,1:T(8,128)(2,1)S(1)} %pad_maximum_fusion), channel_id=1, source_target_pairs={{0,4},{4,8},{8,12},{12,16},{16,20},{20,24},{24,28},{28,32},{32,36}... | collective-permute-start | bytes 983048 | tf_op jit(solution)/shard_map/ppermute | solution.py:17
  8.2 3.6 %collective-permute-start.1 = (bf16[256,640]{0,1:T(8,128)(2,1)S(1)}, bf16[256,640]{0,1:T(8,128)(2,1)S(1)}, u32[]{:S(2)}, u32[]{:S(2)}) collective-permute-start(bf16[256,640]{0,1:T(8,128)(2,1)S(1)} %pad_maximum_fusion), channel_id=1, source_target_pairs={{4,0},{8,4},{12,8},{16,12},{20,16},{24,20},{28,24},{32,28},{36,32}... | collective-permute-start | bytes 983048 | tf_op jit(solution)/shard_map/ppermute | solution.py:17
  13.0 0.7 eq.200
  13.8 0.7 eq.203
  14.5 0.7 eq.206
  15.3 0.7 eq.209
  16.0 0.7 eq.212
  16.8 1.7 %fusion.29 = bf16[256,320]{0,1:T(8,128)(2,1)S(1)} fusion(bf16[3,1280,320]{1,2,0:T(8,128)(2,1)} %param.14, f32[320]{0:T(512)S(1)} %get-tuple-element.5, bf16[256,1280]{1,0:T(8,128)(2,1)S(1)} %copy-done.1, f32[1280]{0:T(1024)S(1)} %copy-done.15, f32[1280]{0:T(1024)S(1)} %copy-done.16, f32[256]{0:T(256)S(1)} %add_rsqrt_fusion, f32[256]{0:T(256)S(1)} %broadcast_multiply_fusion), kind=kOutput, calls=%fused_computation.51 | convolution fusion | flops 211845120 | bytes 1651968 | tf_op jit(solution)/shard_map/dot_general | solution.py:40
  18.5 0.5 broadcast_compare_fusion.8
  19.0 0.7 fusion.85
  19.7 1.4 %reduce_window_sum.11 = s32[64,128]{1,0:T(8,128)} reduce-window(s32[64,128]{1,0:T(8,128)} %fusion.85, s32[]{:T(128)} %constant.118.clone.1), window={size=64x1 pad=63_0x0_0}, to_apply=%region_0.0 | reduce-window | flops 516096 | bytes 65540 | tf_op jit(solution)/shard_map/jit(cumsum)/reduce_window_sum | solution.py:124
  21.2 0.4 fusion.111
  21.6 5.1 %collective-permute-start.3 = (bf16[256,640]{0,1:T(8,128)(2,1)S(1)}, bf16[256,640]{0,1:T(8,128)(2,1)S(1)}, u32[]{:S(2)}, u32[]{:S(2)}) collective-permute-start(bf16[256,640]{0,1:T(8,128)(2,1)S(1)} %collective-permute-done.1), channel_id=1, source_target_pairs={{4,0},{8,4},{12,8},{16,12},{20,16},{24,20},{28,24},{32,28},{36,32}... | collective-permute-start | bytes 983048 | tf_op jit(solution)/shard_map/ppermute | solution.py:17
  26.7 0.4 fusion.109
  27.1 1.9 %collective-permute-start.2 = (bf16[256,640]{0,1:T(8,128)(2,1)S(1)}, bf16[256,640]{0,1:T(8,128)(2,1)S(1)}, u32[]{:S(2)}, u32[]{:S(2)}) collective-permute-start(bf16[256,640]{0,1:T(8,128)(2,1)S(1)} %collective-permute-done), channel_id=1, source_target_pairs={{0,4},{4,8},{8,12},{12,16},{16,20},{20,24},{24,28},{28,32},{32,36}... | collective-permute-start | bytes 983048 | tf_op jit(solution)/shard_map/ppermute | solution.py:17
  29.1 0.4 fusion.110
  29.5 1.8 %collective-permute-done.3 = bf16[256,640]{0,1:T(8,128)(2,1)S(1)} collective-permute-done((bf16[256,640]{0,1:T(8,128)(2,1)S(1)}, bf16[256,640]{0,1:T(8,128)(2,1)S(1)}, u32[]{:S(2)}, u32[]{:S(2)}) %collective-permute-start.3) | collective-permute-done | bytes 327712 | tf_op jit(solution)/shard_map/ppermute | solution.py:17
  31.3 3.8 %collective-permute-start.5 = (bf16[256,640]{0,1:T(8,128)(2,1)S(1)}, bf16[256,640]{0,1:T(8,128)(2,1)S(1)}, u32[]{:S(2)}, u32[]{:S(2)}) collective-permute-start(bf16[256,640]{0,1:T(8,128)(2,1)S(1)} %collective-permute-done.3), channel_id=1, source_target_pairs={{4,0},{8,4},{12,8},{16,12},{20,16},{24,20},{28,24},{32,28},{36,32}... | collective-permute-start | bytes 983048 | tf_op jit(solution)/shard_map/ppermute | solution.py:17
  35.1 0.4 fusion.107
  35.5 1.9 %collective-permute-start.4 = (bf16[256,640]{0,1:T(8,128)(2,1)S(1)}, bf16[256,640]{0,1:T(8,128)(2,1)S(1)}, u32[]{:S(2)}, u32[]{:S(2)}) collective-permute-start(bf16[256,640]{0,1:T(8,128)(2,1)S(1)} %collective-permute-done.2), channel_id=1, source_target_pairs={{0,4},{4,8},{8,12},{12,16},{16,20},{20,24},{24,28},{28,32},{32,36}... | collective-permute-start | bytes 983048 | tf_op jit(solution)/shard_map/ppermute | solution.py:17
  37.5 0.4 fusion.108
  37.8 1.8 %collective-permute-done.5 = bf16[256,640]{0,1:T(8,128)(2,1)S(1)} collective-permute-done((bf16[256,640]{0,1:T(8,128)(2,1)S(1)}, bf16[256,640]{0,1:T(8,128)(2,1)S(1)}, u32[]{:S(2)}, u32[]{:S(2)}) %collective-permute-start.5) | collective-permute-done | bytes 327712 | tf_op jit(solution)/shard_map/ppermute | solution.py:17
  39.7 0.4 fusion.105
  40.1 3.8 %collective-permute-done.4 = bf16[256,640]{0,1:T(8,128)(2,1)S(1)} collective-permute-done((bf16[256,640]{0,1:T(8,128)(2,1)S(1)}, bf16[256,640]{0,1:T(8,128)(2,1)S(1)}, u32[]{:S(2)}, u32[]{:S(2)}) %collective-permute-start.4) | collective-permute-done | bytes 327712 | tf_op jit(solution)/shard_map/ppermute | solution.py:17
  43.9 1.9 %collective-permute-start.6 = (bf16[256,640]{0,1:T(8,128)(2,1)S(1)}, bf16[256,640]{0,1:T(8,128)(2,1)S(1)}, u32[]{:S(2)}, u32[]{:S(2)}) collective-permute-start(bf16[256,640]{0,1:T(8,128)(2,1)S(1)} %collective-permute-done.4), channel_id=1, source_target_pairs={{0,4},{4,8},{8,12},{12,16},{16,20},{20,24},{24,28},{28,32},{32,36}... | collective-permute-start | bytes 983048 | tf_op jit(solution)/shard_map/ppermute | solution.py:17
  45.8 3.6 %collective-permute-start.7 = (bf16[256,640]{0,1:T(8,128)(2,1)S(1)}, bf16[256,640]{0,1:T(8,128)(2,1)S(1)}, u32[]{:S(2)}, u32[]{:S(2)}) collective-permute-start(bf16[256,640]{0,1:T(8,128)(2,1)S(1)} %collective-permute-done.5), channel_id=1, source_target_pairs={{4,0},{8,4},{12,8},{16,12},{20,16},{24,20},{28,24},{32,28},{36,32}... | collective-permute-start | bytes 983048 | tf_op jit(solution)/shard_map/ppermute | solution.py:17
  49.5 0.4 fusion.106
  49.9 2.4 %collective-permute-done.6 = bf16[256,640]{0,1:T(8,128)(2,1)S(1)} collective-permute-done((bf16[256,640]{0,1:T(8,128)(2,1)S(1)}, bf16[256,640]{0,1:T(8,128)(2,1)S(1)}, u32[]{:S(2)}, u32[]{:S(2)}) %collective-permute-start.6) | collective-permute-done | bytes 327712 | tf_op jit(solution)/shard_map/ppermute | solution.py:17
  52.3 0.4 fusion.104
  52.7 1.4 %collective-permute-done.7 = bf16[256,640]{0,1:T(8,128)(2,1)S(1)} collective-permute-done((bf16[256,640]{0,1:T(8,128)(2,1)S(1)}, bf16[256,640]{0,1:T(8,128)(2,1)S(1)}, u32[]{:S(2)}, u32[]{:S(2)}) %collective-permute-start.7) | collective-permute-done | bytes 327712 | tf_op jit(solution)/shard_map/ppermute | solution.py:17
  54.1 0.4 fusion.103
  55.3 0.3 fusion.36
  55.9 0.3 fusion.40
  56.8 0.3 fusion.32
  57.4 0.3 fusion.18
  57.8 0.3 fusion.21
  58.1 0.3 fusion.24
  58.4 0.3 fusion.28
  59.3 1.3 convolution_convert_fusion.1
  60.7 3.7 %all-to-all-start = ((bf16[4,64,1280]{2,1,0:T(8,128)(2,1)}), bf16[4,64,1280]{2,1,0:T(8,128)(2,1)S(1)}, u32[]{:S(2)}, u32[]{:S(2)}) async-start(bf16[4,64,1280]{2,1,0:T(8,128)(2,1)} %convolution_convert_fusion.1), calls=%async_computation | async-start | bytes 1310720 | tf_op jit(solution)/shard_map/all_to_all | solution.py:112
  65.1 10.2 %all-to-all-done = bf16[4,64,1280]{2,1,0:T(8,128)(2,1)S(1)} async-done(((bf16[4,64,1280]{2,1,0:T(8,128)(2,1)}), bf16[4,64,1280]{2,1,0:T(8,128)(2,1)S(1)}, u32[]{:S(2)}, u32[]{:S(2)}) %all-to-all-start) | async-done | bytes 655392 | tf_op jit(solution)/shard_map/all_to_all | solution.py:112
  75.8 0.4 convolution_convert_fusion
  76.4 59.0 %all_to_all.17 = bf16[128,2,1280]{2,1,0:T(2,128)(2,1)S(1)} all-to-all(bf16[128,2,1280]{2,1,0:T(2,128)(2,1)S(1)} %all_to_all.12), channel_id=1, replica_groups=mesh['seq'=128,'tp'=4] {'seq'}, dimensions={0} | all-to-all | bytes 1310720 | tf_op jit(solution)/shard_map/all_to_all | solution.py:133
  135.5 1.1 all_to_all.14
  (87 shorter events, 5.5 us)
Async XLA Ops:
  0.0 59.3 %copy-start = (bf16[320,1280]{1,0:T(8,128)(2,1)S(1)}, bf16[320,1280]{1,0:T(8,128)(2,1)}, u32[]{:S(2)}) copy-start(bf16[320,1280]{1,0:T(8,128)(2,1)} %param.16) | copy-start | bytes 2457604
  0.0 2.9 %copy-start.1 = (bf16[256,1280]{1,0:T(8,128)(2,1)S(1)}, bf16[256,1280]{1,0:T(8,128)(2,1)}, u32[]{:S(2)}) copy-start(bf16[256,1280]{1,0:T(8,128)(2,1)} %param.11) | copy-start | bytes 1966084
  0.0 2.8 %copy-start.12 = (f32[3,320]{1,0:T(4,128)S(1)}, f32[3,320]{1,0:T(4,128)}, u32[]{:S(2)}) copy-start(f32[3,320]{1,0:T(4,128)} %param.15) | copy-start | bytes 11524
  0.0 2.9 %copy-start.16 = (f32[1280]{0:T(1024)S(1)}, f32[1280]{0:T(1024)}, u32[]{:S(2)}) copy-start(f32[1280]{0:T(1024)} %param.12) | copy-start | bytes 15364
  0.0 2.9 %copy-start.15 = (f32[1280]{0:T(1024)S(1)}, f32[1280]{0:T(1024)}, u32[]{:S(2)}) copy-start(f32[1280]{0:T(1024)} %param.13) | copy-start | bytes 15364
  4.6 7.5 %copy-start.3 = (s32[8192]{0:T(1024)S(1)}, s32[8192]{0:T(1024)}, u32[]{:S(2)}) copy-start(s32[8192]{0:T(1024)} %param.20) | copy-start | bytes 98308
  6.3 20.8 %collective-permute-start = (bf16[256,640]{0,1:T(8,128)(2,1)S(1)}, bf16[256,640]{0,1:T(8,128)(2,1)S(1)}, u32[]{:S(2)}, u32[]{:S(2)}) collective-permute-start(bf16[256,640]{0,1:T(8,128)(2,1)S(1)} %pad_maximum_fusion), channel_id=1, source_target_pairs={{0,4},{4,8},{8,12},{12,16},{16,20},{20,24},{24,28},{28,32},{32,36}... | collective-permute-start | bytes 983048 | tf_op jit(solution)/shard_map/ppermute | solution.py:17
  8.2 13.3 %collective-permute-start.1 = (bf16[256,640]{0,1:T(8,128)(2,1)S(1)}, bf16[256,640]{0,1:T(8,128)(2,1)S(1)}, u32[]{:S(2)}, u32[]{:S(2)}) collective-permute-start(bf16[256,640]{0,1:T(8,128)(2,1)S(1)} %pad_maximum_fusion), channel_id=1, source_target_pairs={{4,0},{8,4},{12,8},{16,12},{20,16},{24,20},{28,24},{32,28},{36,32}... | collective-permute-start | bytes 983048 | tf_op jit(solution)/shard_map/ppermute | solution.py:17
  16.7 1.7 %copy-start.7 = (s32[256]{0:T(256)S(1)}, s32[256]{0:T(256)}, u32[]{:S(2)}) copy-start(s32[256]{0:T(256)} %eq.200) | copy-start | bytes 3076
  16.7 1.7 %copy-start.8 = (s32[256]{0:T(256)S(1)}, s32[256]{0:T(256)}, u32[]{:S(2)}) copy-start(s32[256]{0:T(256)} %eq.203) | copy-start | bytes 3076
  16.7 1.7 %copy-start.9 = (s32[256]{0:T(256)S(1)}, s32[256]{0:T(256)}, u32[]{:S(2)}) copy-start(s32[256]{0:T(256)} %eq.206) | copy-start | bytes 3076
  16.7 1.8 %copy-start.10 = (s32[256]{0:T(256)S(1)}, s32[256]{0:T(256)}, u32[]{:S(2)}) copy-start(s32[256]{0:T(256)} %eq.209) | copy-start | bytes 3076
  16.7 1.8 %copy-start.11 = (s32[256]{0:T(256)S(1)}, s32[256]{0:T(256)}, u32[]{:S(2)}) copy-start(s32[256]{0:T(256)} %eq.212) | copy-start | bytes 3076
  16.7 2.3 %copy-start.13 = (s32[64,1]{0,1:T(1,128)S(1)}, s32[64,1]{0,1:T(1,128)}, u32[]{:S(2)}) copy-start(s32[64,1]{0,1:T(1,128)} %param.21) | copy-start | bytes 772
  21.6 9.7 %collective-permute-start.3 = (bf16[256,640]{0,1:T(8,128)(2,1)S(1)}, bf16[256,640]{0,1:T(8,128)(2,1)S(1)}, u32[]{:S(2)}, u32[]{:S(2)}) collective-permute-start(bf16[256,640]{0,1:T(8,128)(2,1)S(1)} %collective-permute-done.1), channel_id=1, source_target_pairs={{4,0},{8,4},{12,8},{16,12},{20,16},{24,20},{28,24},{32,28},{36,32}... | collective-permute-start | bytes 983048 | tf_op jit(solution)/shard_map/ppermute | solution.py:17
  27.1 8.4 %collective-permute-start.2 = (bf16[256,640]{0,1:T(8,128)(2,1)S(1)}, bf16[256,640]{0,1:T(8,128)(2,1)S(1)}, u32[]{:S(2)}, u32[]{:S(2)}) collective-permute-start(bf16[256,640]{0,1:T(8,128)(2,1)S(1)} %collective-permute-done), channel_id=1, source_target_pairs={{0,4},{4,8},{8,12},{12,16},{16,20},{20,24},{24,28},{28,32},{32,36}... | collective-permute-start | bytes 983048 | tf_op jit(solution)/shard_map/ppermute | solution.py:17
  31.3 8.4 %collective-permute-start.5 = (bf16[256,640]{0,1:T(8,128)(2,1)S(1)}, bf16[256,640]{0,1:T(8,128)(2,1)S(1)}, u32[]{:S(2)}, u32[]{:S(2)}) collective-permute-start(bf16[256,640]{0,1:T(8,128)(2,1)S(1)} %collective-permute-done.3), channel_id=1, source_target_pairs={{4,0},{8,4},{12,8},{16,12},{20,16},{24,20},{28,24},{32,28},{36,32}... | collective-permute-start | bytes 983048 | tf_op jit(solution)/shard_map/ppermute | solution.py:17
  35.5 8.4 %collective-permute-start.4 = (bf16[256,640]{0,1:T(8,128)(2,1)S(1)}, bf16[256,640]{0,1:T(8,128)(2,1)S(1)}, u32[]{:S(2)}, u32[]{:S(2)}) collective-permute-start(bf16[256,640]{0,1:T(8,128)(2,1)S(1)} %collective-permute-done.2), channel_id=1, source_target_pairs={{0,4},{4,8},{8,12},{12,16},{16,20},{20,24},{24,28},{28,32},{32,36}... | collective-permute-start | bytes 983048 | tf_op jit(solution)/shard_map/ppermute | solution.py:17
  43.9 8.4 %collective-permute-start.6 = (bf16[256,640]{0,1:T(8,128)(2,1)S(1)}, bf16[256,640]{0,1:T(8,128)(2,1)S(1)}, u32[]{:S(2)}, u32[]{:S(2)}) collective-permute-start(bf16[256,640]{0,1:T(8,128)(2,1)S(1)} %collective-permute-done.4), channel_id=1, source_target_pairs={{0,4},{4,8},{8,12},{12,16},{16,20},{20,24},{24,28},{28,32},{32,36}... | collective-permute-start | bytes 983048 | tf_op jit(solution)/shard_map/ppermute | solution.py:17
  45.8 8.2 %collective-permute-start.7 = (bf16[256,640]{0,1:T(8,128)(2,1)S(1)}, bf16[256,640]{0,1:T(8,128)(2,1)S(1)}, u32[]{:S(2)}, u32[]{:S(2)}) collective-permute-start(bf16[256,640]{0,1:T(8,128)(2,1)S(1)} %collective-permute-done.5), channel_id=1, source_target_pairs={{4,0},{8,4},{12,8},{16,12},{20,16},{24,20},{28,24},{32,28},{36,32}... | collective-permute-start | bytes 983048 | tf_op jit(solution)/shard_map/ppermute | solution.py:17
  59.3 5.0 %copy-start.2 = (s32[64,128]{1,0:T(8,128)S(1)}, s32[64,128]{1,0:T(8,128)}, u32[]{:S(2)}) copy-start(s32[64,128]{1,0:T(8,128)} %reduce_window_sum.11) | copy-start | bytes 98308
  59.3 5.0 %copy-start.14 = (s32[64,1]{0,1:T(1,128)S(1)}, s32[64,1]{0,1:T(1,128)}, u32[]{:S(2)}) copy-start(s32[64,1]{0,1:T(1,128)} %param.21) | copy-start | bytes 772
  60.7 14.6 %all-to-all-start = ((bf16[4,64,1280]{2,1,0:T(8,128)(2,1)}), bf16[4,64,1280]{2,1,0:T(8,128)(2,1)S(1)}, u32[]{:S(2)}, u32[]{:S(2)}) async-start(bf16[4,64,1280]{2,1,0:T(8,128)(2,1)} %convolution_convert_fusion.1), calls=%async_computation | async-start | bytes 1310720 | tf_op jit(solution)/shard_map/all_to_all | solution.py:112
  64.5 10.9 %copy-start.4 = (f32[1280]{0:T(1024)S(1)}, f32[1280]{0:T(1024)}, u32[]{:S(2)}) copy-start(f32[1280]{0:T(1024)} %param.17) | copy-start | bytes 15364
  65.0 10.7 %copy-start.5 = (f32[1280]{0:T(1024)S(1)}, f32[1280]{0:T(1024)}, u32[]{:S(2)}) copy-start(f32[1280]{0:T(1024)} %param.19) | copy-start | bytes 15364
  65.0 10.7 %copy-start.6 = (f32[1280]{0:T(1024)S(1)}, f32[1280]{0:T(1024)}, u32[]{:S(2)}) copy-start(f32[1280]{0:T(1024)} %param.18) | copy-start | bytes 15364

commit v2 on v1

--- a/solution.py
+++ b/solution.py
@@ -93,14 +93,30 @@
         jnp.zeros((local_heads, tok_dev, 1), jnp.float32),
         jnp.zeros((local_heads, tok_dev, HEAD_DIM), jnp.float32),
     )
+    sign = 1 - 2 * (seq_index % 2)
+
+    def swap(value):
+        return lax.ppermute(value, "seq", [(i, i ^ 1) for i in range(seq_count)])
+
+    def absorb_at(state, block, offset):
+        return absorb_remote(state, block, row_start + offset * tok_dev)
+
+    below_2 = from_behind(key_value, "seq", 2)
+    above_2 = from_behind(key_value, "seq", -2)
+    partner_own = swap(key_value)
     state = absorb(start_state, key_value, query_segment)
-    below = key_value
-    above = key_value
-    for distance in range(1, SPAN + 1):
-        below = from_behind(below, "seq", 1)
-        above = from_behind(above, "seq", -1)
-        state = absorb_remote(state, below, row_start - distance * tok_dev)
-        state = absorb_remote(state, above, row_start + distance * tok_dev)
+    below_4 = from_behind(below_2, "seq", 2)
+    above_4 = from_behind(above_2, "seq", -2)
+    partner_near = swap(jnp.concatenate([below_2, above_2], axis=0))
+    state = absorb_at(state, partner_own, sign)
+    state = absorb_at(state, below_2, -2)
+    state = absorb_at(state, above_2, 2)
+    state = absorb_at(state, partner_near[:tok_dev], sign - 2)
+    state = absorb_at(state, partner_near[tok_dev:], sign + 2)
+    partner_far = swap(jnp.where(sign > 0, above_4, below_4))
+    state = absorb_at(state, below_4, -4)
+    state = absorb_at(state, above_4, 4)
+    state = absorb_at(state, partner_far, -3 * sign)
     row_top, totals, summed = state
     tp_index = lax.axis_index("tp")
     quarter = tok_dev // 4

time: 137 us -> 133 us (0.971)
  waiting for transfers between devices: 21.5 us -> 17.7 us
  starting transfers between devices: 27.5 us -> 25.3 us
    ppermute x8 -> x4, starting transfers between devices: 23.9 us -> 14.7 us  [from_behind(): lax.ppermute(value, axis, [(source, source + steps) for source in range(l...]
    ppermute x0 -> x3, starting transfers between devices: none -> 6.37 us  [swap(): return lax.ppermute(value, 'seq', [(i, i ^ 1) for i in range(seq_count)])]
    ppermute x8 -> x4, waiting for transfers between devices: 11.3 us -> 6.85 us  [from_behind(): lax.ppermute(value, axis, [(source, source + steps) for source in range(l...]
  transfers between devices with their start and end apart: 9 -> 8, of which waited for: 6 -> 3; matrix products, arithmetic and copies ran while one was open for 9% -> 11% of each run, Pallas kernels for 0% -> 0%
where the time goes in v2:
time: 133 us; the launch traced here: 132 us
  blocking collectives  58.7 us (44%)
  starting transfers between devices  25.3 us (19%)
  waiting for transfers between devices  17.7 us (13%)
  matrix products  13.8 us (10%)
  other arithmetic  8.52 us (6%)
  local copies, waits for them, and re-layouts  7.01 us (5%)
    all_to_all x1, blocking collectives, per_device(): lax.all_to_all(outgoing, 'seq', split_axis=0, concat_axis=0, tiled=True)  58.7 us
    ppermute x4, starting transfers between devices, from_behind(): lax.ppermute(value, axis, [(source, source + steps) for source in range(l...  14.7 us
    all_to_all x1, waiting for transfers between devices, per_device(): lax.all_to_all(head_term, 'tp', split_axis=0, concat_axis=0, tiled=True)  10.9 us
    ppermute x4, waiting for transfers between devices, from_behind(): lax.ppermute(value, axis, [(source, source + steps) for source in range(l...  6.85 us
    ppermute x3, starting transfers between devices, swap(): return lax.ppermute(value, 'seq', [(i, i ^ 1) for i in range(seq_count)])  6.37 us
    all_to_all x1, starting transfers between devices, per_device(): lax.all_to_all(head_term, 'tp', split_axis=0, concat_axis=0, tiled=True)  4.29 us
    dot_general x9, matrix products, block_scores(): jnp.einsum('qhd,khd->hqk', query_heads, key_heads, preferred_element_type...  4.23 us
    eq x9, local copies, waits for them, and re-layouts, block_scores(): allowed = query_segment[:, None] == key_segment[None, :]  3.88 us
  transfers between devices with their start and end apart: 8, of which 3 were waited for; matrix products, arithmetic and copies ran while one was open for 11% of the time, Pallas kernels for 0%

profile of v2, /device:TPU:32, one launch (start us, length us, event | category | flops | bytes accessed | tf_op | source)
XLA Modules:
  0.0 131.9 jit_solution(4239210992523385389)
XLA Ops:
  0.0 1.4 %convert_reduce_fusion = f32[256]{0:T(256)S(1)} fusion(bf16[256,1280]{1,0:T(8,128)(2,1)} %param.11), kind=kLoop, calls=%fused_computation.3 | loop fusion | flops 655104 | bytes 656384 | tf_op jit(solution)/shard_map/reduce_sum | solution.py:21
  1.4 1.4 %fusion.11 = f32[256]{0:T(256)S(1)} fusion(bf16[256,1280]{1,0:T(8,128)(2,1)} %param.11, f32[256]{0:T(256)S(1)} %broadcast_multiply_fusion), kind=kLoop, calls=%fused_computation.24 | loop fusion | flops 1310464 | bytes 657408 | tf_op jit(solution)/shard_map/reduce_sum | solution.py:23
  2.9 1.7 %fusion.32 = bf16[256,320]{0,1:T(8,128)(2,1)S(1)} fusion(bf16[3,1280,320]{1,2,0:T(8,128)(2,1)} %param.14, f32[320]{0:T(512)S(1)} %get-tuple-element.7, bf16[256,1280]{1,0:T(8,128)(2,1)S(1)} %copy-done.1, f32[1280]{0:T(1024)S(1)} %copy-done.19, f32[1280]{0:T(1024)S(1)} %copy-done.20, f32[256]{0:T(256)S(1)} %add_rsqrt_fusion, f32[256]{0:T(256)S(1)} %broadcast_multiply_fusion), kind=kOutput, calls=%fused_computation.52 | convolution fusion | flops 211845120 | bytes 1651968 | tf_op jit(solution)/shard_map/dot_general | solution.py:43
  4.6 1.7 %fusion.33 = bf16[256,320]{0,1:T(8,128)(2,1)S(1)} fusion(bf16[3,1280,320]{1,2,0:T(8,128)(2,1)} %param.14, f32[320]{0:T(512)S(1)} %get-tuple-element.6, bf16[256,1280]{1,0:T(8,128)(2,1)S(1)} %copy-done.1, f32[1280]{0:T(1024)S(1)} %copy-done.19, f32[1280]{0:T(1024)S(1)} %copy-done.20, f32[256]{0:T(256)S(1)} %add_rsqrt_fusion, f32[256]{0:T(256)S(1)} %broadcast_multiply_fusion), kind=kOutput, calls=%fused_computation.53 | convolution fusion | flops 211845120 | bytes 1651968 | tf_op jit(solution)/shard_map/dot_general | solution.py:46
  6.3 3.8 %collective-permute-start.1 = (bf16[256,640]{0,1:T(8,128)(2,1)S(1)}, bf16[256,640]{0,1:T(8,128)(2,1)S(1)}, u32[]{:S(2)}, u32[]{:S(2)}) collective-permute-start(bf16[256,640]{0,1:T(8,128)(2,1)S(1)} %pad_maximum_fusion.1), channel_id=1, source_target_pairs={{0,8},{4,12},{8,16},{12,20},{16,24},{20,28},{24,32},{28,36},{32,40... | collective-permute-start | bytes 983048 | tf_op jit(solution)/shard_map/ppermute | solution.py:17
  10.1 4.8 %collective-permute-start.2 = (bf16[256,640]{0,1:T(8,128)(2,1)S(1)}, bf16[256,640]{0,1:T(8,128)(2,1)S(1)}, u32[]{:S(2)}, u32[]{:S(2)}) collective-permute-start(bf16[256,640]{0,1:T(8,128)(2,1)S(1)} %pad_maximum_fusion.1), channel_id=1, source_target_pairs={{8,0},{12,4},{16,8},{20,12},{24,16},{28,20},{32,24},{36,28},{40,32... | collective-permute-start | bytes 983048 | tf_op jit(solution)/shard_map/ppermute | solution.py:17
  15.0 1.9 %collective-permute-start = (bf16[256,640]{0,1:T(8,128)(2,1)S(1)}, bf16[256,640]{0,1:T(8,128)(2,1)S(1)}, u32[]{:S(2)}, u32[]{:S(2)}) collective-permute-start(bf16[256,640]{0,1:T(8,128)(2,1)S(1)} %pad_maximum_fusion.1), channel_id=1, source_target_pairs={{0,4},{4,0},{8,12},{12,8},{16,20},{20,16},{24,28},{28,24},{32,36},... | collective-permute-start | bytes 983048 | tf_op jit(solution)/shard_map/ppermute | solution.py:99
  18.1 0.7 eq.202
  18.8 0.7 eq.205
  19.6 0.7 eq.208
  20.4 0.7 eq.211
  21.1 0.7 eq.214
  21.8 1.7 %fusion.31 = bf16[256,320]{0,1:T(8,128)(2,1)S(1)} fusion(bf16[3,1280,320]{1,2,0:T(8,128)(2,1)} %param.14, f32[320]{0:T(512)S(1)} %get-tuple-element.5, bf16[256,1280]{1,0:T(8,128)(2,1)S(1)} %copy-done.1, f32[1280]{0:T(1024)S(1)} %copy-done.19, f32[1280]{0:T(1024)S(1)} %copy-done.20, f32[256]{0:T(256)S(1)} %add_rsqrt_fusion, f32[256]{0:T(256)S(1)} %broadcast_multiply_fusion), kind=kOutput, calls=%fused_computation.51 | convolution fusion | flops 211845120 | bytes 1651968 | tf_op jit(solution)/shard_map/dot_general | solution.py:40
  23.6 1.1 broadcast_compare_fusion.8
  24.7 0.7 fusion.89
  25.4 1.4 %reduce_window_sum.11 = s32[64,128]{1,0:T(8,128)} reduce-window(s32[64,128]{1,0:T(8,128)} %fusion.89, s32[]{:T(128)} %constant.131.clone.1), window={size=64x1 pad=63_0x0_0}, to_apply=%region_0.0 | reduce-window | flops 516096 | bytes 65540 | tf_op jit(solution)/shard_map/jit(cumsum)/reduce_window_sum | solution.py:140
  26.8 1.2 fusion.114
  28.2 2.5 %collective-permute-start.3 = (bf16[512,640]{0,1:T(8,128)(2,1)S(1)}, bf16[512,640]{0,1:T(8,128)(2,1)S(1)}, u32[]{:S(2)}, u32[]{:S(2)}) collective-permute-start(bf16[512,640]{0,1:T(8,128)(2,1)S(1)} %pad_maximum_fusion), channel_id=1, source_target_pairs={{0,4},{4,0},{8,12},{12,8},{16,20},{20,16},{24,28},{28,24},{32,36},... | collective-permute-start | bytes 1966088 | tf_op jit(solution)/shard_map/ppermute | solution.py:99
  30.7 0.4 fusion.111
  31.1 2.1 %collective-permute-start.4 = (bf16[256,640]{0,1:T(8,128)(2,1)S(1)}, bf16[256,640]{0,1:T(8,128)(2,1)S(1)}, u32[]{:S(2)}, u32[]{:S(2)}) collective-permute-start(bf16[256,640]{0,1:T(8,128)(2,1)S(1)} %collective-permute-done.1), channel_id=1, source_target_pairs={{0,8},{4,12},{8,16},{12,20},{16,24},{20,28},{24,32},{28,36},{32,40... | collective-permute-start | bytes 983048 | tf_op jit(solution)/shard_map/ppermute | solution.py:17
  33.2 3.9 %collective-permute-start.5 = (bf16[256,640]{0,1:T(8,128)(2,1)S(1)}, bf16[256,640]{0,1:T(8,128)(2,1)S(1)}, u32[]{:S(2)}, u32[]{:S(2)}) collective-permute-start(bf16[256,640]{0,1:T(8,128)(2,1)S(1)} %collective-permute-done.2), channel_id=1, source_target_pairs={{8,0},{12,4},{16,8},{20,12},{24,16},{28,20},{32,24},{36,28},{40,32... | collective-permute-start | bytes 983048 | tf_op jit(solution)/shard_map/ppermute | solution.py:17
  37.2 0.4 fusion.112
  37.6 0.4 fusion.113
  38.0 4.8 %collective-permute-done.4 = bf16[256,640]{0,1:T(8,128)(2,1)S(1)} collective-permute-done((bf16[256,640]{0,1:T(8,128)(2,1)S(1)}, bf16[256,640]{0,1:T(8,128)(2,1)S(1)}, u32[]{:S(2)}, u32[]{:S(2)}) %collective-permute-start.4) | collective-permute-done | bytes 327712 | tf_op jit(solution)/shard_map/ppermute | solution.py:17
  42.8 2.1 %collective-permute-done.5 = bf16[256,640]{0,1:T(8,128)(2,1)S(1)} collective-permute-done((bf16[256,640]{0,1:T(8,128)(2,1)S(1)}, bf16[256,640]{0,1:T(8,128)(2,1)S(1)}, u32[]{:S(2)}, u32[]{:S(2)}) %collective-permute-start.5) | collective-permute-done | bytes 327712 | tf_op jit(solution)/shard_map/ppermute | solution.py:17
  44.9 1.9 %collective-permute-start.6 = (bf16[256,640]{0,1:T(8,128)(2,1)S(1)}, bf16[256,640]{0,1:T(8,128)(2,1)S(1)}, u32[]{:S(2)}, u32[]{:S(2)}) collective-permute-start(bf16[256,640]{0,1:T(8,128)(2,1)S(1)} %broadcast_select_fusion), channel_id=1, source_target_pairs={{0,4},{4,0},{8,12},{12,8},{16,20},{20,16},{24,28},{28,24},{32,36},... | collective-permute-start | bytes 983048 | tf_op jit(solution)/shard_map/ppermute | solution.py:99
  46.9 0.4 fusion.108
  47.3 0.4 fusion.107
  47.7 0.4 fusion.109
  48.1 0.4 fusion.110
  48.5 0.4 fusion.106
  48.9 0.3 fusion.70
  49.2 0.3 fusion.38
  49.5 0.3 fusion.68
  50.1 0.3 fusion.42
  51.2 0.3 fusion.61
  51.5 0.3 fusion.46
  51.8 0.3 fusion.34
  52.2 0.3 fusion.15
  52.5 0.3 fusion.24
  52.8 0.3 fusion.30
  53.8 1.3 %convolution_convert_fusion.1 = bf16[4,64,1280]{2,1,0:T(8,128)(2,1)} fusion(bf16[4,64,320]{2,1,0:T(8,128)(2,1)S(1)} %convert_element_type.96, bf16[320,1280]{1,0:T(8,128)(2,1)S(1)} %copy-done), kind=kOutput, calls=%fused_computation.1 | convolution fusion | flops 210042880 | bytes 1638400 | tf_op jit(solution)/shard_map/tgc,cd->tgd/dot_general | solution.py:125
  55.1 4.3 %all-to-all-start = ((bf16[4,64,1280]{2,1,0:T(8,128)(2,1)}), bf16[4,64,1280]{2,1,0:T(8,128)(2,1)S(1)}, u32[]{:S(2)}, u32[]{:S(2)}) async-start(bf16[4,64,1280]{2,1,0:T(8,128)(2,1)} %convolution_convert_fusion.1), calls=%async_computation | async-start | bytes 1310720 | tf_op jit(solution)/shard_map/all_to_all | solution.py:128
  59.7 0.3 dynamic-slice_convert_fusion
  60.1 10.9 %all-to-all-done = bf16[4,64,1280]{2,1,0:T(8,128)(2,1)S(1)} async-done(((bf16[4,64,1280]{2,1,0:T(8,128)(2,1)}), bf16[4,64,1280]{2,1,0:T(8,128)(2,1)S(1)}, u32[]{:S(2)}, u32[]{:S(2)}) %all-to-all-start) | async-done | bytes 655392 | tf_op jit(solution)/shard_map/all_to_all | solution.py:128
  71.4 0.4 convolution_convert_fusion
  72.1 58.7 %all_to_all.17 = bf16[128,2,1280]{2,1,0:T(2,128)(2,1)S(1)} all-to-all(bf16[128,2,1280]{2,1,0:T(2,128)(2,1)S(1)} %all_to_all.12), channel_id=1, replica_groups=mesh['seq'=128,'tp'=4] {'seq'}, dimensions={0} | all-to-all | bytes 1310720 | tf_op jit(solution)/shard_map/all_to_all | solution.py:149
  130.8 1.1 all_to_all.14
  (94 shorter events, 4.4 us)
Async XLA Ops:
  0.0 53.7 %copy-start = (bf16[320,1280]{1,0:T(8,128)(2,1)S(1)}, bf16[320,1280]{1,0:T(8,128)(2,1)}, u32[]{:S(2)}) copy-start(bf16[320,1280]{1,0:T(8,128)(2,1)} %param.16) | copy-start | bytes 2457604
  0.0 2.9 %copy-start.1 = (bf16[256,1280]{1,0:T(8,128)(2,1)S(1)}, bf16[256,1280]{1,0:T(8,128)(2,1)}, u32[]{:S(2)}) copy-start(bf16[256,1280]{1,0:T(8,128)(2,1)} %param.11) | copy-start | bytes 1966084
  0.0 2.8 %copy-start.16 = (f32[3,320]{1,0:T(4,128)S(1)}, f32[3,320]{1,0:T(4,128)}, u32[]{:S(2)}) copy-start(f32[3,320]{1,0:T(4,128)} %param.15) | copy-start | bytes 11524
  0.0 2.9 %copy-start.20 = (f32[1280]{0:T(1024)S(1)}, f32[1280]{0:T(1024)}, u32[]{:S(2)}) copy-start(f32[1280]{0:T(1024)} %param.12) | copy-start | bytes 15364
  0.0 2.9 %copy-start.19 = (f32[1280]{0:T(1024)S(1)}, f32[1280]{0:T(1024)}, u32[]{:S(2)}) copy-start(f32[1280]{0:T(1024)} %param.13) | copy-start | bytes 15364
  4.6 12.5 %copy-start.7 = (s32[8192]{0:T(1024)S(1)}, s32[8192]{0:T(1024)}, u32[]{:S(2)}) copy-start(s32[8192]{0:T(1024)} %param.20) | copy-start | bytes 98308
  6.3 21.8 %collective-permute-start.1 = (bf16[256,640]{0,1:T(8,128)(2,1)S(1)}, bf16[256,640]{0,1:T(8,128)(2,1)S(1)}, u32[]{:S(2)}, u32[]{:S(2)}) collective-permute-start(bf16[256,640]{0,1:T(8,128)(2,1)S(1)} %pad_maximum_fusion.1), channel_id=1, source_target_pairs={{0,8},{4,12},{8,16},{12,20},{16,24},{20,28},{24,32},{28,36},{32,40... | collective-permute-start | bytes 983048 | tf_op jit(solution)/shard_map/ppermute | solution.py:17
  10.1 18.0 %collective-permute-start.2 = (bf16[256,640]{0,1:T(8,128)(2,1)S(1)}, bf16[256,640]{0,1:T(8,128)(2,1)S(1)}, u32[]{:S(2)}, u32[]{:S(2)}) collective-permute-start(bf16[256,640]{0,1:T(8,128)(2,1)S(1)} %pad_maximum_fusion.1), channel_id=1, source_target_pairs={{8,0},{12,4},{16,8},{20,12},{24,16},{28,20},{32,24},{36,28},{40,32... | collective-permute-start | bytes 983048 | tf_op jit(solution)/shard_map/ppermute | solution.py:17
  15.0 22.6 %collective-permute-start = (bf16[256,640]{0,1:T(8,128)(2,1)S(1)}, bf16[256,640]{0,1:T(8,128)(2,1)S(1)}, u32[]{:S(2)}, u32[]{:S(2)}) collective-permute-start(bf16[256,640]{0,1:T(8,128)(2,1)S(1)} %pad_maximum_fusion.1), channel_id=1, source_target_pairs={{0,4},{4,0},{8,12},{12,8},{16,20},{20,16},{24,28},{28,24},{32,36},... | collective-permute-start | bytes 983048 | tf_op jit(solution)/shard_map/ppermute | solution.py:99
  21.8 1.7 %copy-start.11 = (s32[256]{0:T(256)S(1)}, s32[256]{0:T(256)}, u32[]{:S(2)}) copy-start(s32[256]{0:T(256)} %eq.202) | copy-start | bytes 3076
  21.8 1.7 %copy-start.12 = (s32[256]{0:T(256)S(1)}, s32[256]{0:T(256)}, u32[]{:S(2)}) copy-start(s32[256]{0:T(256)} %eq.205) | copy-start | bytes 3076
  21.8 1.7 %copy-start.13 = (s32[256]{0:T(256)S(1)}, s32[256]{0:T(256)}, u32[]{:S(2)}) copy-start(s32[256]{0:T(256)} %eq.208) | copy-start | bytes 3076
  21.8 1.8 %copy-start.14 = (s32[256]{0:T(256)S(1)}, s32[256]{0:T(256)}, u32[]{:S(2)}) copy-start(s32[256]{0:T(256)} %eq.211) | copy-start | bytes 3076
  21.8 1.8 %copy-start.15 = (s32[256]{0:T(256)S(1)}, s32[256]{0:T(256)}, u32[]{:S(2)}) copy-start(s32[256]{0:T(256)} %eq.214) | copy-start | bytes 3076
  21.8 2.9 %copy-start.17 = (s32[64,1]{0,1:T(1,128)S(1)}, s32[64,1]{0,1:T(1,128)}, u32[]{:S(2)}) copy-start(s32[64,1]{0,1:T(1,128)} %param.21) | copy-start | bytes 772
  28.1 2.7 %copy-start.5 = (pred[256,256]{0,1:T(8,128)(4,1)S(1)}, pred[256,256]{0,1:T(8,128)(4,1)}, u32[]{:S(2)}) copy-start(pred[256,256]{0,1:T(8,128)(4,1)} %get-tuple-element.56) | copy-start | bytes 196612
  28.1 9.0 %copy-start.4 = (pred[256,256]{0,1:T(8,128)(4,1)S(1)}, pred[256,256]{0,1:T(8,128)(4,1)}, u32[]{:S(2)}) copy-start(pred[256,256]{0,1:T(8,128)(4,1)} %get-tuple-element.55) | copy-start | bytes 196612
  28.2 19.5 %collective-permute-start.3 = (bf16[512,640]{0,1:T(8,128)(2,1)S(1)}, bf16[512,640]{0,1:T(8,128)(2,1)S(1)}, u32[]{:S(2)}, u32[]{:S(2)}) collective-permute-start(bf16[512,640]{0,1:T(8,128)(2,1)S(1)} %pad_maximum_fusion), channel_id=1, source_target_pairs={{0,4},{4,0},{8,12},{12,8},{16,20},{20,16},{24,28},{28,24},{32,36},... | collective-permute-start | bytes 1966088 | tf_op jit(solution)/shard_map/ppermute | solution.py:99
  31.1 6.5 %copy-start.3 = (pred[256,256]{0,1:T(8,128)(4,1)S(1)}, pred[256,256]{0,1:T(8,128)(4,1)}, u32[]{:S(2)}) copy-start(pred[256,256]{0,1:T(8,128)(4,1)} %get-tuple-element.62) | copy-start | bytes 196612
  31.1 11.7 %collective-permute-start.4 = (bf16[256,640]{0,1:T(8,128)(2,1)S(1)}, bf16[256,640]{0,1:T(8,128)(2,1)S(1)}, u32[]{:S(2)}, u32[]{:S(2)}) collective-permute-start(bf16[256,640]{0,1:T(8,128)(2,1)S(1)} %collective-permute-done.1), channel_id=1, source_target_pairs={{0,8},{4,12},{8,16},{12,20},{16,24},{20,28},{24,32},{28,36},{32,40... | collective-permute-start | bytes 983048 | tf_op jit(solution)/shard_map/ppermute | solution.py:17
  33.2 11.6 %collective-permute-start.5 = (bf16[256,640]{0,1:T(8,128)(2,1)S(1)}, bf16[256,640]{0,1:T(8,128)(2,1)S(1)}, u32[]{:S(2)}, u32[]{:S(2)}) collective-permute-start(bf16[256,640]{0,1:T(8,128)(2,1)S(1)} %collective-permute-done.2), channel_id=1, source_target_pairs={{8,0},{12,4},{16,8},{20,12},{24,16},{28,20},{32,24},{36,28},{40,32... | collective-permute-start | bytes 983048 | tf_op jit(solution)/shard_map/ppermute | solution.py:17
  38.0 8.9 %copy-start.2 = (pred[256,256]{0,1:T(8,128)(4,1)S(1)}, pred[256,256]{0,1:T(8,128)(4,1)}, u32[]{:S(2)}) copy-start(pred[256,256]{0,1:T(8,128)(4,1)} %get-tuple-element.59) | copy-start | bytes 196612
  44.9 3.6 %collective-permute-start.6 = (bf16[256,640]{0,1:T(8,128)(2,1)S(1)}, bf16[256,640]{0,1:T(8,128)(2,1)S(1)}, u32[]{:S(2)}, u32[]{:S(2)}) collective-permute-start(bf16[256,640]{0,1:T(8,128)(2,1)S(1)} %broadcast_select_fusion), channel_id=1, source_target_pairs={{0,4},{4,0},{8,12},{12,8},{16,20},{20,16},{24,28},{28,24},{32,36},... | collective-permute-start | bytes 983048 | tf_op jit(solution)/shard_map/ppermute | solution.py:99
  53.7 5.6 %copy-start.6 = (s32[64,128]{1,0:T(8,128)S(1)}, s32[64,128]{1,0:T(8,128)}, u32[]{:S(2)}) copy-start(s32[64,128]{1,0:T(8,128)} %reduce_window_sum.11) | copy-start | bytes 98308
  53.7 5.6 %copy-start.18 = (s32[64,1]{0,1:T(1,128)S(1)}, s32[64,1]{0,1:T(1,128)}, u32[]{:S(2)}) copy-start(s32[64,1]{0,1:T(1,128)} %param.21) | copy-start | bytes 772
  55.1 15.8 %all-to-all-start = ((bf16[4,64,1280]{2,1,0:T(8,128)(2,1)}), bf16[4,64,1280]{2,1,0:T(8,128)(2,1)S(1)}, u32[]{:S(2)}, u32[]{:S(2)}) async-start(bf16[4,64,1280]{2,1,0:T(8,128)(2,1)} %convolution_convert_fusion.1), calls=%async_computation | async-start | bytes 1310720 | tf_op jit(solution)/shard_map/all_to_all | solution.py:128
  59.6 11.5 %copy-start.8 = (f32[1280]{0:T(1024)S(1)}, f32[1280]{0:T(1024)}, u32[]{:S(2)}) copy-start(f32[1280]{0:T(1024)} %param.17) | copy-start | bytes 15364
  60.1 11.3 %copy-start.9 = (f32[1280]{0:T(1024)S(1)}, f32[1280]{0:T(1024)}, u32[]{:S(2)}) copy-start(f32[1280]{0:T(1024)} %param.19) | copy-start | bytes 15364
  60.1 11.3 %copy-start.10 = (f32[1280]{0:T(1024)S(1)}, f32[1280]{0:T(1024)}, u32[]{:S(2)}) copy-start(f32[1280]{0:T(1024)} %param.18) | copy-start | bytes 15364

commit v3 on v2

--- a/solution.py
+++ b/solution.py
@@ -103,20 +103,19 @@
 
     below_2 = from_behind(key_value, "seq", 2)
     above_2 = from_behind(key_value, "seq", -2)
+    below_4 = from_behind(key_value, "seq", 4)
+    above_4 = from_behind(key_value, "seq", -4)
     partner_own = swap(key_value)
     state = absorb(start_state, key_value, query_segment)
-    below_4 = from_behind(below_2, "seq", 2)
-    above_4 = from_behind(above_2, "seq", -2)
-    partner_near = swap(jnp.concatenate([below_2, above_2], axis=0))
+    partner_rest = swap(jnp.concatenate([below_2, above_2, jnp.where(sign > 0, above_4, below_4)], axis=0))
     state = absorb_at(state, partner_own, sign)
     state = absorb_at(state, below_2, -2)
     state = absorb_at(state, above_2, 2)
-    state = absorb_at(state, partner_near[:tok_dev], sign - 2)
-    state = absorb_at(state, partner_near[tok_dev:], sign + 2)
-    partner_far = swap(jnp.where(sign > 0, above_4, below_4))
     state = absorb_at(state, below_4, -4)
     state = absorb_at(state, above_4, 4)
-    state = absorb_at(state, partner_far, -3 * sign)
+    state = absorb_at(state, partner_rest[:tok_dev], sign - 2)
+    state = absorb_at(state, partner_rest[tok_dev : 2 * tok_dev], sign + 2)
+    state = absorb_at(state, partner_rest[2 * tok_dev :], -3 * sign)
     row_top, totals, summed = state
     tp_index = lax.axis_index("tp")
     quarter = tok_dev // 4

time: 133 us -> 132 us (level)
  starting transfers between devices: 25.3 us -> 22.2 us
  waiting for transfers between devices: 17.7 us -> 19.9 us
  blocking collectives: 58.7 us -> 56.9 us
    slice x6, local copies, waits for them, and re-layouts: 0.16 us -> 3.23 us  [block_scores(): value_heads = block[:, local_width:].reshape(-1, local_heads, HEAD_DIM)]
    eq x9, local copies, waits for them, and re-layouts: 3.88 us -> 1.01 us  [block_scores(): allowed = query_segment[:, None] == key_segment[None, :]]
    ppermute x3 -> x2, starting transfers between devices: 6.37 us -> 3.84 us  [swap(): return lax.ppermute(value, 'seq', [(i, i ^ 1) for i in range(seq_count)])]
    ppermute x4, waiting for transfers between devices: 6.85 us -> 9.01 us  [from_behind(): lax.ppermute(value, axis, [(source, source + steps) for source in range(l...]
    all_to_all x1, blocking collectives: 58.7 us -> 56.9 us  [per_device(): lax.all_to_all(outgoing, 'seq', split_axis=0, concat_axis=0, tiled=True)]
  transfers between devices with their start and end apart: 8 -> 7, of which waited for: 3 -> 4; matrix products, arithmetic and copies ran while one was open for 11% -> 10% of each run, Pallas kernels for 0% -> 0%
where the time goes in v3:
time: 132 us; the launch traced here: 131 us
  blocking collectives  56.9 us (43%)
  starting transfers between devices  22.2 us (17%)
  waiting for transfers between devices  19.9 us (15%)
  matrix products  13.1 us (10%)
  other arithmetic  9.82 us (7%)
  local copies, waits for them, and re-layouts  8.03 us (6%)
    all_to_all x1, blocking collectives, per_device(): lax.all_to_all(outgoing, 'seq', split_axis=0, concat_axis=0, tiled=True)  56.9 us
    ppermute x4, starting transfers between devices, from_behind(): lax.ppermute(value, axis, [(source, source + steps) for source in range(l...  14 us
    all_to_all x1, waiting for transfers between devices, per_device(): lax.all_to_all(head_term, 'tp', split_axis=0, concat_axis=0, tiled=True)  10.9 us
    ppermute x4, waiting for transfers between devices, from_behind(): lax.ppermute(value, axis, [(source, source + steps) for source in range(l...  9.01 us
    all_to_all x1, starting transfers between devices, per_device(): lax.all_to_all(head_term, 'tp', split_axis=0, concat_axis=0, tiled=True)  4.31 us
    ppermute x2, starting transfers between devices, swap(): return lax.ppermute(value, 'seq', [(i, i ^ 1) for i in range(seq_count)])  3.84 us
    dot_general x9, matrix products, block_scores(): jnp.einsum('qhd,khd->hqk', query_heads, key_heads, preferred_element_type...  3.4 us
    slice x6, local copies, waits for them, and re-layouts, block_scores(): value_heads = block[:, local_width:].reshape(-1, local_heads, HEAD_DIM)  3.23 us
  transfers between devices with their start and end apart: 7, of which 4 were waited for; matrix products, arithmetic and copies ran while one was open for 10% of the time, Pallas kernels for 0%

profile of v3, /device:TPU:32, one launch (start us, length us, event | category | flops | bytes accessed | tf_op | source)
XLA Modules:
  0.0 130.8 jit_solution(13068506745006054635)
XLA Ops:
  0.0 1.4 %convert_reduce_fusion = f32[256]{0:T(256)S(1)} fusion(bf16[256,1280]{1,0:T(8,128)(2,1)} %param.11), kind=kLoop, calls=%fused_computation.3 | loop fusion | flops 655104 | bytes 656384 | tf_op jit(solution)/shard_map/reduce_sum | solution.py:21
  1.4 1.4 %fusion.11 = f32[256]{0:T(256)S(1)} fusion(bf16[256,1280]{1,0:T(8,128)(2,1)} %param.11, f32[256]{0:T(256)S(1)} %broadcast_multiply_fusion), kind=kLoop, calls=%fused_computation.24 | loop fusion | flops 1310464 | bytes 657408 | tf_op jit(solution)/shard_map/reduce_sum | solution.py:23
  2.9 1.7 %fusion.33 = bf16[256,320]{0,1:T(8,128)(2,1)S(1)} fusion(bf16[3,1280,320]{1,2,0:T(8,128)(2,1)} %param.14, f32[320]{0:T(512)S(1)} %get-tuple-element.7, bf16[256,1280]{1,0:T(8,128)(2,1)S(1)} %copy-done.1, f32[1280]{0:T(1024)S(1)} %copy-done.18, f32[1280]{0:T(1024)S(1)} %copy-done.19, f32[256]{0:T(256)S(1)} %add_rsqrt_fusion, f32[256]{0:T(256)S(1)} %broadcast_multiply_fusion), kind=kOutput, calls=%fused_computation.52 | convolution fusion | flops 211845120 | bytes 1651968 | tf_op jit(solution)/shard_map/dot_general | solution.py:43
  4.6 1.7 %fusion.34 = bf16[256,320]{0,1:T(8,128)(2,1)S(1)} fusion(bf16[3,1280,320]{1,2,0:T(8,128)(2,1)} %param.14, f32[320]{0:T(512)S(1)} %get-tuple-element.6, bf16[256,1280]{1,0:T(8,128)(2,1)S(1)} %copy-done.1, f32[1280]{0:T(1024)S(1)} %copy-done.18, f32[1280]{0:T(1024)S(1)} %copy-done.19, f32[256]{0:T(256)S(1)} %add_rsqrt_fusion, f32[256]{0:T(256)S(1)} %broadcast_multiply_fusion), kind=kOutput, calls=%fused_computation.53 | convolution fusion | flops 211845120 | bytes 1651968 | tf_op jit(solution)/shard_map/dot_general | solution.py:46
  6.4 0.7 pad_maximum_fusion.1
  7.1 5.2 %collective-permute-start.3 = (bf16[256,640]{0,1:T(8,128)(2,1)}, bf16[256,640]{0,1:T(8,128)(2,1)S(1)}, u32[]{:S(2)}, u32[]{:S(2)}) collective-permute-start(bf16[256,640]{0,1:T(8,128)(2,1)} %pad_maximum_fusion.1), channel_id=1, source_target_pairs={{0,16},{4,20},{8,24},{12,28},{16,32},{20,36},{24,40},{28,44},{32,4... | collective-permute-start | bytes 983048 | tf_op jit(solution)/shard_map/ppermute | solution.py:17
  12.3 1.3 collective-permute-start.4
  13.6 5.7 %collective-permute-start.1 = (bf16[256,640]{0,1:T(8,128)(2,1)}, bf16[256,640]{0,1:T(8,128)(2,1)}, u32[]{:S(2)}, u32[]{:S(2)}) collective-permute-start(bf16[256,640]{0,1:T(8,128)(2,1)} %pad_maximum_fusion.1), channel_id=1, source_target_pairs={{0,8},{4,12},{8,16},{12,20},{16,24},{20,28},{24,32},{28,36},{32,40... | collective-permute-start | bytes 983048 | tf_op jit(solution)/shard_map/ppermute | solution.py:17
  19.3 1.9 %collective-permute-start.2 = (bf16[256,640]{0,1:T(8,128)(2,1)}, bf16[256,640]{0,1:T(8,128)(2,1)}, u32[]{:S(2)}, u32[]{:S(2)}) collective-permute-start(bf16[256,640]{0,1:T(8,128)(2,1)} %pad_maximum_fusion.1), channel_id=1, source_target_pairs={{8,0},{12,4},{16,8},{20,12},{24,16},{28,20},{32,24},{36,28},{40,32... | collective-permute-start | bytes 983048 | tf_op jit(solution)/shard_map/ppermute | solution.py:17
  21.2 1.9 %collective-permute-start = (bf16[256,640]{0,1:T(8,128)(2,1)}, bf16[256,640]{0,1:T(8,128)(2,1)}, u32[]{:S(2)}, u32[]{:S(2)}) collective-permute-start(bf16[256,640]{0,1:T(8,128)(2,1)} %pad_maximum_fusion.1), channel_id=1, source_target_pairs={{0,4},{4,0},{8,12},{12,8},{16,20},{20,16},{24,28},{28,24},{32,36},... | collective-permute-start | bytes 983048 | tf_op jit(solution)/shard_map/ppermute | solution.py:99
  25.2 1.7 %fusion.32 = bf16[256,320]{0,1:T(8,128)(2,1)S(1)} fusion(bf16[3,1280,320]{1,2,0:T(8,128)(2,1)} %param.14, f32[320]{0:T(512)S(1)} %get-tuple-element.5, bf16[256,1280]{1,0:T(8,128)(2,1)S(1)} %copy-done.1, f32[1280]{0:T(1024)S(1)} %copy-done.18, f32[1280]{0:T(1024)S(1)} %copy-done.19, f32[256]{0:T(256)S(1)} %add_rsqrt_fusion, f32[256]{0:T(256)S(1)} %broadcast_multiply_fusion), kind=kOutput, calls=%fused_computation.51 | convolution fusion | flops 211845120 | bytes 1651968 | tf_op jit(solution)/shard_map/dot_general | solution.py:40
  26.9 1.2 broadcast_compare_fusion.8
  28.1 0.4 fusion.115
  28.5 0.7 fusion.91
  29.2 0.9 reduce_window_sum.11
  30.0 1.2 collective-permute-done.4
  31.3 2.9 %collective-permute-done.1 = bf16[256,640]{0,1:T(8,128)(2,1)} collective-permute-done((bf16[256,640]{0,1:T(8,128)(2,1)}, bf16[256,640]{0,1:T(8,128)(2,1)}, u32[]{:S(2)}, u32[]{:S(2)}) %collective-permute-start.1) | collective-permute-done | bytes 327712 | tf_op jit(solution)/shard_map/ppermute | solution.py:17
  34.2 4.9 %collective-permute-done.2 = bf16[256,640]{0,1:T(8,128)(2,1)} collective-permute-done((bf16[256,640]{0,1:T(8,128)(2,1)}, bf16[256,640]{0,1:T(8,128)(2,1)}, u32[]{:S(2)}, u32[]{:S(2)}) %collective-permute-start.2) | collective-permute-done | bytes 327712 | tf_op jit(solution)/shard_map/ppermute | solution.py:17
  39.1 1.1 pad_maximum_fusion
  40.2 1.9 %collective-permute-start.5 = (bf16[768,640]{0,1:T(8,128)(2,1)S(1)}, bf16[768,640]{0,1:T(8,128)(2,1)S(1)}, u32[]{:S(2)}, u32[]{:S(2)}) collective-permute-start(bf16[768,640]{0,1:T(8,128)(2,1)S(1)} %pad_maximum_fusion), channel_id=1, source_target_pairs={{0,4},{4,0},{8,12},{12,8},{16,20},{20,16},{24,28},{28,24},{32,36},... | collective-permute-start | bytes 2949128 | tf_op jit(solution)/shard_map/ppermute | solution.py:99
  42.2 0.4 fusion.110
  42.6 1.0 fusion.103
  43.7 1.0 fusion.102
  44.7 0.4 fusion.111
  45.1 1.0 fusion.101
  46.2 0.4 fusion.112
  46.6 0.4 fusion.113
  47.0 0.4 fusion.114
  47.5 0.7 copy-done.6
  48.2 0.4 fusion.109
  48.6 0.4 fusion.108
  49.1 0.4 fusion.107
  49.5 0.3 fusion.72
  49.8 0.3 fusion.39
  50.4 0.3 fusion.68
  50.7 0.3 fusion.43
  51.3 0.3 fusion.64
  51.6 0.3 fusion.47
  51.9 0.3 fusion.62
  52.7 0.3 fusion.35
  53.1 0.3 fusion.15
  53.4 0.4 fusion.31
  54.4 1.3 %convolution_convert_fusion.1 = bf16[4,64,1280]{2,1,0:T(8,128)(2,1)} fusion(bf16[4,64,320]{2,1,0:T(8,128)(2,1)S(1)} %convert_element_type.96, bf16[320,1280]{1,0:T(8,128)(2,1)S(1)} %copy-done), kind=kOutput, calls=%fused_computation.1 | convolution fusion | flops 210042880 | bytes 1638400 | tf_op jit(solution)/shard_map/tgc,cd->tgd/dot_general | solution.py:124
  55.7 4.3 %all-to-all-start = ((bf16[4,64,1280]{2,1,0:T(8,128)(2,1)}), bf16[4,64,1280]{2,1,0:T(8,128)(2,1)S(1)}, u32[]{:S(2)}, u32[]{:S(2)}) async-start(bf16[4,64,1280]{2,1,0:T(8,128)(2,1)} %convolution_convert_fusion.1), calls=%async_computation | async-start | bytes 1310720 | tf_op jit(solution)/shard_map/all_to_all | solution.py:127
  60.7 10.9 %all-to-all-done = bf16[4,64,1280]{2,1,0:T(8,128)(2,1)S(1)} async-done(((bf16[4,64,1280]{2,1,0:T(8,128)(2,1)}), bf16[4,64,1280]{2,1,0:T(8,128)(2,1)S(1)}, u32[]{:S(2)}, u32[]{:S(2)}) %all-to-all-start) | async-done | bytes 655392 | tf_op jit(solution)/shard_map/all_to_all | solution.py:127
  72.1 0.4 convolution_convert_fusion
  72.7 56.9 %all_to_all.17 = bf16[128,2,1280]{2,1,0:T(2,128)(2,1)S(1)} all-to-all(bf16[128,2,1280]{2,1,0:T(2,128)(2,1)S(1)} %all_to_all.12), channel_id=1, replica_groups=mesh['seq'=128,'tp'=4] {'seq'}, dimensions={0} | all-to-all | bytes 1310720 | tf_op jit(solution)/shard_map/all_to_all | solution.py:148
  129.7 1.1 all_to_all.14
  (89 shorter events, 5.2 us)
Async XLA Ops:
  0.0 54.4 %copy-start = (bf16[320,1280]{1,0:T(8,128)(2,1)S(1)}, bf16[320,1280]{1,0:T(8,128)(2,1)}, u32[]{:S(2)}) copy-start(bf16[320,1280]{1,0:T(8,128)(2,1)} %param.16) | copy-start | bytes 2457604
  0.0 2.9 %copy-start.1 = (bf16[256,1280]{1,0:T(8,128)(2,1)S(1)}, bf16[256,1280]{1,0:T(8,128)(2,1)}, u32[]{:S(2)}) copy-start(bf16[256,1280]{1,0:T(8,128)(2,1)} %param.11) | copy-start | bytes 1966084
  0.0 2.8 %copy-start.16 = (f32[3,320]{1,0:T(4,128)S(1)}, f32[3,320]{1,0:T(4,128)}, u32[]{:S(2)}) copy-start(f32[3,320]{1,0:T(4,128)} %param.15) | copy-start | bytes 11524
  0.0 2.9 %copy-start.19 = (f32[1280]{0:T(1024)S(1)}, f32[1280]{0:T(1024)}, u32[]{:S(2)}) copy-start(f32[1280]{0:T(1024)} %param.12) | copy-start | bytes 15364
  0.0 2.9 %copy-start.18 = (f32[1280]{0:T(1024)S(1)}, f32[1280]{0:T(1024)}, u32[]{:S(2)}) copy-start(f32[1280]{0:T(1024)} %param.13) | copy-start | bytes 15364
  4.6 1.8 %copy-start.2 = (bf16[256,320]{0,1:T(8,128)(2,1)}, bf16[256,320]{0,1:T(8,128)(2,1)S(1)}, u32[]{:S(2)}) copy-start(bf16[256,320]{0,1:T(8,128)(2,1)S(1)} %fusion.33) | copy-start | bytes 491524
  4.6 18.7 %copy-start.12 = (s32[8192]{0:T(1024)S(1)}, s32[8192]{0:T(1024)}, u32[]{:S(2)}) copy-start(s32[8192]{0:T(1024)} %param.20) | copy-start | bytes 98308
  7.1 22.9 %collective-permute-start.3 = (bf16[256,640]{0,1:T(8,128)(2,1)}, bf16[256,640]{0,1:T(8,128)(2,1)S(1)}, u32[]{:S(2)}, u32[]{:S(2)}) collective-permute-start(bf16[256,640]{0,1:T(8,128)(2,1)} %pad_maximum_fusion.1), channel_id=1, source_target_pairs={{0,16},{4,20},{8,24},{12,28},{16,32},{20,36},{24,40},{28,44},{32,4... | collective-permute-start | bytes 983048 | tf_op jit(solution)/shard_map/ppermute | solution.py:17
  12.3 18.9 %collective-permute-start.4 = (bf16[256,640]{0,1:T(8,128)(2,1)}, bf16[256,640]{0,1:T(8,128)(2,1)S(1)}, u32[]{:S(2)}, u32[]{:S(2)}) collective-permute-start(bf16[256,640]{0,1:T(8,128)(2,1)} %pad_maximum_fusion.1), channel_id=1, source_target_pairs={{16,0},{20,4},{24,8},{28,12},{32,16},{36,20},{40,24},{44,28},{48,3... | collective-permute-start | bytes 983048 | tf_op jit(solution)/shard_map/ppermute | solution.py:17
  13.6 20.6 %collective-permute-start.1 = (bf16[256,640]{0,1:T(8,128)(2,1)}, bf16[256,640]{0,1:T(8,128)(2,1)}, u32[]{:S(2)}, u32[]{:S(2)}) collective-permute-start(bf16[256,640]{0,1:T(8,128)(2,1)} %pad_maximum_fusion.1), channel_id=1, source_target_pairs={{0,8},{4,12},{8,16},{12,20},{16,24},{20,28},{24,32},{28,36},{32,40... | collective-permute-start | bytes 983048 | tf_op jit(solution)/shard_map/ppermute | solution.py:17
  19.3 19.8 %collective-permute-start.2 = (bf16[256,640]{0,1:T(8,128)(2,1)}, bf16[256,640]{0,1:T(8,128)(2,1)}, u32[]{:S(2)}, u32[]{:S(2)}) collective-permute-start(bf16[256,640]{0,1:T(8,128)(2,1)} %pad_maximum_fusion.1), channel_id=1, source_target_pairs={{8,0},{12,4},{16,8},{20,12},{24,16},{28,20},{32,24},{36,28},{40,32... | collective-permute-start | bytes 983048 | tf_op jit(solution)/shard_map/ppermute | solution.py:17
  21.2 23.9 %collective-permute-start = (bf16[256,640]{0,1:T(8,128)(2,1)}, bf16[256,640]{0,1:T(8,128)(2,1)}, u32[]{:S(2)}, u32[]{:S(2)}) collective-permute-start(bf16[256,640]{0,1:T(8,128)(2,1)} %pad_maximum_fusion.1), channel_id=1, source_target_pairs={{0,4},{4,0},{8,12},{12,8},{16,20},{20,16},{24,28},{28,24},{32,36},... | collective-permute-start | bytes 983048 | tf_op jit(solution)/shard_map/ppermute | solution.py:99
  25.2 2.9 %copy-start.3 = (bf16[256,320]{0,1:T(8,128)(2,1)S(1)}, bf16[256,320]{0,1:T(8,128)(2,1)}, u32[]{:S(2)}) copy-start(bf16[256,320]{0,1:T(8,128)(2,1)} %copy-done.2) | copy-start | bytes 491524
  26.9 1.6 %copy-start.17 = (s32[64,1]{0,1:T(1,128)S(1)}, s32[64,1]{0,1:T(1,128)}, u32[]{:S(2)}) copy-start(s32[64,1]{0,1:T(1,128)} %param.21) | copy-start | bytes 772
  31.3 10.9 %copy-start.11 = (pred[256,256]{0,1:T(8,128)(4,1)S(1)}, pred[256,256]{0,1:T(8,128)(4,1)}, u32[]{:S(2)}) copy-start(pred[256,256]{0,1:T(8,128)(4,1)} %get-tuple-element.58) | copy-start | bytes 196612
  40.2 7.2 %collective-permute-start.5 = (bf16[768,640]{0,1:T(8,128)(2,1)S(1)}, bf16[768,640]{0,1:T(8,128)(2,1)S(1)}, u32[]{:S(2)}, u32[]{:S(2)}) collective-permute-start(bf16[768,640]{0,1:T(8,128)(2,1)S(1)} %pad_maximum_fusion), channel_id=1, source_target_pairs={{0,4},{4,0},{8,12},{12,8},{16,20},{20,16},{24,28},{28,24},{32,36},... | collective-permute-start | bytes 2949128 | tf_op jit(solution)/shard_map/ppermute | solution.py:99
  42.6 2.1 %copy-start.10 = (pred[256,256]{0,1:T(8,128)(4,1)S(1)}, pred[256,256]{0,1:T(8,128)(4,1)}, u32[]{:S(2)}) copy-start(pred[256,256]{0,1:T(8,128)(4,1)} %get-tuple-element.57) | copy-start | bytes 196612
  43.7 2.5 %copy-start.9 = (pred[256,256]{0,1:T(8,128)(4,1)S(1)}, pred[256,256]{0,1:T(8,128)(4,1)}, u32[]{:S(2)}) copy-start(pred[256,256]{0,1:T(8,128)(4,1)} %get-tuple-element.56) | copy-start | bytes 196612
  45.1 1.5 %copy-start.8 = (pred[256,256]{0,1:T(8,128)(4,1)S(1)}, pred[256,256]{0,1:T(8,128)(4,1)}, u32[]{:S(2)}) copy-start(pred[256,256]{0,1:T(8,128)(4,1)} %get-tuple-element.55) | copy-start | bytes 196612
  46.2 0.8 copy-start.7
  47.4 0.8 copy-start.6
  47.4 1.2 copy-start.5
  48.2 0.8 copy-start.4
  55.7 15.9 %all-to-all-start = ((bf16[4,64,1280]{2,1,0:T(8,128)(2,1)}), bf16[4,64,1280]{2,1,0:T(8,128)(2,1)S(1)}, u32[]{:S(2)}, u32[]{:S(2)}) async-start(bf16[4,64,1280]{2,1,0:T(8,128)(2,1)} %convolution_convert_fusion.1), calls=%async_computation | async-start | bytes 1310720 | tf_op jit(solution)/shard_map/all_to_all | solution.py:127
  60.2 11.5 %copy-start.13 = (f32[1280]{0:T(1024)S(1)}, f32[1280]{0:T(1024)}, u32[]{:S(2)}) copy-start(f32[1280]{0:T(1024)} %param.17) | copy-start | bytes 15364
  60.7 11.3 %copy-start.14 = (f32[1280]{0:T(1024)S(1)}, f32[1280]{0:T(1024)}, u32[]{:S(2)}) copy-start(f32[1280]{0:T(1024)} %param.19) | copy-start | bytes 15364
  60.7 11.3 %copy-start.15 = (f32[1280]{0:T(1024)S(1)}, f32[1280]{0:T(1024)}, u32[]{:S(2)}) copy-start(f32[1280]{0:T(1024)} %param.18) | copy-start | bytes 15364

commit v4 on v2

--- a/solution.py
+++ b/solution.py
@@ -40,13 +40,9 @@
     query = (jnp.dot(normed, w_qkv[0], preferred_element_type=jnp.float32) + b_qkv[0]).astype(
         jnp.bfloat16
     )
-    key_rows = (jnp.dot(normed, w_qkv[1], preferred_element_type=jnp.float32) + b_qkv[1]).astype(
-        jnp.bfloat16
-    )
-    value_rows = (jnp.dot(normed, w_qkv[2], preferred_element_type=jnp.float32) + b_qkv[2]).astype(
-        jnp.bfloat16
-    )
-    key_value = jnp.concatenate([key_rows, value_rows], axis=1)
+    key_value = (
+        jnp.einsum("tc,kcd->tkd", normed, w_qkv[1:], preferred_element_type=jnp.float32) + b_qkv[1:]
+    ).astype(jnp.bfloat16).reshape(tok_dev, 2 * local_width)
     group_rows = tok_dev // 4
     reach_groups = SPAN * group_rows
     padding = jnp.full((reach_groups,), -1, jnp.int32)
@@ -103,17 +99,17 @@
 
     below_2 = from_behind(key_value, "seq", 2)
     above_2 = from_behind(key_value, "seq", -2)
+    below_4 = from_behind(key_value, "seq", 4)
+    above_4 = from_behind(key_value, "seq", -4)
     partner_own = swap(key_value)
     state = absorb(start_state, key_value, query_segment)
-    below_4 = from_behind(below_2, "seq", 2)
-    above_4 = from_behind(above_2, "seq", -2)
     partner_near = swap(jnp.concatenate([below_2, above_2], axis=0))
+    partner_far = swap(jnp.where(sign > 0, above_4, below_4))
     state = absorb_at(state, partner_own, sign)
     state = absorb_at(state, below_2, -2)
     state = absorb_at(state, above_2, 2)
     state = absorb_at(state, partner_near[:tok_dev], sign - 2)
     state = absorb_at(state, partner_near[tok_dev:], sign + 2)
-    partner_far = swap(jnp.where(sign > 0, above_4, below_4))
     state = absorb_at(state, below_4, -4)
     state = absorb_at(state, above_4, 4)
     state = absorb_at(state, partner_far, -3 * sign)

time: 133 us -> 127 us (0.955)
  waiting for transfers between devices: 17.7 us -> 10.9 us
  local copies, waits for them, and re-layouts: 7.01 us -> 9.39 us
    ppermute x4, waiting for transfers between devices: 6.85 us -> 0.01 us  [from_behind(): lax.ppermute(value, axis, [(source, source + steps) for source in range(l...]
    slice x6 -> x7, local copies, waits for them, and re-layouts: 0.16 us -> 2.18 us  [block_scores(): value_heads = block[:, local_width:].reshape(-1, local_heads, HEAD_DIM)]
    dot_general x2 -> x1, matrix products: 3.35 us -> 2.92 us  [per_device(): jnp.einsum('tc,kcd->tkd', normed, w_qkv[1:], preferred_element_type=jnp.f...]
  transfers between devices with their start and end apart: 8 -> 8, of which waited for: 3 -> 1; matrix products, arithmetic and copies ran while one was open for 11% -> 13% of each run, Pallas kernels for 0% -> 0%
where the time goes in v4:
time: 127 us; the launch traced here: 126 us
  blocking collectives  57.9 us (46%)
  starting transfers between devices  25.4 us (20%)
  matrix products  13.4 us (11%)
  waiting for transfers between devices  10.9 us (9%)
  local copies, waits for them, and re-layouts  9.39 us (7%)
  other arithmetic  8.54 us (7%)
    all_to_all x1, blocking collectives, per_device(): lax.all_to_all(outgoing, 'seq', split_axis=0, concat_axis=0, tiled=True)  57.9 us
    ppermute x4, starting transfers between devices, from_behind(): lax.ppermute(value, axis, [(source, source + steps) for source in range(l...  15.4 us
    all_to_all x1, waiting for transfers between devices, per_device(): lax.all_to_all(head_term, 'tp', split_axis=0, concat_axis=0, tiled=True)  10.9 us
    ppermute x3, starting transfers between devices, swap(): return lax.ppermute(value, 'seq', [(i, i ^ 1) for i in range(seq_count)])  6.38 us
    dot_general x9, matrix products, block_scores(): jnp.einsum('qhd,khd->hqk', query_heads, key_heads, preferred_element_type...  4.23 us
    eq x9, local copies, waits for them, and re-layouts, block_scores(): allowed = query_segment[:, None] == key_segment[None, :]  3.85 us
    all_to_all x1, starting transfers between devices, per_device(): lax.all_to_all(head_term, 'tp', split_axis=0, concat_axis=0, tiled=True)  3.66 us
    dot_general x1, matrix products, per_device(): jnp.einsum('tc,kcd->tkd', normed, w_qkv[1:], preferred_element_type=jnp.f...  2.92 us
  transfers between devices with their start and end apart: 8, of which 1 were waited for; matrix products, arithmetic and copies ran while one was open for 13% of the time, Pallas kernels for 0%

profile of v4, /device:TPU:32, one launch (start us, length us, event | category | flops | bytes accessed | tf_op | source)
XLA Modules:
  0.0 126.4 jit_solution(5505705240104473773)
XLA Ops:
  0.0 1.4 %convert_reduce_fusion = f32[256]{0:T(256)S(1)} fusion(bf16[256,1280]{1,0:T(8,128)(2,1)} %param.11), kind=kLoop, calls=%fused_computation.5 | loop fusion | flops 655104 | bytes 656384 | tf_op jit(solution)/shard_map/reduce_sum | solution.py:21
  1.4 1.4 %fusion.13 = f32[256]{0:T(256)S(1)} fusion(bf16[256,1280]{1,0:T(8,128)(2,1)} %param.11, f32[256]{0:T(256)S(1)} %broadcast_multiply_fusion), kind=kLoop, calls=%fused_computation.26 | loop fusion | flops 1310464 | bytes 657408 | tf_op jit(solution)/shard_map/reduce_sum | solution.py:23
  2.9 2.9 %fusion.20 = bf16[256,2,320]{0,2,1:T(8,128)(2,1)} fusion(bf16[3,1280,320]{1,2,0:T(8,128)(2,1)} %param.14, f32[2,320]{1,0:T(2,128)S(1)} %slice.75, bf16[256,1280]{1,0:T(8,128)(2,1)S(1)} %copy-done.1, f32[1280]{0:T(1024)S(1)} %copy-done.19, f32[1280]{0:T(1024)S(1)} %copy-done.20, f32[256]{0:T(256)S(1)} %add_rsqrt_fusion, f32[256]{0:T(256)S(1)} %broadcast_multiply_fusion), kind=kOutput, calls=%fused_computation.32 | convolution fusion | flops 421724160 | bytes 2636288 | tf_op jit(solution)/shard_map/tc,kcd->tkd/dot_general | solution.py:44
  5.8 3.8 %collective-permute-start.1 = (bf16[256,640]{0,1:T(8,128)(2,1)}, bf16[256,640]{0,1:T(8,128)(2,1)S(1)}, u32[]{:S(2)}, u32[]{:S(2)}) collective-permute-start(bf16[256,640]{0,1:T(8,128)(2,1)} %bitcast.4), channel_id=1, source_target_pairs={{0,8},{4,12},{8,16},{12,20},{16,24},{20,28},{24,32},{28,36},{32,40... | collective-permute-start | bytes 983048 | tf_op jit(solution)/shard_map/ppermute | solution.py:17
  9.6 4.8 %collective-permute-start.2 = (bf16[256,640]{0,1:T(8,128)(2,1)}, bf16[256,640]{0,1:T(8,128)(2,1)S(1)}, u32[]{:S(2)}, u32[]{:S(2)}) collective-permute-start(bf16[256,640]{0,1:T(8,128)(2,1)} %bitcast.4), channel_id=1, source_target_pairs={{8,0},{12,4},{16,8},{20,12},{24,16},{28,20},{32,24},{36,28},{40,32... | collective-permute-start | bytes 983048 | tf_op jit(solution)/shard_map/ppermute | solution.py:17
  14.5 1.3 %collective-permute-start.5 = (bf16[256,640]{0,1:T(8,128)(2,1)}, bf16[256,640]{0,1:T(8,128)(2,1)S(1)}, u32[]{:S(2)}, u32[]{:S(2)}) collective-permute-start(bf16[256,640]{0,1:T(8,128)(2,1)} %bitcast.4), channel_id=1, source_target_pairs={{16,0},{20,4},{24,8},{28,12},{32,16},{36,20},{40,24},{44,28},{48,3... | collective-permute-start | bytes 983048 | tf_op jit(solution)/shard_map/ppermute | solution.py:17
  15.8 5.5 %collective-permute-start.4 = (bf16[256,640]{0,1:T(8,128)(2,1)}, bf16[256,640]{0,1:T(8,128)(2,1)S(1)}, u32[]{:S(2)}, u32[]{:S(2)}) collective-permute-start(bf16[256,640]{0,1:T(8,128)(2,1)} %bitcast.4), channel_id=1, source_target_pairs={{0,16},{4,20},{8,24},{12,28},{16,32},{20,36},{24,40},{28,44},{32,4... | collective-permute-start | bytes 983048 | tf_op jit(solution)/shard_map/ppermute | solution.py:17
  21.2 1.9 %collective-permute-start = (bf16[256,640]{0,1:T(8,128)(2,1)}, bf16[256,640]{0,1:T(8,128)(2,1)}, u32[]{:S(2)}, u32[]{:S(2)}) collective-permute-start(bf16[256,640]{0,1:T(8,128)(2,1)} %bitcast.4), channel_id=1, source_target_pairs={{0,4},{4,0},{8,12},{12,8},{16,20},{20,16},{24,28},{28,24},{32,36},... | collective-permute-start | bytes 983048 | tf_op jit(solution)/shard_map/ppermute | solution.py:95
  23.3 1.0 fusion.104
  25.4 0.7 eq.202
  26.2 0.7 eq.205
  27.0 0.7 eq.208
  27.7 0.7 eq.211
  28.4 0.7 eq.214
  29.1 1.7 %fusion.40 = bf16[256,320]{0,1:T(8,128)(2,1)S(1)} fusion(bf16[3,1280,320]{1,2,0:T(8,128)(2,1)} %param.14, f32[320]{0:T(512)S(1)} %slice_reduce_fusion, bf16[256,1280]{1,0:T(8,128)(2,1)S(1)} %copy-done.1, f32[1280]{0:T(1024)S(1)} %copy-done.19, f32[1280]{0:T(1024)S(1)} %copy-done.20, f32[256]{0:T(256)S(1)} %add_rsqrt_fusion, f32[256]{0:T(256)S(1)} %broadcast_multiply_fusion), kind=kOutput, calls=%fused_computation.53 | convolution fusion | flops 211845120 | bytes 1651968 | tf_op jit(solution)/shard_map/dot_general | solution.py:40
  30.9 1.2 broadcast_compare_fusion.8
  32.1 0.7 fusion.94
  32.7 1.4 %reduce_window_sum.11 = s32[64,128]{1,0:T(8,128)} reduce-window(s32[64,128]{1,0:T(8,128)} %fusion.94, s32[]{:T(128)} %constant.131.clone.1), window={size=64x1 pad=63_0x0_0}, to_apply=%region_0.0 | reduce-window | flops 516096 | bytes 65540 | tf_op jit(solution)/shard_map/jit(cumsum)/reduce_window_sum | solution.py:136
  34.2 1.2 fusion.119
  35.5 2.4 %collective-permute-start.3 = (bf16[512,640]{0,1:T(8,128)(2,1)S(1)}, bf16[512,640]{0,1:T(8,128)(2,1)S(1)}, u32[]{:S(2)}, u32[]{:S(2)}) collective-permute-start(bf16[512,640]{0,1:T(8,128)(2,1)S(1)} %pad_maximum_fusion), channel_id=1, source_target_pairs={{0,4},{4,0},{8,12},{12,8},{16,20},{20,16},{24,28},{28,24},{32,36},... | collective-permute-start | bytes 1966088 | tf_op jit(solution)/shard_map/ppermute | solution.py:95
  38.0 2.1 %collective-permute-start.6 = (bf16[256,640]{0,1:T(8,128)(2,1)S(1)}, bf16[256,640]{0,1:T(8,128)(2,1)S(1)}, u32[]{:S(2)}, u32[]{:S(2)}) collective-permute-start(bf16[256,640]{0,1:T(8,128)(2,1)S(1)} %broadcast_select_fusion), channel_id=1, source_target_pairs={{0,4},{4,0},{8,12},{12,8},{16,20},{20,16},{24,28},{28,24},{32,36},... | collective-permute-start | bytes 983048 | tf_op jit(solution)/shard_map/ppermute | solution.py:95
  40.1 0.4 fusion.112
  40.5 0.4 fusion.113
  40.9 0.4 copy-done.3
  41.3 0.4 fusion.116
  41.7 0.4 fusion.117
  42.1 1.0 fusion.103
  43.2 0.4 fusion.118
  43.6 0.4 fusion.111
  44.0 0.4 fusion.114
  44.4 0.4 fusion.115
  45.1 0.3 fusion.45
  45.4 0.3 fusion.73
  45.7 0.3 fusion.71
  46.0 0.3 fusion.49
  46.6 0.3 fusion.67
  46.9 0.3 fusion.53
  47.2 0.3 fusion.65
  48.0 0.3 fusion.41
  48.4 0.3 fusion.23
  48.7 0.4 fusion.39
  49.7 1.3 %convolution_convert_fusion.1 = bf16[4,64,1280]{2,1,0:T(8,128)(2,1)} fusion(bf16[4,64,320]{2,1,0:T(8,128)(2,1)S(1)} %convert_element_type.92, bf16[320,1280]{1,0:T(8,128)(2,1)S(1)} %copy-done), kind=kOutput, calls=%fused_computation.1 | convolution fusion | flops 210042880 | bytes 1638400 | tf_op jit(solution)/shard_map/tgc,cd->tgd/dot_general | solution.py:121
  51.0 3.7 %all-to-all-start = ((bf16[4,64,1280]{2,1,0:T(8,128)(2,1)}), bf16[4,64,1280]{2,1,0:T(8,128)(2,1)S(1)}, u32[]{:S(2)}, u32[]{:S(2)}) async-start(bf16[4,64,1280]{2,1,0:T(8,128)(2,1)} %convolution_convert_fusion.1), calls=%async_computation | async-start | bytes 1310720 | tf_op jit(solution)/shard_map/all_to_all | solution.py:124
  55.1 0.3 dynamic-slice_convert_fusion
  55.4 10.9 %all-to-all-done = bf16[4,64,1280]{2,1,0:T(8,128)(2,1)S(1)} async-done(((bf16[4,64,1280]{2,1,0:T(8,128)(2,1)}), bf16[4,64,1280]{2,1,0:T(8,128)(2,1)S(1)}, u32[]{:S(2)}, u32[]{:S(2)}) %all-to-all-start) | async-done | bytes 655392 | tf_op jit(solution)/shard_map/all_to_all | solution.py:124
  66.8 0.4 convolution_convert_fusion
  67.4 57.9 %all_to_all.17 = bf16[128,2,1280]{2,1,0:T(2,128)(2,1)S(1)} all-to-all(bf16[128,2,1280]{2,1,0:T(2,128)(2,1)S(1)} %all_to_all.12), channel_id=1, replica_groups=mesh['seq'=128,'tp'=4] {'seq'}, dimensions={0} | all-to-all | bytes 1310720 | tf_op jit(solution)/shard_map/all_to_all | solution.py:145
  125.3 1.1 all_to_all.14
  (94 shorter events, 4.4 us)
Async XLA Ops:
  0.0 49.7 %copy-start = (bf16[320,1280]{1,0:T(8,128)(2,1)S(1)}, bf16[320,1280]{1,0:T(8,128)(2,1)}, u32[]{:S(2)}) copy-start(bf16[320,1280]{1,0:T(8,128)(2,1)} %param.16) | copy-start | bytes 2457604
  0.0 2.8 %copy-start.1 = (bf16[256,1280]{1,0:T(8,128)(2,1)S(1)}, bf16[256,1280]{1,0:T(8,128)(2,1)}, u32[]{:S(2)}) copy-start(bf16[256,1280]{1,0:T(8,128)(2,1)} %param.11) | copy-start | bytes 1966084
  0.0 2.8 %copy-start.16 = (f32[3,320]{1,0:T(4,128)S(1)}, f32[3,320]{1,0:T(4,128)}, u32[]{:S(2)}) copy-start(f32[3,320]{1,0:T(4,128)} %param.15) | copy-start | bytes 11524
  0.0 2.8 %copy-start.20 = (f32[1280]{0:T(1024)S(1)}, f32[1280]{0:T(1024)}, u32[]{:S(2)}) copy-start(f32[1280]{0:T(1024)} %param.12) | copy-start | bytes 15364
  0.0 2.8 %copy-start.19 = (f32[1280]{0:T(1024)S(1)}, f32[1280]{0:T(1024)}, u32[]{:S(2)}) copy-start(f32[1280]{0:T(1024)} %param.13) | copy-start | bytes 15364
  2.9 21.6 %copy-start.7 = (s32[8192]{0:T(1024)S(1)}, s32[8192]{0:T(1024)}, u32[]{:S(2)}) copy-start(s32[8192]{0:T(1024)} %param.20) | copy-start | bytes 98308
  5.8 29.6 %collective-permute-start.1 = (bf16[256,640]{0,1:T(8,128)(2,1)}, bf16[256,640]{0,1:T(8,128)(2,1)S(1)}, u32[]{:S(2)}, u32[]{:S(2)}) collective-permute-start(bf16[256,640]{0,1:T(8,128)(2,1)} %bitcast.4), channel_id=1, source_target_pairs={{0,8},{4,12},{8,16},{12,20},{16,24},{20,28},{24,32},{28,36},{32,40... | collective-permute-start | bytes 983048 | tf_op jit(solution)/shard_map/ppermute | solution.py:17
  9.6 25.8 %collective-permute-start.2 = (bf16[256,640]{0,1:T(8,128)(2,1)}, bf16[256,640]{0,1:T(8,128)(2,1)S(1)}, u32[]{:S(2)}, u32[]{:S(2)}) collective-permute-start(bf16[256,640]{0,1:T(8,128)(2,1)} %bitcast.4), channel_id=1, source_target_pairs={{8,0},{12,4},{16,8},{20,12},{24,16},{28,20},{32,24},{36,28},{40,32... | collective-permute-start | bytes 983048 | tf_op jit(solution)/shard_map/ppermute | solution.py:17
  14.5 23.4 %collective-permute-start.5 = (bf16[256,640]{0,1:T(8,128)(2,1)}, bf16[256,640]{0,1:T(8,128)(2,1)S(1)}, u32[]{:S(2)}, u32[]{:S(2)}) collective-permute-start(bf16[256,640]{0,1:T(8,128)(2,1)} %bitcast.4), channel_id=1, source_target_pairs={{16,0},{20,4},{24,8},{28,12},{32,16},{36,20},{40,24},{44,28},{48,3... | collective-permute-start | bytes 983048 | tf_op jit(solution)/shard_map/ppermute | solution.py:17
  15.8 22.1 %collective-permute-start.4 = (bf16[256,640]{0,1:T(8,128)(2,1)}, bf16[256,640]{0,1:T(8,128)(2,1)S(1)}, u32[]{:S(2)}, u32[]{:S(2)}) collective-permute-start(bf16[256,640]{0,1:T(8,128)(2,1)} %bitcast.4), channel_id=1, source_target_pairs={{0,16},{4,20},{8,24},{12,28},{16,32},{20,36},{24,40},{28,44},{32,4... | collective-permute-start | bytes 983048 | tf_op jit(solution)/shard_map/ppermute | solution.py:17
  21.2 20.9 %collective-permute-start = (bf16[256,640]{0,1:T(8,128)(2,1)}, bf16[256,640]{0,1:T(8,128)(2,1)}, u32[]{:S(2)}, u32[]{:S(2)}) collective-permute-start(bf16[256,640]{0,1:T(8,128)(2,1)} %bitcast.4), channel_id=1, source_target_pairs={{0,4},{4,0},{8,12},{12,8},{16,20},{20,16},{24,28},{28,24},{32,36},... | collective-permute-start | bytes 983048 | tf_op jit(solution)/shard_map/ppermute | solution.py:95
  29.1 1.7 %copy-start.11 = (s32[256]{0:T(256)S(1)}, s32[256]{0:T(256)}, u32[]{:S(2)}) copy-start(s32[256]{0:T(256)} %eq.202) | copy-start | bytes 3076
  29.1 1.7 %copy-start.12 = (s32[256]{0:T(256)S(1)}, s32[256]{0:T(256)}, u32[]{:S(2)}) copy-start(s32[256]{0:T(256)} %eq.205) | copy-start | bytes 3076
  29.1 1.7 %copy-start.13 = (s32[256]{0:T(256)S(1)}, s32[256]{0:T(256)}, u32[]{:S(2)}) copy-start(s32[256]{0:T(256)} %eq.208) | copy-start | bytes 3076
  29.1 1.7 %copy-start.14 = (s32[256]{0:T(256)S(1)}, s32[256]{0:T(256)}, u32[]{:S(2)}) copy-start(s32[256]{0:T(256)} %eq.211) | copy-start | bytes 3076
  29.1 1.7 %copy-start.15 = (s32[256]{0:T(256)S(1)}, s32[256]{0:T(256)}, u32[]{:S(2)}) copy-start(s32[256]{0:T(256)} %eq.214) | copy-start | bytes 3076
  29.1 2.9 %copy-start.17 = (s32[64,1]{0,1:T(1,128)S(1)}, s32[64,1]{0,1:T(1,128)}, u32[]{:S(2)}) copy-start(s32[64,1]{0,1:T(1,128)} %param.21) | copy-start | bytes 772
  35.4 4.7 %copy-start.5 = (pred[256,256]{0,1:T(8,128)(4,1)S(1)}, pred[256,256]{0,1:T(8,128)(4,1)}, u32[]{:S(2)}) copy-start(pred[256,256]{0,1:T(8,128)(4,1)} %get-tuple-element.59) | copy-start | bytes 196612
  35.5 8.5 %collective-permute-start.3 = (bf16[512,640]{0,1:T(8,128)(2,1)S(1)}, bf16[512,640]{0,1:T(8,128)(2,1)S(1)}, u32[]{:S(2)}, u32[]{:S(2)}) collective-permute-start(bf16[512,640]{0,1:T(8,128)(2,1)S(1)} %pad_maximum_fusion), channel_id=1, source_target_pairs={{0,4},{4,0},{8,12},{12,8},{16,20},{20,16},{24,28},{28,24},{32,36},... | collective-permute-start | bytes 1966088 | tf_op jit(solution)/shard_map/ppermute | solution.py:95
  38.0 2.5 %copy-start.4 = (pred[256,256]{0,1:T(8,128)(4,1)S(1)}, pred[256,256]{0,1:T(8,128)(4,1)}, u32[]{:S(2)}) copy-start(pred[256,256]{0,1:T(8,128)(4,1)} %get-tuple-element.58) | copy-start | bytes 196612
  38.0 5.6 %collective-permute-start.6 = (bf16[256,640]{0,1:T(8,128)(2,1)S(1)}, bf16[256,640]{0,1:T(8,128)(2,1)S(1)}, u32[]{:S(2)}, u32[]{:S(2)}) collective-permute-start(bf16[256,640]{0,1:T(8,128)(2,1)S(1)} %broadcast_select_fusion), channel_id=1, source_target_pairs={{0,4},{4,0},{8,12},{12,8},{16,20},{20,16},{24,28},{28,24},{32,36},... | collective-permute-start | bytes 983048 | tf_op jit(solution)/shard_map/ppermute | solution.py:95
  40.5 0.8 copy-start.3
  40.9 0.8 copy-start.2
  49.7 5.0 %copy-start.6 = (s32[64,128]{1,0:T(8,128)S(1)}, s32[64,128]{1,0:T(8,128)}, u32[]{:S(2)}) copy-start(s32[64,128]{1,0:T(8,128)} %reduce_window_sum.11) | copy-start | bytes 98308
  49.7 5.0 %copy-start.18 = (s32[64,1]{0,1:T(1,128)S(1)}, s32[64,1]{0,1:T(1,128)}, u32[]{:S(2)}) copy-start(s32[64,1]{0,1:T(1,128)} %param.21) | copy-start | bytes 772
  51.0 15.3 %all-to-all-start = ((bf16[4,64,1280]{2,1,0:T(8,128)(2,1)}), bf16[4,64,1280]{2,1,0:T(8,128)(2,1)S(1)}, u32[]{:S(2)}, u32[]{:S(2)}) async-start(bf16[4,64,1280]{2,1,0:T(8,128)(2,1)} %convolution_convert_fusion.1), calls=%async_computation | async-start | bytes 1310720 | tf_op jit(solution)/shard_map/all_to_all | solution.py:124
  54.9 11.5 %copy-start.8 = (f32[1280]{0:T(1024)S(1)}, f32[1280]{0:T(1024)}, u32[]{:S(2)}) copy-start(f32[1280]{0:T(1024)} %param.17) | copy-start | bytes 15364
  55.4 11.4 %copy-start.9 = (f32[1280]{0:T(1024)S(1)}, f32[1280]{0:T(1024)}, u32[]{:S(2)}) copy-start(f32[1280]{0:T(1024)} %param.19) | copy-start | bytes 15364
  55.4 11.4 %copy-start.10 = (f32[1280]{0:T(1024)S(1)}, f32[1280]{0:T(1024)}, u32[]{:S(2)}) copy-start(f32[1280]{0:T(1024)} %param.18) | copy-start | bytes 15364

commit v5 on v4

--- a/solution.py
+++ b/solution.py
@@ -48,9 +48,14 @@
     padding = jnp.full((reach_groups,), -1, jnp.int32)
     padded_segment = jnp.concatenate([padding, segments, padding])
 
+    window_segment = lax.optimization_barrier(
+        jnp.repeat(
+            lax.dynamic_slice_in_dim(padded_segment, seq_index * group_rows, (2 * SPAN + 1) * group_rows), 4
+        )
+    )
+
     def segment_window(key_start, length):
-        groups = lax.dynamic_slice_in_dim(padded_segment, key_start // 4 + reach_groups, length // 4)
-        return jnp.repeat(groups, 4)
+        return lax.dynamic_slice_in_dim(window_segment, key_start - row_start + reach_rows, length)
 
     query_segment = segment_window(row_start, tok_dev)
     query_heads = query.reshape(tok_dev, local_heads, HEAD_DIM)

time: 127 us -> 126 us (level)
  local copies, waits for them, and re-layouts: 9.39 us -> 5.82 us
  blocking collectives: 57.9 us -> 59.3 us
    eq x9 -> x0, local copies, waits for them, and re-layouts: 3.85 us -> none  [block_scores(): allowed = query_segment[:, None] == key_segment[None, :]]
    all_to_all x1, blocking collectives: 57.9 us -> 59.3 us  [per_device(): lax.all_to_all(outgoing, 'seq', split_axis=0, concat_axis=0, tiled=True)]
  transfers between devices with their start and end apart: 8 -> 8, of which waited for: 1 -> 2; matrix products, arithmetic and copies ran while one was open for 13% -> 10% of each run, Pallas kernels for 0% -> 0%
where the time goes in v5:
time: 126 us; the launch traced here: 125 us
  blocking collectives  59.3 us (47%)
  starting transfers between devices  26.1 us (21%)
  matrix products  13.4 us (11%)
  waiting for transfers between devices  11.2 us (9%)
  other arithmetic  8.55 us (7%)
  local copies, waits for them, and re-layouts  5.82 us (5%)
    all_to_all x1, blocking collectives, per_device(): lax.all_to_all(outgoing, 'seq', split_axis=0, concat_axis=0, tiled=True)  59.3 us
    ppermute x4, starting transfers between devices, from_behind(): lax.ppermute(value, axis, [(source, source + steps) for source in range(l...  15.4 us
    all_to_all x1, waiting for transfers between devices, per_device(): lax.all_to_all(head_term, 'tp', split_axis=0, concat_axis=0, tiled=True)  10.9 us
    ppermute x3, starting transfers between devices, swap(): return lax.ppermute(value, 'seq', [(i, i ^ 1) for i in range(seq_count)])  6.39 us
    all_to_all x1, starting transfers between devices, per_device(): lax.all_to_all(head_term, 'tp', split_axis=0, concat_axis=0, tiled=True)  4.31 us
    dot_general x9, matrix products, block_scores(): jnp.einsum('qhd,khd->hqk', query_heads, key_heads, preferred_element_type...  4.21 us
    dot_general x1, matrix products, per_device(): jnp.einsum('tc,kcd->tkd', normed, w_qkv[1:], preferred_element_type=jnp.f...  2.91 us
    dot_general x9, matrix products, absorb(): jnp.einsum('hqk,khd->hqd', weights.astype(jnp.bfloat16), value_heads, pre...  2.85 us
  transfers between devices with their start and end apart: 8, of which 2 were waited for; matrix products, arithmetic and copies ran while one was open for 10% of the time, Pallas kernels for 0%

profile of v5, /device:TPU:32, one launch (start us, length us, event | category | flops | bytes accessed | tf_op | source)
XLA Modules:
  0.0 125.0 jit_solution(2489035881763951900)
XLA Ops:
  0.0 1.4 %convert_reduce_fusion = f32[256]{0:T(256)S(1)} fusion(bf16[256,1280]{1,0:T(8,128)(2,1)} %param.11), kind=kLoop, calls=%fused_computation.5 | loop fusion | flops 655104 | bytes 656384 | tf_op jit(solution)/shard_map/reduce_sum | solution.py:21
  1.4 1.4 %fusion.13 = f32[256]{0:T(256)S(1)} fusion(bf16[256,1280]{1,0:T(8,128)(2,1)} %param.11, f32[256]{0:T(256)S(1)} %broadcast_multiply_fusion), kind=kLoop, calls=%fused_computation.26 | loop fusion | flops 1310464 | bytes 657408 | tf_op jit(solution)/shard_map/reduce_sum | solution.py:23
  2.9 2.9 %fusion.20 = bf16[256,2,320]{0,2,1:T(8,128)(2,1)} fusion(bf16[3,1280,320]{1,2,0:T(8,128)(2,1)} %param.14, f32[2,320]{1,0:T(2,128)S(1)} %slice.79, bf16[256,1280]{1,0:T(8,128)(2,1)S(1)} %copy-done.1, f32[1280]{0:T(1024)S(1)} %copy-done.14, f32[1280]{0:T(1024)S(1)} %copy-done.15, f32[256]{0:T(256)S(1)} %add_rsqrt_fusion, f32[256]{0:T(256)S(1)} %broadcast_multiply_fusion), kind=kOutput, calls=%fused_computation.32 | convolution fusion | flops 421724160 | bytes 2636288 | tf_op jit(solution)/shard_map/tc,kcd->tkd/dot_general | solution.py:44
  5.8 3.8 %collective-permute-start.1 = (bf16[256,640]{0,1:T(8,128)(2,1)}, bf16[256,640]{0,1:T(8,128)(2,1)S(1)}, u32[]{:S(2)}, u32[]{:S(2)}) collective-permute-start(bf16[256,640]{0,1:T(8,128)(2,1)} %bitcast.4), channel_id=1, source_target_pairs={{0,8},{4,12},{8,16},{12,20},{16,24},{20,28},{24,32},{28,36},{32,40... | collective-permute-start | bytes 983048 | tf_op jit(solution)/shard_map/ppermute | solution.py:17
  9.6 4.8 %collective-permute-start.2 = (bf16[256,640]{0,1:T(8,128)(2,1)}, bf16[256,640]{0,1:T(8,128)(2,1)S(1)}, u32[]{:S(2)}, u32[]{:S(2)}) collective-permute-start(bf16[256,640]{0,1:T(8,128)(2,1)} %bitcast.4), channel_id=1, source_target_pairs={{8,0},{12,4},{16,8},{20,12},{24,16},{28,20},{32,24},{36,28},{40,32... | collective-permute-start | bytes 983048 | tf_op jit(solution)/shard_map/ppermute | solution.py:17
  14.5 1.3 %collective-permute-start.5 = (bf16[256,640]{0,1:T(8,128)(2,1)}, bf16[256,640]{0,1:T(8,128)(2,1)S(1)}, u32[]{:S(2)}, u32[]{:S(2)}) collective-permute-start(bf16[256,640]{0,1:T(8,128)(2,1)} %bitcast.4), channel_id=1, source_target_pairs={{16,0},{20,4},{24,8},{28,12},{32,16},{36,20},{40,24},{44,28},{48,3... | collective-permute-start | bytes 983048 | tf_op jit(solution)/shard_map/ppermute | solution.py:17
  15.8 5.5 %collective-permute-start.4 = (bf16[256,640]{0,1:T(8,128)(2,1)}, bf16[256,640]{0,1:T(8,128)(2,1)S(1)}, u32[]{:S(2)}, u32[]{:S(2)}) collective-permute-start(bf16[256,640]{0,1:T(8,128)(2,1)} %bitcast.4), channel_id=1, source_target_pairs={{0,16},{4,20},{8,24},{12,28},{16,32},{20,36},{24,40},{28,44},{32,4... | collective-permute-start | bytes 983048 | tf_op jit(solution)/shard_map/ppermute | solution.py:17
  21.2 1.9 %collective-permute-start = (bf16[256,640]{0,1:T(8,128)(2,1)}, bf16[256,640]{0,1:T(8,128)(2,1)}, u32[]{:S(2)}, u32[]{:S(2)}) collective-permute-start(bf16[256,640]{0,1:T(8,128)(2,1)} %bitcast.4), channel_id=1, source_target_pairs={{0,4},{4,0},{8,12},{12,8},{16,20},{20,16},{24,28},{28,24},{32,36},... | collective-permute-start | bytes 983048 | tf_op jit(solution)/shard_map/ppermute | solution.py:100
  23.2 1.7 %fusion.106 = (bf16[256,320]{0,1:T(8,128)(2,1)S(1)}, bf16[256,320]{0,1:T(8,128)(2,1)}) fusion(bf16[256,640]{0,1:T(8,128)(2,1)} %bitcast.4), kind=kLoop, calls=%fused_computation.153 | loop fusion | bytes 655360 | tf_op jit(solution)/shard_map/slice | solution.py:65
  25.3 1.7 %fusion.40 = bf16[256,320]{0,1:T(8,128)(2,1)S(1)} fusion(bf16[3,1280,320]{1,2,0:T(8,128)(2,1)} %param.14, f32[320]{0:T(512)S(1)} %slice_reduce_fusion, bf16[256,1280]{1,0:T(8,128)(2,1)S(1)} %copy-done.1, f32[1280]{0:T(1024)S(1)} %copy-done.14, f32[1280]{0:T(1024)S(1)} %copy-done.15, f32[256]{0:T(256)S(1)} %add_rsqrt_fusion, f32[256]{0:T(256)S(1)} %broadcast_multiply_fusion), kind=kOutput, calls=%fused_computation.53 | convolution fusion | flops 211845120 | bytes 1651968 | tf_op jit(solution)/shard_map/dot_general | solution.py:40
  27.2 1.1 broadcast_compare_fusion.8
  28.3 0.7 fusion.94
  29.0 1.4 %reduce_window_sum.11 = s32[64,128]{1,0:T(8,128)} reduce-window(s32[64,128]{1,0:T(8,128)} %fusion.94, s32[]{:T(128)} %constant.77.clone.1), window={size=64x1 pad=63_0x0_0}, to_apply=%region_0.0 | reduce-window | flops 516096 | bytes 65540 | tf_op jit(solution)/shard_map/jit(cumsum)/reduce_window_sum | solution.py:141
  30.4 1.2 fusion.121
  31.7 2.4 %collective-permute-start.3 = (bf16[512,640]{0,1:T(8,128)(2,1)S(1)}, bf16[512,640]{0,1:T(8,128)(2,1)S(1)}, u32[]{:S(2)}, u32[]{:S(2)}) collective-permute-start(bf16[512,640]{0,1:T(8,128)(2,1)S(1)} %pad_maximum_fusion), channel_id=1, source_target_pairs={{0,4},{4,0},{8,12},{12,8},{16,20},{20,16},{24,28},{28,24},{32,36},... | collective-permute-start | bytes 1966088 | tf_op jit(solution)/shard_map/ppermute | solution.py:100
  34.1 0.3 collective-permute-done.5
  34.5 2.1 %collective-permute-start.6 = (bf16[256,640]{0,1:T(8,128)(2,1)S(1)}, bf16[256,640]{0,1:T(8,128)(2,1)S(1)}, u32[]{:S(2)}, u32[]{:S(2)}) collective-permute-start(bf16[256,640]{0,1:T(8,128)(2,1)S(1)} %broadcast_select_fusion), channel_id=1, source_target_pairs={{0,4},{4,0},{8,12},{12,8},{16,20},{20,16},{24,28},{28,24},{32,36},... | collective-permute-start | bytes 983048 | tf_op jit(solution)/shard_map/ppermute | solution.py:100
  36.6 0.4 fusion.114
  37.0 0.4 fusion.115
  37.4 0.4 copy-done.4
  37.8 0.4 fusion.118
  38.3 0.4 fusion.119
  38.6 1.0 fusion.105
  39.7 0.4 fusion.120
  40.1 0.4 fusion.113
  40.5 0.4 fusion.116
  40.9 0.4 fusion.117
  41.3 0.3 fusion.75
  41.6 0.3 fusion.45
  41.9 0.3 fusion.73
  42.2 0.3 fusion.71
  42.5 0.3 fusion.49
  42.8 0.3 fusion.69
  43.1 0.3 fusion.67
  43.4 0.3 fusion.53
  43.8 0.3 fusion.65
  44.2 0.3 fusion.63
  44.5 0.3 fusion.41
  44.9 0.3 fusion.23
  45.2 0.4 fusion.39
  46.2 1.3 %convolution_convert_fusion.1 = bf16[4,64,1280]{2,1,0:T(8,128)(2,1)} fusion(bf16[4,64,320]{2,1,0:T(8,128)(2,1)S(1)} %convert_element_type.92, bf16[320,1280]{1,0:T(8,128)(2,1)S(1)} %copy-done), kind=kOutput, calls=%fused_computation.1 | convolution fusion | flops 210042880 | bytes 1638400 | tf_op jit(solution)/shard_map/tgc,cd->tgd/dot_general | solution.py:126
  47.6 4.3 %all-to-all-start = ((bf16[4,64,1280]{2,1,0:T(8,128)(2,1)}), bf16[4,64,1280]{2,1,0:T(8,128)(2,1)S(1)}, u32[]{:S(2)}, u32[]{:S(2)}) async-start(bf16[4,64,1280]{2,1,0:T(8,128)(2,1)} %convolution_convert_fusion.1), calls=%async_computation | async-start | bytes 1310720 | tf_op jit(solution)/shard_map/all_to_all | solution.py:129
  52.2 0.3 dynamic-slice_convert_fusion
  52.6 10.9 %all-to-all-done = bf16[4,64,1280]{2,1,0:T(8,128)(2,1)S(1)} async-done(((bf16[4,64,1280]{2,1,0:T(8,128)(2,1)}), bf16[4,64,1280]{2,1,0:T(8,128)(2,1)S(1)}, u32[]{:S(2)}, u32[]{:S(2)}) %all-to-all-start) | async-done | bytes 655392 | tf_op jit(solution)/shard_map/all_to_all | solution.py:129
  63.9 0.4 convolution_convert_fusion
  64.3 0.2 all_to_all.12
  64.6 59.3 %all_to_all.17 = bf16[128,2,1280]{2,1,0:T(2,128)(2,1)S(1)} all-to-all(bf16[128,2,1280]{2,1,0:T(2,128)(2,1)S(1)} %all_to_all.12), channel_id=1, replica_groups=mesh['seq'=128,'tp'=4] {'seq'}, dimensions={0} | all-to-all | bytes 1310720 | tf_op jit(solution)/shard_map/all_to_all | solution.py:150
  123.9 1.1 all_to_all.14
  (68 shorter events, 2.5 us)
Async XLA Ops:
  0.0 46.2 %copy-start = (bf16[320,1280]{1,0:T(8,128)(2,1)S(1)}, bf16[320,1280]{1,0:T(8,128)(2,1)}, u32[]{:S(2)}) copy-start(bf16[320,1280]{1,0:T(8,128)(2,1)} %param.16) | copy-start | bytes 2457604
  0.0 2.8 %copy-start.1 = (bf16[256,1280]{1,0:T(8,128)(2,1)S(1)}, bf16[256,1280]{1,0:T(8,128)(2,1)}, u32[]{:S(2)}) copy-start(bf16[256,1280]{1,0:T(8,128)(2,1)} %param.11) | copy-start | bytes 1966084
  0.0 2.8 %copy-start.12 = (f32[3,320]{1,0:T(4,128)S(1)}, f32[3,320]{1,0:T(4,128)}, u32[]{:S(2)}) copy-start(f32[3,320]{1,0:T(4,128)} %param.15) | copy-start | bytes 11524
  0.0 2.8 %copy-start.15 = (f32[1280]{0:T(1024)S(1)}, f32[1280]{0:T(1024)}, u32[]{:S(2)}) copy-start(f32[1280]{0:T(1024)} %param.12) | copy-start | bytes 15364
  0.0 2.8 %copy-start.14 = (f32[1280]{0:T(1024)S(1)}, f32[1280]{0:T(1024)}, u32[]{:S(2)}) copy-start(f32[1280]{0:T(1024)} %param.13) | copy-start | bytes 15364
  2.9 22.0 %copy-start.8 = (s32[8192]{0:T(1024)S(1)}, s32[8192]{0:T(1024)}, u32[]{:S(2)}) copy-start(s32[8192]{0:T(1024)} %param.20) | copy-start | bytes 98308
  5.8 25.8 %collective-permute-start.1 = (bf16[256,640]{0,1:T(8,128)(2,1)}, bf16[256,640]{0,1:T(8,128)(2,1)S(1)}, u32[]{:S(2)}, u32[]{:S(2)}) collective-permute-start(bf16[256,640]{0,1:T(8,128)(2,1)} %bitcast.4), channel_id=1, source_target_pairs={{0,8},{4,12},{8,16},{12,20},{16,24},{20,28},{24,32},{28,36},{32,40... | collective-permute-start | bytes 983048 | tf_op jit(solution)/shard_map/ppermute | solution.py:17
  9.6 22.0 %collective-permute-start.2 = (bf16[256,640]{0,1:T(8,128)(2,1)}, bf16[256,640]{0,1:T(8,128)(2,1)S(1)}, u32[]{:S(2)}, u32[]{:S(2)}) collective-permute-start(bf16[256,640]{0,1:T(8,128)(2,1)} %bitcast.4), channel_id=1, source_target_pairs={{8,0},{12,4},{16,8},{20,12},{24,16},{28,20},{32,24},{36,28},{40,32... | collective-permute-start | bytes 983048 | tf_op jit(solution)/shard_map/ppermute | solution.py:17
  14.5 20.0 %collective-permute-start.5 = (bf16[256,640]{0,1:T(8,128)(2,1)}, bf16[256,640]{0,1:T(8,128)(2,1)S(1)}, u32[]{:S(2)}, u32[]{:S(2)}) collective-permute-start(bf16[256,640]{0,1:T(8,128)(2,1)} %bitcast.4), channel_id=1, source_target_pairs={{16,0},{20,4},{24,8},{28,12},{32,16},{36,20},{40,24},{44,28},{48,3... | collective-permute-start | bytes 983048 | tf_op jit(solution)/shard_map/ppermute | solution.py:17
  15.8 18.7 %collective-permute-start.4 = (bf16[256,640]{0,1:T(8,128)(2,1)}, bf16[256,640]{0,1:T(8,128)(2,1)S(1)}, u32[]{:S(2)}, u32[]{:S(2)}) collective-permute-start(bf16[256,640]{0,1:T(8,128)(2,1)} %bitcast.4), channel_id=1, source_target_pairs={{0,16},{4,20},{8,24},{12,28},{16,32},{20,36},{24,40},{28,44},{32,4... | collective-permute-start | bytes 983048 | tf_op jit(solution)/shard_map/ppermute | solution.py:17
  21.2 17.4 %collective-permute-start = (bf16[256,640]{0,1:T(8,128)(2,1)}, bf16[256,640]{0,1:T(8,128)(2,1)}, u32[]{:S(2)}, u32[]{:S(2)}) collective-permute-start(bf16[256,640]{0,1:T(8,128)(2,1)} %bitcast.4), channel_id=1, source_target_pairs={{0,4},{4,0},{8,12},{12,8},{16,20},{20,16},{24,28},{28,24},{32,36},... | collective-permute-start | bytes 983048 | tf_op jit(solution)/shard_map/ppermute | solution.py:100
  25.3 3.0 %copy-start.13 = (s32[64,1]{0,1:T(1,128)S(1)}, s32[64,1]{0,1:T(1,128)}, u32[]{:S(2)}) copy-start(s32[64,1]{0,1:T(1,128)} %param.21) | copy-start | bytes 772
  25.3 5.1 %copy-start.2 = (bf16[256,320]{0,1:T(8,128)(2,1)S(1)}, bf16[256,320]{0,1:T(8,128)(2,1)}, u32[]{:S(2)}) copy-start(bf16[256,320]{0,1:T(8,128)(2,1)} %get-tuple-element.31) | copy-start | bytes 491524
  31.6 5.0 %copy-start.6 = (pred[256,256]{0,1:T(8,128)(4,1)S(1)}, pred[256,256]{0,1:T(8,128)(4,1)}, u32[]{:S(2)}) copy-start(pred[256,256]{0,1:T(8,128)(4,1)} %get-tuple-element.59) | copy-start | bytes 196612
  31.7 8.8 %collective-permute-start.3 = (bf16[512,640]{0,1:T(8,128)(2,1)S(1)}, bf16[512,640]{0,1:T(8,128)(2,1)S(1)}, u32[]{:S(2)}, u32[]{:S(2)}) collective-permute-start(bf16[512,640]{0,1:T(8,128)(2,1)S(1)} %pad_maximum_fusion), channel_id=1, source_target_pairs={{0,4},{4,0},{8,12},{12,8},{16,20},{20,16},{24,28},{28,24},{32,36},... | collective-permute-start | bytes 1966088 | tf_op jit(solution)/shard_map/ppermute | solution.py:100
  34.5 2.5 %copy-start.5 = (pred[256,256]{0,1:T(8,128)(4,1)S(1)}, pred[256,256]{0,1:T(8,128)(4,1)}, u32[]{:S(2)}) copy-start(pred[256,256]{0,1:T(8,128)(4,1)} %get-tuple-element.58) | copy-start | bytes 196612
  34.5 5.5 %collective-permute-start.6 = (bf16[256,640]{0,1:T(8,128)(2,1)S(1)}, bf16[256,640]{0,1:T(8,128)(2,1)S(1)}, u32[]{:S(2)}, u32[]{:S(2)}) collective-permute-start(bf16[256,640]{0,1:T(8,128)(2,1)S(1)} %broadcast_select_fusion), channel_id=1, source_target_pairs={{0,4},{4,0},{8,12},{12,8},{16,20},{20,16},{24,28},{28,24},{32,36},... | collective-permute-start | bytes 983048 | tf_op jit(solution)/shard_map/ppermute | solution.py:100
  37.0 0.8 copy-start.4
  37.4 0.8 copy-start.3
  46.2 5.7 %copy-start.7 = (s32[64,128]{1,0:T(8,128)S(1)}, s32[64,128]{1,0:T(8,128)}, u32[]{:S(2)}) copy-start(s32[64,128]{1,0:T(8,128)} %reduce_window_sum.11) | copy-start | bytes 98308
  47.6 15.9 %all-to-all-start = ((bf16[4,64,1280]{2,1,0:T(8,128)(2,1)}), bf16[4,64,1280]{2,1,0:T(8,128)(2,1)S(1)}, u32[]{:S(2)}, u32[]{:S(2)}) async-start(bf16[4,64,1280]{2,1,0:T(8,128)(2,1)} %convolution_convert_fusion.1), calls=%async_computation | async-start | bytes 1310720 | tf_op jit(solution)/shard_map/all_to_all | solution.py:129
  52.1 11.5 %copy-start.9 = (f32[1280]{0:T(1024)S(1)}, f32[1280]{0:T(1024)}, u32[]{:S(2)}) copy-start(f32[1280]{0:T(1024)} %param.17) | copy-start | bytes 15364
  52.5 11.4 %copy-start.10 = (f32[1280]{0:T(1024)S(1)}, f32[1280]{0:T(1024)}, u32[]{:S(2)}) copy-start(f32[1280]{0:T(1024)} %param.19) | copy-start | bytes 15364
  52.6 11.4 %copy-start.11 = (f32[1280]{0:T(1024)S(1)}, f32[1280]{0:T(1024)}, u32[]{:S(2)}) copy-start(f32[1280]{0:T(1024)} %param.18) | copy-start | bytes 15364

commit v6 on v5

--- a/solution.py
+++ b/solution.py
@@ -70,24 +70,25 @@
         allowed = query_segment[:, None] == key_segment[None, :]
         return (jnp.where(allowed[None], scores, masked_score), value_heads)
 
-    def absorb(state, block, key_segment):
+    def absorb(state, blocks):
         row_top, totals, summed = state
-        scores, value_heads = block_scores(block, key_segment)
-        new_top = jnp.maximum(row_top, jnp.max(scores, axis=-1, keepdims=True))
+        parts = [block_scores(block, key_segment) for block, key_segment in blocks]
+        new_top = row_top
+        for scores, _ in parts:
+            new_top = jnp.maximum(new_top, jnp.max(scores, axis=-1, keepdims=True))
         factor = jnp.exp(row_top - new_top)
-        weights = jnp.exp(scores - new_top)
-        totals = totals * factor + jnp.sum(weights, axis=-1, keepdims=True)
-        summed = summed * factor + jnp.einsum(
-            "hqk,khd->hqd",
-            weights.astype(jnp.bfloat16),
-            value_heads,
-            preferred_element_type=jnp.float32,
-        )
+        totals = totals * factor
+        summed = summed * factor
+        for scores, value_heads in parts:
+            weights = jnp.exp(scores - new_top)
+            totals = totals + jnp.sum(weights, axis=-1, keepdims=True)
+            summed = summed + jnp.einsum(
+                "hqk,khd->hqd",
+                weights.astype(jnp.bfloat16),
+                value_heads,
+                preferred_element_type=jnp.float32,
+            )
         return (new_top, totals, summed)
-
-    def absorb_remote(state, block, key_start):
-        key_segment = segment_window(key_start, tok_dev)
-        return absorb(state, block, key_segment)
 
     start_state = (
         jnp.full((local_heads, tok_dev, 1), masked_score, jnp.float32),
@@ -99,25 +100,27 @@
     def swap(value):
         return lax.ppermute(value, "seq", [(i, i ^ 1) for i in range(seq_count)])
 
-    def absorb_at(state, block, offset):
-        return absorb_remote(state, block, row_start + offset * tok_dev)
+    def at(block, offset):
+        return (block, segment_window(row_start + offset * tok_dev, tok_dev))
 
+    below_4 = from_behind(key_value, "seq", 4)
+    above_4 = from_behind(key_value, "seq", -4)
     below_2 = from_behind(key_value, "seq", 2)
     above_2 = from_behind(key_value, "seq", -2)
-    below_4 = from_behind(key_value, "seq", 4)
-    above_4 = from_behind(key_value, "seq", -4)
     partner_own = swap(key_value)
-    state = absorb(start_state, key_value, query_segment)
     partner_near = swap(jnp.concatenate([below_2, above_2], axis=0))
     partner_far = swap(jnp.where(sign > 0, above_4, below_4))
-    state = absorb_at(state, partner_own, sign)
-    state = absorb_at(state, below_2, -2)
-    state = absorb_at(state, above_2, 2)
-    state = absorb_at(state, partner_near[:tok_dev], sign - 2)
-    state = absorb_at(state, partner_near[tok_dev:], sign + 2)
-    state = absorb_at(state, below_4, -4)
-    state = absorb_at(state, above_4, 4)
-    state = absorb_at(state, partner_far, -3 * sign)
+    state = absorb(start_state, [(key_value, query_segment), at(partner_own, sign)])
+    state = absorb(
+        state,
+        [
+            at(below_2, -2),
+            at(above_2, 2),
+            at(partner_near[:tok_dev], sign - 2),
+            at(partner_near[tok_dev:], sign + 2),
+        ],
+    )
+    state = absorb(state, [at(below_4, -4), at(above_4, 4), at(partner_far, -3 * sign)])
     row_top, totals, summed = state
     tp_index = lax.axis_index("tp")
     quarter = tok_dev // 4

time: 126 us -> 136 us (1.079)
  waiting for transfers between devices: 11.2 us -> 23.2 us
  blocking collectives: 59.3 us -> 55.6 us
  local copies, waits for them, and re-layouts: 5.82 us -> 8.82 us
  starting transfers between devices: 26.1 us -> 24.1 us
    ppermute x4, waiting for transfers between devices: 0.33 us -> 12.8 us  [from_behind(): lax.ppermute(value, axis, [(source, source + steps) for source in range(l...]
    all_to_all x1, blocking collectives: 59.3 us -> 55.6 us  [per_device(): lax.all_to_all(outgoing, 'seq', split_axis=0, concat_axis=0, tiled=True)]
    slice x7, local copies, waits for them, and re-layouts: 2.83 us -> 4.87 us  [block_scores(): value_heads = block[:, local_width:].reshape(-1, local_heads, HEAD_DIM)]
    ppermute x4, starting transfers between devices: 15.4 us -> 13.4 us  [from_behind(): lax.ppermute(value, axis, [(source, source + steps) for source in range(l...]
  transfers between devices with their start and end apart: 8 -> 8, of which waited for: 2 -> 2; matrix products, arithmetic and copies ran while one was open for 10% -> 12% of each run, Pallas kernels for 0% -> 0%
where the time goes in v6:
time: 136 us; the launch traced here: 135 us
  blocking collectives  55.6 us (41%)
  starting transfers between devices  24.1 us (18%)
  waiting for transfers between devices  23.2 us (17%)
  matrix products  13.4 us (10%)
  other arithmetic  9.25 us (7%)
  local copies, waits for them, and re-layouts  8.82 us (6%)
    all_to_all x1, blocking collectives, per_device(): lax.all_to_all(outgoing, 'seq', split_axis=0, concat_axis=0, tiled=True)  55.6 us
    ppermute x4, starting transfers between devices, from_behind(): lax.ppermute(value, axis, [(source, source + steps) for source in range(l...  13.4 us
    ppermute x4, waiting for transfers between devices, from_behind(): lax.ppermute(value, axis, [(source, source + steps) for source in range(l...  12.8 us
    all_to_all x1, waiting for transfers between devices, per_device(): lax.all_to_all(head_term, 'tp', split_axis=0, concat_axis=0, tiled=True)  10.4 us
    ppermute x3, starting transfers between devices, swap(): return lax.ppermute(value, 'seq', [(i, i ^ 1) for i in range(seq_count)])  6.38 us
    slice x7, local copies, waits for them, and re-layouts, block_scores(): value_heads = block[:, local_width:].reshape(-1, local_heads, HEAD_DIM)  4.87 us
    dot_general x9, matrix products, block_scores(): jnp.einsum('qhd,khd->hqk', query_heads, key_heads, preferred_element_type...  4.3 us
    all_to_all x1, starting transfers between devices, per_device(): lax.all_to_all(head_term, 'tp', split_axis=0, concat_axis=0, tiled=True)  4.28 us
  transfers between devices with their start and end apart: 8, of which 2 were waited for; matrix products, arithmetic and copies ran while one was open for 12% of the time, Pallas kernels for 0%

profile of v6, /device:TPU:32, one launch (start us, length us, event | category | flops | bytes accessed | tf_op | source)
XLA Modules:
  0.0 135.0 jit_solution(8503131715022139566)
XLA Ops:
  0.0 1.4 %convert_reduce_fusion = f32[256]{0:T(256)S(1)} fusion(bf16[256,1280]{1,0:T(8,128)(2,1)} %param.11), kind=kLoop, calls=%fused_computation.5 | loop fusion | flops 655104 | bytes 656384 | tf_op jit(solution)/shard_map/reduce_sum | solution.py:21
  1.4 1.4 %fusion.13 = f32[256]{0:T(256)S(1)} fusion(bf16[256,1280]{1,0:T(8,128)(2,1)} %param.11, f32[256]{0:T(256)S(1)} %broadcast_multiply_fusion), kind=kLoop, calls=%fused_computation.26 | loop fusion | flops 1310464 | bytes 657408 | tf_op jit(solution)/shard_map/reduce_sum | solution.py:23
  2.9 2.9 %fusion.20 = bf16[256,2,320]{0,2,1:T(8,128)(2,1)} fusion(bf16[3,1280,320]{1,2,0:T(8,128)(2,1)} %param.14, f32[2,320]{1,0:T(2,128)S(1)} %slice.79, bf16[256,1280]{1,0:T(8,128)(2,1)S(1)} %copy-done.1, f32[1280]{0:T(1024)S(1)} %copy-done.16, f32[1280]{0:T(1024)S(1)} %copy-done.17, f32[256]{0:T(256)S(1)} %add_rsqrt_fusion, f32[256]{0:T(256)S(1)} %broadcast_multiply_fusion), kind=kOutput, calls=%fused_computation.32 | convolution fusion | flops 421724160 | bytes 2636288 | tf_op jit(solution)/shard_map/tc,kcd->tkd/dot_general | solution.py:44
  5.8 5.2 %collective-permute-start.4 = (bf16[256,640]{0,1:T(8,128)(2,1)}, bf16[256,640]{0,1:T(8,128)(2,1)S(1)}, u32[]{:S(2)}, u32[]{:S(2)}) collective-permute-start(bf16[256,640]{0,1:T(8,128)(2,1)} %bitcast.4), channel_id=1, source_target_pairs={{0,16},{4,20},{8,24},{12,28},{16,32},{20,36},{24,40},{28,44},{32,4... | collective-permute-start | bytes 983048 | tf_op jit(solution)/shard_map/ppermute | solution.py:17
  11.0 3.5 %collective-permute-start.2 = (bf16[256,640]{0,1:T(8,128)(2,1)}, bf16[256,640]{0,1:T(8,128)(2,1)}, u32[]{:S(2)}, u32[]{:S(2)}) collective-permute-start(bf16[256,640]{0,1:T(8,128)(2,1)} %bitcast.4), channel_id=1, source_target_pairs={{8,0},{12,4},{16,8},{20,12},{24,16},{28,20},{32,24},{36,28},{40,32... | collective-permute-start | bytes 983048 | tf_op jit(solution)/shard_map/ppermute | solution.py:17
  14.5 3.5 %collective-permute-start.1 = (bf16[256,640]{0,1:T(8,128)(2,1)}, bf16[256,640]{0,1:T(8,128)(2,1)}, u32[]{:S(2)}, u32[]{:S(2)}) collective-permute-start(bf16[256,640]{0,1:T(8,128)(2,1)} %bitcast.4), channel_id=1, source_target_pairs={{0,8},{4,12},{8,16},{12,20},{16,24},{20,28},{24,32},{28,36},{32,40... | collective-permute-start | bytes 983048 | tf_op jit(solution)/shard_map/ppermute | solution.py:17
  17.9 1.9 %collective-permute-start = (bf16[256,640]{0,1:T(8,128)(2,1)}, bf16[256,640]{0,1:T(8,128)(2,1)}, u32[]{:S(2)}, u32[]{:S(2)}) collective-permute-start(bf16[256,640]{0,1:T(8,128)(2,1)} %bitcast.4), channel_id=1, source_target_pairs={{0,4},{4,0},{8,12},{12,8},{16,20},{20,16},{24,28},{28,24},{32,36},... | collective-permute-start | bytes 983048 | tf_op jit(solution)/shard_map/ppermute | solution.py:101
  19.9 1.3 collective-permute-start.5
  21.2 1.7 %fusion.97 = (bf16[256,320]{0,1:T(8,128)(2,1)S(1)}, bf16[256,320]{0,1:T(8,128)(2,1)}) fusion(bf16[256,640]{0,1:T(8,128)(2,1)} %bitcast.4), kind=kLoop, calls=%fused_computation.141 | loop fusion | bytes 655360 | tf_op jit(solution)/shard_map/slice | solution.py:65
  22.9 1.7 %fusion.34 = bf16[256,320]{0,1:T(8,128)(2,1)S(1)} fusion(bf16[3,1280,320]{1,2,0:T(8,128)(2,1)} %param.14, f32[320]{0:T(512)S(1)} %slice_reduce_fusion, bf16[256,1280]{1,0:T(8,128)(2,1)S(1)} %copy-done.1, f32[1280]{0:T(1024)S(1)} %copy-done.16, f32[1280]{0:T(1024)S(1)} %copy-done.17, f32[256]{0:T(256)S(1)} %add_rsqrt_fusion, f32[256]{0:T(256)S(1)} %broadcast_multiply_fusion), kind=kOutput, calls=%fused_computation.47 | convolution fusion | flops 211845120 | bytes 1651968 | tf_op jit(solution)/shard_map/dot_general | solution.py:40
  25.2 1.2 broadcast_compare_fusion.6
  26.3 1.3 fusion.111
  27.6 0.7 fusion.88
  28.3 0.9 reduce_window_sum.11
  29.2 12.8 %collective-permute-done.5 = bf16[256,640]{0,1:T(8,128)(2,1)S(1)} collective-permute-done((bf16[256,640]{0,1:T(8,128)(2,1)}, bf16[256,640]{0,1:T(8,128)(2,1)S(1)}, u32[]{:S(2)}, u32[]{:S(2)}) %collective-permute-start.5) | collective-permute-done | bytes 327712 | tf_op jit(solution)/shard_map/ppermute | solution.py:17
  42.0 1.9 %collective-permute-start.6 = (bf16[256,640]{0,1:T(8,128)(2,1)S(1)}, bf16[256,640]{0,1:T(8,128)(2,1)S(1)}, u32[]{:S(2)}, u32[]{:S(2)}) collective-permute-start(bf16[256,640]{0,1:T(8,128)(2,1)S(1)} %broadcast_select_fusion), channel_id=1, source_target_pairs={{0,4},{4,0},{8,12},{12,8},{16,20},{20,16},{24,28},{28,24},{32,36},... | collective-permute-start | bytes 983048 | tf_op jit(solution)/shard_map/ppermute | solution.py:101
  44.0 1.1 pad_maximum_fusion
  45.1 2.5 %collective-permute-start.3 = (bf16[512,640]{0,1:T(8,128)(2,1)S(1)}, bf16[512,640]{0,1:T(8,128)(2,1)S(1)}, u32[]{:S(2)}, u32[]{:S(2)}) collective-permute-start(bf16[512,640]{0,1:T(8,128)(2,1)S(1)} %pad_maximum_fusion), channel_id=1, source_target_pairs={{0,4},{4,0},{8,12},{12,8},{16,20},{20,16},{24,28},{28,24},{32,36},... | collective-permute-start | bytes 1966088 | tf_op jit(solution)/shard_map/ppermute | solution.py:101
  47.7 1.0 fusion.98
  48.7 0.4 fusion.112
  49.1 1.0 fusion.99
  50.2 0.4 fusion.109
  50.6 0.4 fusion.106
  51.0 1.0 fusion.96
  52.0 0.4 fusion.110
  52.7 0.5 copy-done.5
  53.2 0.4 fusion.105
  53.6 0.3 fusion.35
  54.0 0.5 copy-done.4
  54.5 0.4 fusion.104
  54.9 0.4 copy-done.3
  55.3 0.4 fusion.107
  55.7 0.4 fusion.108
  56.1 0.3 fusion.61
  56.4 0.3 fusion.59
  56.7 0.3 fusion.57
  57.0 0.3 fusion.65
  57.3 0.3 fusion.63
  57.6 1.2 fusion.39
  59.1 0.3 fusion.69
  59.5 0.4 fusion.33
  60.5 1.3 convolution_convert_fusion.1
  61.8 4.3 %all-to-all-start = ((bf16[4,64,1280]{2,1,0:T(8,128)(2,1)}), bf16[4,64,1280]{2,1,0:T(8,128)(2,1)S(1)}, u32[]{:S(2)}, u32[]{:S(2)}) async-start(bf16[4,64,1280]{2,1,0:T(8,128)(2,1)} %convolution_convert_fusion.1), calls=%async_computation | async-start | bytes 1310720 | tf_op jit(solution)/shard_map/all_to_all | solution.py:132
  66.4 0.3 dynamic-slice_convert_fusion
  66.8 10.4 %all-to-all-done = bf16[4,64,1280]{2,1,0:T(8,128)(2,1)S(1)} async-done(((bf16[4,64,1280]{2,1,0:T(8,128)(2,1)}), bf16[4,64,1280]{2,1,0:T(8,128)(2,1)S(1)}, u32[]{:S(2)}, u32[]{:S(2)}) %all-to-all-start) | async-done | bytes 655392 | tf_op jit(solution)/shard_map/all_to_all | solution.py:132
  77.6 0.4 convolution_convert_fusion
  78.3 55.6 %all_to_all.17 = bf16[128,2,1280]{2,1,0:T(2,128)(2,1)S(1)} all-to-all(bf16[128,2,1280]{2,1,0:T(2,128)(2,1)S(1)} %all_to_all.12), channel_id=1, replica_groups=mesh['seq'=128,'tp'=4] {'seq'}, dimensions={0} | all-to-all | bytes 1310720 | tf_op jit(solution)/shard_map/all_to_all | solution.py:153
  133.9 1.1 all_to_all.14
  (70 shorter events, 3.0 us)
Async XLA Ops:
  0.0 60.5 %copy-start = (bf16[320,1280]{1,0:T(8,128)(2,1)S(1)}, bf16[320,1280]{1,0:T(8,128)(2,1)}, u32[]{:S(2)}) copy-start(bf16[320,1280]{1,0:T(8,128)(2,1)} %param.16) | copy-start | bytes 2457604
  0.0 2.8 %copy-start.1 = (bf16[256,1280]{1,0:T(8,128)(2,1)S(1)}, bf16[256,1280]{1,0:T(8,128)(2,1)}, u32[]{:S(2)}) copy-start(bf16[256,1280]{1,0:T(8,128)(2,1)} %param.11) | copy-start | bytes 1966084
  0.0 2.8 %copy-start.14 = (f32[3,320]{1,0:T(4,128)S(1)}, f32[3,320]{1,0:T(4,128)}, u32[]{:S(2)}) copy-start(f32[3,320]{1,0:T(4,128)} %param.15) | copy-start | bytes 11524
  0.0 2.8 %copy-start.16 = (f32[1280]{0:T(1024)S(1)}, f32[1280]{0:T(1024)}, u32[]{:S(2)}) copy-start(f32[1280]{0:T(1024)} %param.13) | copy-start | bytes 15364
  0.0 2.8 %copy-start.17 = (f32[1280]{0:T(1024)S(1)}, f32[1280]{0:T(1024)}, u32[]{:S(2)}) copy-start(f32[1280]{0:T(1024)} %param.12) | copy-start | bytes 15364
  5.8 23.4 %collective-permute-start.4 = (bf16[256,640]{0,1:T(8,128)(2,1)}, bf16[256,640]{0,1:T(8,128)(2,1)S(1)}, u32[]{:S(2)}, u32[]{:S(2)}) collective-permute-start(bf16[256,640]{0,1:T(8,128)(2,1)} %bitcast.4), channel_id=1, source_target_pairs={{0,16},{4,20},{8,24},{12,28},{16,32},{20,36},{24,40},{28,44},{32,4... | collective-permute-start | bytes 983048 | tf_op jit(solution)/shard_map/ppermute | solution.py:17
  11.0 33.0 %collective-permute-start.2 = (bf16[256,640]{0,1:T(8,128)(2,1)}, bf16[256,640]{0,1:T(8,128)(2,1)}, u32[]{:S(2)}, u32[]{:S(2)}) collective-permute-start(bf16[256,640]{0,1:T(8,128)(2,1)} %bitcast.4), channel_id=1, source_target_pairs={{8,0},{12,4},{16,8},{20,12},{24,16},{28,20},{32,24},{36,28},{40,32... | collective-permute-start | bytes 983048 | tf_op jit(solution)/shard_map/ppermute | solution.py:17
  14.5 29.5 %collective-permute-start.1 = (bf16[256,640]{0,1:T(8,128)(2,1)}, bf16[256,640]{0,1:T(8,128)(2,1)}, u32[]{:S(2)}, u32[]{:S(2)}) collective-permute-start(bf16[256,640]{0,1:T(8,128)(2,1)} %bitcast.4), channel_id=1, source_target_pairs={{0,8},{4,12},{8,16},{12,20},{16,24},{20,28},{24,32},{28,36},{32,40... | collective-permute-start | bytes 983048 | tf_op jit(solution)/shard_map/ppermute | solution.py:17
  17.9 33.0 %collective-permute-start = (bf16[256,640]{0,1:T(8,128)(2,1)}, bf16[256,640]{0,1:T(8,128)(2,1)}, u32[]{:S(2)}, u32[]{:S(2)}) collective-permute-start(bf16[256,640]{0,1:T(8,128)(2,1)} %bitcast.4), channel_id=1, source_target_pairs={{0,4},{4,0},{8,12},{12,8},{16,20},{20,16},{24,28},{28,24},{32,36},... | collective-permute-start | bytes 983048 | tf_op jit(solution)/shard_map/ppermute | solution.py:101
  19.9 22.1 %collective-permute-start.5 = (bf16[256,640]{0,1:T(8,128)(2,1)}, bf16[256,640]{0,1:T(8,128)(2,1)S(1)}, u32[]{:S(2)}, u32[]{:S(2)}) collective-permute-start(bf16[256,640]{0,1:T(8,128)(2,1)} %bitcast.4), channel_id=1, source_target_pairs={{16,0},{20,4},{24,8},{28,12},{32,16},{36,20},{40,24},{44,28},{48,3... | collective-permute-start | bytes 983048 | tf_op jit(solution)/shard_map/ppermute | solution.py:17
  22.9 1.7 %copy-start.10 = (s32[8192]{0:T(1024)S(1)}, s32[8192]{0:T(1024)}, u32[]{:S(2)}) copy-start(s32[8192]{0:T(1024)} %param.20) | copy-start | bytes 98308
  24.7 2.9 %copy-start.15 = (s32[64,1]{0,1:T(1,128)S(1)}, s32[64,1]{0,1:T(1,128)}, u32[]{:S(2)}) copy-start(s32[64,1]{0,1:T(1,128)} %param.21) | copy-start | bytes 772
  29.2 19.5 %copy-start.9 = (pred[256,256]{0,1:T(8,128)(4,1)S(1)}, pred[256,256]{0,1:T(8,128)(4,1)}, u32[]{:S(2)}) copy-start(pred[256,256]{0,1:T(8,128)(4,1)} %get-tuple-element.50) | copy-start | bytes 196612
  42.0 11.9 %collective-permute-start.6 = (bf16[256,640]{0,1:T(8,128)(2,1)S(1)}, bf16[256,640]{0,1:T(8,128)(2,1)S(1)}, u32[]{:S(2)}, u32[]{:S(2)}) collective-permute-start(bf16[256,640]{0,1:T(8,128)(2,1)S(1)} %broadcast_select_fusion), channel_id=1, source_target_pairs={{0,4},{4,0},{8,12},{12,8},{16,20},{20,16},{24,28},{28,24},{32,36},... | collective-permute-start | bytes 983048 | tf_op jit(solution)/shard_map/ppermute | solution.py:101
  45.1 5.0 %copy-start.8 = (pred[256,256]{0,1:T(8,128)(4,1)S(1)}, pred[256,256]{0,1:T(8,128)(4,1)}, u32[]{:S(2)}) copy-start(pred[256,256]{0,1:T(8,128)(4,1)} %get-tuple-element.51) | copy-start | bytes 196612
  45.1 9.7 %collective-permute-start.3 = (bf16[512,640]{0,1:T(8,128)(2,1)S(1)}, bf16[512,640]{0,1:T(8,128)(2,1)S(1)}, u32[]{:S(2)}, u32[]{:S(2)}) collective-permute-start(bf16[512,640]{0,1:T(8,128)(2,1)S(1)} %pad_maximum_fusion), channel_id=1, source_target_pairs={{0,4},{4,0},{8,12},{12,8},{16,20},{20,16},{24,28},{28,24},{32,36},... | collective-permute-start | bytes 1966088 | tf_op jit(solution)/shard_map/ppermute | solution.py:101
  49.1 1.5 %copy-start.7 = (pred[256,256]{0,1:T(8,128)(4,1)S(1)}, pred[256,256]{0,1:T(8,128)(4,1)}, u32[]{:S(2)}) copy-start(pred[256,256]{0,1:T(8,128)(4,1)} %get-tuple-element.54) | copy-start | bytes 196612
  50.5 1.5 %copy-start.6 = (pred[256,256]{0,1:T(8,128)(4,1)S(1)}, pred[256,256]{0,1:T(8,128)(4,1)}, u32[]{:S(2)}) copy-start(pred[256,256]{0,1:T(8,128)(4,1)} %get-tuple-element.57) | copy-start | bytes 196612
  52.4 0.8 copy-start.5
  53.6 0.8 copy-start.4
  54.5 0.8 copy-start.3
  54.8 0.8 copy-start.2
  61.8 15.3 %all-to-all-start = ((bf16[4,64,1280]{2,1,0:T(8,128)(2,1)}), bf16[4,64,1280]{2,1,0:T(8,128)(2,1)S(1)}, u32[]{:S(2)}, u32[]{:S(2)}) async-start(bf16[4,64,1280]{2,1,0:T(8,128)(2,1)} %convolution_convert_fusion.1), calls=%async_computation | async-start | bytes 1310720 | tf_op jit(solution)/shard_map/all_to_all | solution.py:132
  66.3 11.0 %copy-start.11 = (f32[1280]{0:T(1024)S(1)}, f32[1280]{0:T(1024)}, u32[]{:S(2)}) copy-start(f32[1280]{0:T(1024)} %param.17) | copy-start | bytes 15364
  66.8 10.9 %copy-start.12 = (f32[1280]{0:T(1024)S(1)}, f32[1280]{0:T(1024)}, u32[]{:S(2)}) copy-start(f32[1280]{0:T(1024)} %param.19) | copy-start | bytes 15364
  66.8 10.9 %copy-start.13 = (f32[1280]{0:T(1024)S(1)}, f32[1280]{0:T(1024)}, u32[]{:S(2)}) copy-start(f32[1280]{0:T(1024)} %param.18) | copy-start | bytes 15364

commit v7 on v1

--- a/solution.py
+++ b/solution.py
@@ -37,41 +37,57 @@
     reach_rows = SPAN * tok_dev
     scale_factor = HEAD_DIM ** (-0.5)
     normed = layer_norm(tokens.astype(jnp.float32), ln_gain, ln_bias).astype(jnp.bfloat16)
-    query = (jnp.dot(normed, w_qkv[0], preferred_element_type=jnp.float32) + b_qkv[0]).astype(
-        jnp.bfloat16
-    )
-    key_rows = (jnp.dot(normed, w_qkv[1], preferred_element_type=jnp.float32) + b_qkv[1]).astype(
-        jnp.bfloat16
-    )
-    value_rows = (jnp.dot(normed, w_qkv[2], preferred_element_type=jnp.float32) + b_qkv[2]).astype(
-        jnp.bfloat16
-    )
-    key_value = jnp.concatenate([key_rows, value_rows], axis=1)
+    core = seq_index % 2
+    pair_heads = local_heads // 2
+    pair_width = pair_heads * HEAD_DIM
+    chip_rows = 2 * tok_dev
+    chip_start = (seq_index - core) * tok_dev
+    reach_chips = SPAN // 2
+
+    def swap(value):
+        return lax.ppermute(value, "seq", [(i, i ^ 1) for i in range(seq_count)])
+
+    def by_core(first, second):
+        return jnp.where(core == 0, first, second)
+
+    qkv = (
+        jnp.einsum("tc,kcd->tkd", normed, w_qkv, preferred_element_type=jnp.float32) + b_qkv
+    ).astype(jnp.bfloat16).reshape(tok_dev, 3, 2, pair_width)
+    mine = lax.dynamic_index_in_dim(qkv, core, 2, keepdims=False)
+    other = lax.dynamic_index_in_dim(qkv, 1 - core, 2, keepdims=False)
+    received = swap(other)
+    chip_qkv = jnp.concatenate([by_core(mine, received), by_core(received, mine)], axis=0)
+    query_heads = chip_qkv[:, 0].reshape(chip_rows, pair_heads, HEAD_DIM)
+    chip_kv = chip_qkv[:, 1:]
+
     group_rows = tok_dev // 4
     reach_groups = SPAN * group_rows
     padding = jnp.full((reach_groups,), -1, jnp.int32)
     padded_segment = jnp.concatenate([padding, segments, padding])
+    window_segment = lax.optimization_barrier(
+        jnp.repeat(
+            lax.dynamic_slice_in_dim(
+                padded_segment, chip_start // 4, (2 * reach_chips + 1) * chip_rows // 4
+            ),
+            4,
+        )
+    )
 
-    def segment_window(key_start, length):
-        groups = lax.dynamic_slice_in_dim(padded_segment, key_start // 4 + reach_groups, length // 4)
-        return jnp.repeat(groups, 4)
+    def segment_window(offset):
+        return lax.dynamic_slice_in_dim(window_segment, (offset + reach_chips) * chip_rows, chip_rows)
 
-    query_segment = segment_window(row_start, tok_dev)
-    query_heads = query.reshape(tok_dev, local_heads, HEAD_DIM)
+    query_segment = segment_window(0)
 
-    def block_scores(block, key_segment):
-        key_heads = block[:, :local_width].reshape(-1, local_heads, HEAD_DIM)
-        value_heads = block[:, local_width:].reshape(-1, local_heads, HEAD_DIM)
+    def absorb(state, block, offset):
+        row_top, totals, summed = state
+        key_heads = block[:, 0].reshape(-1, pair_heads, HEAD_DIM)
+        value_heads = block[:, 1].reshape(-1, pair_heads, HEAD_DIM)
         scores = (
             jnp.einsum("qhd,khd->hqk", query_heads, key_heads, preferred_element_type=jnp.float32)
             * scale_factor
         )
-        allowed = query_segment[:, None] == key_segment[None, :]
-        return (jnp.where(allowed[None], scores, masked_score), value_heads)
-
-    def absorb(state, block, key_segment):
-        row_top, totals, summed = state
-        scores, value_heads = block_scores(block, key_segment)
+        allowed = query_segment[:, None] == segment_window(offset)[None, :]
+        scores = jnp.where(allowed[None], scores, masked_score)
         new_top = jnp.maximum(row_top, jnp.max(scores, axis=-1, keepdims=True))
         factor = jnp.exp(row_top - new_top)
         weights = jnp.exp(scores - new_top)
@@ -84,28 +100,28 @@
         )
         return (new_top, totals, summed)
 
-    def absorb_remote(state, block, key_start):
-        key_segment = segment_window(key_start, tok_dev)
-        return absorb(state, block, key_segment)
-
     start_state = (
-        jnp.full((local_heads, tok_dev, 1), masked_score, jnp.float32),
-        jnp.zeros((local_heads, tok_dev, 1), jnp.float32),
-        jnp.zeros((local_heads, tok_dev, HEAD_DIM), jnp.float32),
+        jnp.full((pair_heads, chip_rows, 1), masked_score, jnp.float32),
+        jnp.zeros((pair_heads, chip_rows, 1), jnp.float32),
+        jnp.zeros((pair_heads, chip_rows, HEAD_DIM), jnp.float32),
     )
-    state = absorb(start_state, key_value, query_segment)
-    below = key_value
-    above = key_value
-    for distance in range(1, SPAN + 1):
-        below = from_behind(below, "seq", 1)
-        above = from_behind(above, "seq", -1)
-        state = absorb_remote(state, below, row_start - distance * tok_dev)
-        state = absorb_remote(state, above, row_start + distance * tok_dev)
+    below_1 = from_behind(chip_kv, "seq", 2)
+    above_1 = from_behind(chip_kv, "seq", -2)
+    below_2 = from_behind(chip_kv, "seq", 4)
+    above_2 = from_behind(chip_kv, "seq", -4)
+    state = absorb(start_state, chip_kv, 0)
+    state = absorb(state, below_1, -1)
+    state = absorb(state, above_1, 1)
+    state = absorb(state, below_2, -2)
+    state = absorb(state, above_2, 2)
     row_top, totals, summed = state
+    pair_out = jnp.transpose(summed / totals, (1, 0, 2)).reshape(chip_rows, pair_width).astype(jnp.bfloat16)
+    own_part = by_core(pair_out[:tok_dev], pair_out[tok_dev:])
+    other_part = swap(by_core(pair_out[tok_dev:], pair_out[:tok_dev]))
+    attended_rows = jnp.concatenate([by_core(own_part, other_part), by_core(other_part, own_part)], axis=1)
     tp_index = lax.axis_index("tp")
     quarter = tok_dev // 4
-    by_token = (summed / totals).reshape(local_heads, quarter, 4, HEAD_DIM)
-    attended = jnp.transpose(by_token, (2, 1, 0, 3)).reshape(4, quarter, local_width).astype(jnp.bfloat16)
+    attended = jnp.transpose(attended_rows.reshape(quarter, 4, local_width), (1, 0, 2))
     head_term = jnp.einsum(
         "tgc,cd->tgd", attended, w_out, preferred_element_type=jnp.float32
     ).astype(jnp.bfloat16)

time: 137 us -> 133 us (0.971)
  starting transfers between devices: 27.5 us -> 22 us
  waiting for transfers between devices: 21.5 us -> 25.5 us
  other arithmetic: 7.84 us -> 10.8 us
  local copies, waits for them, and re-layouts: 6.99 us -> 4.6 us
  blocking collectives: 59 us -> 57.2 us
    ppermute x8 -> x4, starting transfers between devices: 23.9 us -> 13.5 us  [from_behind(): lax.ppermute(value, axis, [(source, source + steps) for source in range(l...]
    ppermute x8 -> x4, waiting for transfers between devices: 11.3 us -> 15.4 us  [from_behind(): lax.ppermute(value, axis, [(source, source + steps) for source in range(l...]
    ppermute x0 -> x2, starting transfers between devices: none -> 4.01 us  [swap(): return lax.ppermute(value, 'seq', [(i, i ^ 1) for i in range(seq_count)])]
    eq x9 -> x0, local copies, waits for them, and re-layouts: 3.88 us -> none  [block_scores(): allowed = query_segment[:, None] == key_segment[None, :]]
    dot_general x12 -> x6, matrix products: 8.44 us -> 5.27 us  [the longest x5 3.21 us: absorb(): jnp.einsum('qhd,khd->hqk', query_heads, key_heads, preferred_element_type...]
    all_to_all x1, blocking collectives: 59 us -> 57.2 us  [per_device(): lax.all_to_all(outgoing, 'seq', split_axis=0, concat_axis=0, tiled=True)]
    all_to_all x1, waiting for transfers between devices: 10.2 us -> 8.8 us  [per_device(): lax.all_to_all(head_term, 'tp', split_axis=0, concat_axis=0, tiled=True)]
    dot_general x9 -> x5, matrix products: 2.74 us -> 3.59 us  [absorb(): jnp.einsum('hqk,khd->hqd', weights.astype(jnp.bfloat16), value_heads, pre...]
  transfers between devices with their start and end apart: 9 -> 7, of which waited for: 6 -> 7; matrix products, arithmetic and copies ran while one was open for 9% -> 5% of each run, Pallas kernels for 0% -> 0%
where the time goes in v7:
time: 133 us; the launch traced here: 132 us
  blocking collectives  57.2 us (43%)
  waiting for transfers between devices  25.5 us (19%)
  starting transfers between devices  22 us (17%)
  matrix products  11.8 us (9%)
  other arithmetic  10.8 us (8%)
  local copies, waits for them, and re-layouts  4.6 us (3%)
    all_to_all x1, blocking collectives, per_device(): lax.all_to_all(outgoing, 'seq', split_axis=0, concat_axis=0, tiled=True)  57.2 us
    ppermute x4, waiting for transfers between devices, from_behind(): lax.ppermute(value, axis, [(source, source + steps) for source in range(l...  15.4 us
    ppermute x4, starting transfers between devices, from_behind(): lax.ppermute(value, axis, [(source, source + steps) for source in range(l...  13.5 us
    all_to_all x1, waiting for transfers between devices, per_device(): lax.all_to_all(head_term, 'tp', split_axis=0, concat_axis=0, tiled=True)  8.8 us
    all_to_all x1, starting transfers between devices, per_device(): lax.all_to_all(head_term, 'tp', split_axis=0, concat_axis=0, tiled=True)  4.42 us
    ppermute x2, starting transfers between devices, swap(): return lax.ppermute(value, 'seq', [(i, i ^ 1) for i in range(seq_count)])  4.01 us
    dot_general x5, matrix products, absorb(): jnp.einsum('hqk,khd->hqd', weights.astype(jnp.bfloat16), value_heads, pre...  3.59 us
    dot_general x5, matrix products, absorb(): jnp.einsum('qhd,khd->hqk', query_heads, key_heads, preferred_element_type...  3.21 us
  transfers between devices with their start and end apart: 7, of which 7 were waited for; matrix products, arithmetic and copies ran while one was open for 5% of the time, Pallas kernels for 0%

profile of v7, /device:TPU:32, one launch (start us, length us, event | category | flops | bytes accessed | tf_op | source)
XLA Modules:
  0.0 132.1 jit_solution(15399611028789030590)
XLA Ops:
  0.0 1.4 %convert_reduce_fusion = f32[256]{0:T(256)S(1)} fusion(bf16[256,1280]{1,0:T(8,128)(2,1)} %param.11), kind=kLoop, calls=%fused_computation.18 | loop fusion | flops 655104 | bytes 656384 | tf_op jit(solution)/shard_map/reduce_sum | solution.py:21
  1.4 1.4 %fusion.17 = f32[256]{0:T(256)S(1)} fusion(bf16[256,1280]{1,0:T(8,128)(2,1)} %param.11, f32[256]{0:T(256)S(1)} %broadcast_multiply_fusion), kind=kLoop, calls=%fused_computation.32 | loop fusion | flops 1310464 | bytes 657408 | tf_op jit(solution)/shard_map/reduce_sum | solution.py:23
  2.9 2.1 %fusion.21 = bf16[256,3,320]{0,2,1:T(8,128)(2,1)S(1)} fusion(bf16[3,1280,320]{1,2,0:T(8,128)(2,1)S(1)} %copy-done, bf16[256,1280]{1,0:T(8,128)(2,1)} %param.11, f32[1280]{0:T(1024)} %param.13, f32[1280]{0:T(1024)} %param.12, f32[256]{0:T(256)S(1)} %add_rsqrt_fusion, f32[256]{0:T(256)S(1)} %broadcast_multiply_fusion, f32[3,320]{1,0:T(4,128)} %param.15), kind=kOutput, calls=%fused_computation.37 | convolution fusion | flops 631603200 | bytes 3620608 | tf_op jit(solution)/shard_map/tc,kcd->tkd/dot_general | solution.py:54
  5.0 1.9 %collective-permute-start = (bf16[256,3,160]{0,2,1:T(8,128)(2,1)S(1)}, bf16[256,3,160]{0,2,1:T(8,128)(2,1)}, u32[]{:S(2)}, u32[]{:S(2)}) collective-permute-start(bf16[256,3,160]{0,2,1:T(8,128)(2,1)S(1)} %dynamic-slice_bitcast_fusion), channel_id=1, source_target_pairs={{0,4},{4,0},{8,12},{12,8},{16,20},{20,16},{24,28},{28,24},{32,36},... | collective-permute-start | bytes 737288 | tf_op jit(solution)/shard_map/ppermute | solution.py:48
  7.0 0.1 broadcast_in_dim.48
  7.2 0.2 reshape.320
  7.4 0.9 broadcast_compare_fusion.4
  8.3 0.2 collective-permute-done
  8.5 1.0 bitcast_select_fusion.1
  9.5 7.4 %collective-permute-start.2 = (bf16[512,2,160]{0,2,1:T(8,128)(2,1)S(1)}, bf16[512,2,160]{0,2,1:T(8,128)(2,1)S(1)}, u32[]{:S(2)}, u32[]{:S(2)}) collective-permute-start(bf16[512,2,160]{0,2,1:T(8,128)(2,1)S(1)} %pad_maximum_fusion), channel_id=1, source_target_pairs={{8,0},{12,4},{16,8},{20,12},{24,16},{28,20},{32,24},{36,28},{40,32... | collective-permute-start | bytes 983048 | tf_op jit(solution)/shard_map/ppermute | solution.py:17
  16.9 1.9 %collective-permute-start.1 = (bf16[512,2,160]{0,2,1:T(8,128)(2,1)S(1)}, bf16[512,2,160]{0,2,1:T(8,128)(2,1)S(1)}, u32[]{:S(2)}, u32[]{:S(2)}) collective-permute-start(bf16[512,2,160]{0,2,1:T(8,128)(2,1)S(1)} %pad_maximum_fusion), channel_id=1, source_target_pairs={{0,8},{4,12},{8,16},{12,20},{16,24},{20,28},{24,32},{28,36},{32,40... | collective-permute-start | bytes 983048 | tf_op jit(solution)/shard_map/ppermute | solution.py:17
  18.9 3.0 %collective-permute-start.3 = (bf16[512,2,160]{0,2,1:T(8,128)(2,1)S(1)}, bf16[512,2,160]{0,2,1:T(8,128)(2,1)S(1)}, u32[]{:S(2)}, u32[]{:S(2)}) collective-permute-start(bf16[512,2,160]{0,2,1:T(8,128)(2,1)S(1)} %pad_maximum_fusion), channel_id=1, source_target_pairs={{0,16},{4,20},{8,24},{12,28},{16,32},{20,36},{24,40},{28,44},{32,4... | collective-permute-start | bytes 983048 | tf_op jit(solution)/shard_map/ppermute | solution.py:17
  21.8 1.3 collective-permute-start.4
  23.1 0.6 fusion
  23.8 0.5 collective-permute-done.2
  24.3 0.6 fusion.2
  25.0 4.4 %collective-permute-done.1 = bf16[512,2,160]{0,2,1:T(8,128)(2,1)S(1)} collective-permute-done((bf16[512,2,160]{0,2,1:T(8,128)(2,1)S(1)}, bf16[512,2,160]{0,2,1:T(8,128)(2,1)S(1)}, u32[]{:S(2)}, u32[]{:S(2)}) %collective-permute-start.1) | collective-permute-done | bytes 327712 | tf_op jit(solution)/shard_map/ppermute | solution.py:17
  29.4 0.6 fusion.1
  30.1 10.2 %collective-permute-done.3 = bf16[512,2,160]{0,2,1:T(8,128)(2,1)S(1)} collective-permute-done((bf16[512,2,160]{0,2,1:T(8,128)(2,1)S(1)}, bf16[512,2,160]{0,2,1:T(8,128)(2,1)S(1)}, u32[]{:S(2)}, u32[]{:S(2)}) %collective-permute-start.3) | collective-permute-done | bytes 327712 | tf_op jit(solution)/shard_map/ppermute | solution.py:17
  40.3 0.6 fusion.3
  41.0 0.2 collective-permute-done.4
  41.2 0.6 fusion.4
  41.9 0.7 convolution_bitcast_fusion.2
  42.6 1.0 fusion.9
  43.6 0.7 convolution_bitcast_fusion.1
  44.3 0.5 fusion.13
  44.8 0.7 convolution_bitcast_fusion
  45.5 1.0 fusion.5
  46.5 0.7 fusion.23
  47.3 0.7 fusion.32
  48.0 0.8 copy.22
  48.8 2.1 %collective-permute-start.5 = (bf16[256,160]{1,0:T(8,128)(2,1)}, bf16[256,160]{1,0:T(8,128)(2,1)S(1)}, u32[]{:S(2)}, u32[]{:S(2)}) collective-permute-start(bf16[256,160]{1,0:T(8,128)(2,1)} %copy.22), channel_id=1, source_target_pairs={{0,4},{4,0},{8,12},{12,8},{16,20},{20,16},{24,28},{28,24},{32,36},... | collective-permute-start | bytes 245768 | tf_op jit(solution)/shard_map/ppermute | solution.py:48
  51.1 0.1 copy.23
  51.2 1.0 collective-permute-done.5
  52.3 0.1 pad_maximum_fusion.1
  52.4 2.5 %convolution_convert_fusion.1 = bf16[4,64,1280]{2,1,0:T(8,128)(2,1)} fusion(bf16[320,1280]{1,0:T(8,128)(2,1)} %param.16, bf16[64,4,320]{2,1,0:T(4,128)(2,1)S(1)} %reshape.322), kind=kOutput, calls=%fused_computation.1 | convolution fusion | flops 210042880 | bytes 1638400 | tf_op jit(solution)/shard_map/tgc,cd->tgd/dot_general | solution.py:125
  54.9 4.4 %all-to-all-start = ((bf16[4,64,1280]{2,1,0:T(8,128)(2,1)}), bf16[4,64,1280]{2,1,0:T(8,128)(2,1)}, u32[]{:S(2)}, u32[]{:S(2)}) async-start(bf16[4,64,1280]{2,1,0:T(8,128)(2,1)} %convolution_convert_fusion.1), calls=%async_computation | async-start | bytes 1310720 | tf_op jit(solution)/shard_map/all_to_all | solution.py:128
  59.3 0.2 select_reduce_fusion
  59.5 1.0 reshape.319
  60.6 1.4 %dynamic-slice_convert_fusion = f32[64,1,1280]{2,1,0:T(1,128)S(1)} fusion(bf16[64,4,1280]{2,1,0:T(4,128)(2,1)} %reshape.319, s32[]{:T(128)S(6)} %select_n.81), kind=kLoop, calls=%fused_computation.91 | loop fusion | flops 81920 | bytes 491524 | tf_op jit(solution)/shard_map/convert_element_type | solution.py:133
  61.9 8.8 %all-to-all-done = bf16[4,64,1280]{2,1,0:T(8,128)(2,1)} async-done(((bf16[4,64,1280]{2,1,0:T(8,128)(2,1)}), bf16[4,64,1280]{2,1,0:T(8,128)(2,1)}, u32[]{:S(2)}, u32[]{:S(2)}) %all-to-all-start) | async-done | bytes 655392 | tf_op jit(solution)/shard_map/all_to_all | solution.py:128
  70.7 1.2 convert_reduce_fusion.1
  72.0 0.1 fusion.93
  72.1 0.2 multiply_reduce_fusion
  72.3 0.4 convolution_convert_fusion
  72.8 1.1 all_to_all.12
  73.8 57.2 %all_to_all.17 = bf16[128,2,1280]{2,1,0:T(2,128)(2,1)S(1)} all-to-all(bf16[128,2,1280]{2,1,0:T(2,128)(2,1)} %all_to_all.12), channel_id=1, replica_groups=mesh['seq'=128,'tp'=4] {'seq'}, dimensions={0} | all-to-all | bytes 1310720 | tf_op jit(solution)/shard_map/all_to_all | solution.py:149
  131.0 1.1 all_to_all.14
  (36 shorter events, 0.7 us)
Async XLA Ops:
  0.0 2.8 %copy-start = (bf16[3,1280,320]{1,2,0:T(8,128)(2,1)S(1)}, bf16[3,1280,320]{1,2,0:T(8,128)(2,1)}, u32[]{:S(2)}) copy-start(bf16[3,1280,320]{1,2,0:T(8,128)(2,1)} %param.14) | copy-start | bytes 7372804
  2.8 4.1 %copy-start.2 = (s32[8192]{0:T(1024)S(1)}, s32[8192]{0:T(1024)}, u32[]{:S(2)}) copy-start(s32[8192]{0:T(1024)} %param.20) | copy-start | bytes 98308
  5.0 3.5 %collective-permute-start = (bf16[256,3,160]{0,2,1:T(8,128)(2,1)S(1)}, bf16[256,3,160]{0,2,1:T(8,128)(2,1)}, u32[]{:S(2)}, u32[]{:S(2)}) collective-permute-start(bf16[256,3,160]{0,2,1:T(8,128)(2,1)S(1)} %dynamic-slice_bitcast_fusion), channel_id=1, source_target_pairs={{0,4},{4,0},{8,12},{12,8},{16,20},{20,16},{24,28},{28,24},{32,36},... | collective-permute-start | bytes 737288 | tf_op jit(solution)/shard_map/ppermute | solution.py:48
  9.5 14.8 %collective-permute-start.2 = (bf16[512,2,160]{0,2,1:T(8,128)(2,1)S(1)}, bf16[512,2,160]{0,2,1:T(8,128)(2,1)S(1)}, u32[]{:S(2)}, u32[]{:S(2)}) collective-permute-start(bf16[512,2,160]{0,2,1:T(8,128)(2,1)S(1)} %pad_maximum_fusion), channel_id=1, source_target_pairs={{8,0},{12,4},{16,8},{20,12},{24,16},{28,20},{32,24},{36,28},{40,32... | collective-permute-start | bytes 983048 | tf_op jit(solution)/shard_map/ppermute | solution.py:17
  16.9 12.5 %collective-permute-start.1 = (bf16[512,2,160]{0,2,1:T(8,128)(2,1)S(1)}, bf16[512,2,160]{0,2,1:T(8,128)(2,1)S(1)}, u32[]{:S(2)}, u32[]{:S(2)}) collective-permute-start(bf16[512,2,160]{0,2,1:T(8,128)(2,1)S(1)} %pad_maximum_fusion), channel_id=1, source_target_pairs={{0,8},{4,12},{8,16},{12,20},{16,24},{20,28},{24,32},{28,36},{32,40... | collective-permute-start | bytes 983048 | tf_op jit(solution)/shard_map/ppermute | solution.py:17
  18.9 21.5 %collective-permute-start.3 = (bf16[512,2,160]{0,2,1:T(8,128)(2,1)S(1)}, bf16[512,2,160]{0,2,1:T(8,128)(2,1)S(1)}, u32[]{:S(2)}, u32[]{:S(2)}) collective-permute-start(bf16[512,2,160]{0,2,1:T(8,128)(2,1)S(1)} %pad_maximum_fusion), channel_id=1, source_target_pairs={{0,16},{4,20},{8,24},{12,28},{16,32},{20,36},{24,40},{28,44},{32,4... | collective-permute-start | bytes 983048 | tf_op jit(solution)/shard_map/ppermute | solution.py:17
  21.8 19.4 %collective-permute-start.4 = (bf16[512,2,160]{0,2,1:T(8,128)(2,1)S(1)}, bf16[512,2,160]{0,2,1:T(8,128)(2,1)S(1)}, u32[]{:S(2)}, u32[]{:S(2)}) collective-permute-start(bf16[512,2,160]{0,2,1:T(8,128)(2,1)S(1)} %pad_maximum_fusion), channel_id=1, source_target_pairs={{16,0},{20,4},{24,8},{28,12},{32,16},{36,20},{40,24},{44,28},{48,3... | collective-permute-start | bytes 983048 | tf_op jit(solution)/shard_map/ppermute | solution.py:17
  47.2 3.6 %copy-start.6 = (s32[64,1]{0,1:T(1,128)S(1)}, s32[64,1]{0,1:T(1,128)}, u32[]{:S(2)}) copy-start(s32[64,1]{0,1:T(1,128)} %param.21) | copy-start | bytes 772
  48.8 3.4 %collective-permute-start.5 = (bf16[256,160]{1,0:T(8,128)(2,1)}, bf16[256,160]{1,0:T(8,128)(2,1)S(1)}, u32[]{:S(2)}, u32[]{:S(2)}) collective-permute-start(bf16[256,160]{1,0:T(8,128)(2,1)} %copy.22), channel_id=1, source_target_pairs={{0,4},{4,0},{8,12},{12,8},{16,20},{20,16},{24,28},{28,24},{32,36},... | collective-permute-start | bytes 245768 | tf_op jit(solution)/shard_map/ppermute | solution.py:48
  51.2 8.3 %copy-start.1 = (bf16[256,1280]{1,0:T(8,128)(2,1)S(1)}, bf16[256,1280]{1,0:T(8,128)(2,1)}, u32[]{:S(2)}) copy-start(bf16[256,1280]{1,0:T(8,128)(2,1)} %param.11) | copy-start | bytes 1966084
  54.9 17.0 %copy-start.3 = (f32[1280]{0:T(1024)S(1)}, f32[1280]{0:T(1024)}, u32[]{:S(2)}) copy-start(f32[1280]{0:T(1024)} %param.17) | copy-start | bytes 15364
  54.9 15.8 %all-to-all-start = ((bf16[4,64,1280]{2,1,0:T(8,128)(2,1)}), bf16[4,64,1280]{2,1,0:T(8,128)(2,1)}, u32[]{:S(2)}, u32[]{:S(2)}) async-start(bf16[4,64,1280]{2,1,0:T(8,128)(2,1)} %convolution_convert_fusion.1), calls=%async_computation | async-start | bytes 1310720 | tf_op jit(solution)/shard_map/all_to_all | solution.py:128
  59.5 12.8 %copy-start.4 = (f32[1280]{0:T(1024)S(1)}, f32[1280]{0:T(1024)}, u32[]{:S(2)}) copy-start(f32[1280]{0:T(1024)} %param.19) | copy-start | bytes 15364
  59.5 12.8 %copy-start.5 = (f32[1280]{0:T(1024)S(1)}, f32[1280]{0:T(1024)}, u32[]{:S(2)}) copy-start(f32[1280]{0:T(1024)} %param.18) | copy-start | bytes 15364

commit v8 on v5

--- a/solution.py
+++ b/solution.py
@@ -41,8 +41,9 @@
         jnp.bfloat16
     )
     key_value = (
-        jnp.einsum("tc,kcd->tkd", normed, w_qkv[1:], preferred_element_type=jnp.float32) + b_qkv[1:]
-    ).astype(jnp.bfloat16).reshape(tok_dev, 2 * local_width)
+        jnp.einsum("tc,kcd->ktd", normed, w_qkv[1:], preferred_element_type=jnp.float32)
+        + b_qkv[1:, None, :]
+    ).astype(jnp.bfloat16)
     group_rows = tok_dev // 4
     reach_groups = SPAN * group_rows
     padding = jnp.full((reach_groups,), -1, jnp.int32)
@@ -61,8 +62,8 @@
     query_heads = query.reshape(tok_dev, local_heads, HEAD_DIM)
 
     def block_scores(block, key_segment):
-        key_heads = block[:, :local_width].reshape(-1, local_heads, HEAD_DIM)
-        value_heads = block[:, local_width:].reshape(-1, local_heads, HEAD_DIM)
+        key_heads = block[0].reshape(-1, local_heads, HEAD_DIM)
+        value_heads = block[1].reshape(-1, local_heads, HEAD_DIM)
         scores = (
             jnp.einsum("qhd,khd->hqk", query_heads, key_heads, preferred_element_type=jnp.float32)
             * scale_factor
@@ -113,8 +114,8 @@
     state = absorb_at(state, partner_own, sign)
     state = absorb_at(state, below_2, -2)
     state = absorb_at(state, above_2, 2)
-    state = absorb_at(state, partner_near[:tok_dev], sign - 2)
-    state = absorb_at(state, partner_near[tok_dev:], sign + 2)
+    state = absorb_at(state, partner_near[:2], sign - 2)
+    state = absorb_at(state, partner_near[2:], sign + 2)
     state = absorb_at(state, below_4, -4)
     state = absorb_at(state, above_4, 4)
     state = absorb_at(state, partner_far, -3 * sign)

time: 126 us -> 126 us (level)
  no operation moved by 1% of the time
where the time goes in v8:
time: 126 us; the launch traced here: 125 us
  blocking collectives  59.3 us (47%)
  starting transfers between devices  26.1 us (21%)
  matrix products  13.4 us (11%)
  waiting for transfers between devices  11.2 us (9%)
  other arithmetic  8.56 us (7%)
  local copies, waits for them, and re-layouts  5.82 us (5%)
    all_to_all x1, blocking collectives, per_device(): lax.all_to_all(outgoing, 'seq', split_axis=0, concat_axis=0, tiled=True)  59.3 us
    ppermute x4, starting transfers between devices, from_behind(): lax.ppermute(value, axis, [(source, source + steps) for source in range(l...  15.4 us
    all_to_all x1, waiting for transfers between devices, per_device(): lax.all_to_all(head_term, 'tp', split_axis=0, concat_axis=0, tiled=True)  10.9 us
    ppermute x3, starting transfers between devices, swap(): return lax.ppermute(value, 'seq', [(i, i ^ 1) for i in range(seq_count)])  6.39 us
    all_to_all x1, starting transfers between devices, per_device(): lax.all_to_all(head_term, 'tp', split_axis=0, concat_axis=0, tiled=True)  4.31 us
    dot_general x9, matrix products, block_scores(): jnp.einsum('qhd,khd->hqk', query_heads, key_heads, preferred_element_type...  4.21 us
    dot_general x1, matrix products, per_device(): jnp.einsum('tc,kcd->ktd', normed, w_qkv[1:], preferred_element_type=jnp.f...  2.91 us
    dot_general x9, matrix products, absorb(): jnp.einsum('hqk,khd->hqd', weights.astype(jnp.bfloat16), value_heads, pre...  2.85 us
  transfers between devices with their start and end apart: 8, of which 2 were waited for; matrix products, arithmetic and copies ran while one was open for 10% of the time, Pallas kernels for 0%

profile of v8, /device:TPU:32, one launch (start us, length us, event | category | flops | bytes accessed | tf_op | source)
XLA Modules:
  0.0 125.0 jit_solution(12747946590803541609)
XLA Ops:
  0.0 1.4 %convert_reduce_fusion = f32[256]{0:T(256)S(1)} fusion(bf16[256,1280]{1,0:T(8,128)(2,1)} %param.11), kind=kLoop, calls=%fused_computation.5 | loop fusion | flops 655104 | bytes 656384 | tf_op jit(solution)/shard_map/reduce_sum | solution.py:21
  1.4 1.4 %fusion.13 = f32[256]{0:T(256)S(1)} fusion(bf16[256,1280]{1,0:T(8,128)(2,1)} %param.11, f32[256]{0:T(256)S(1)} %broadcast_multiply_fusion), kind=kLoop, calls=%fused_computation.26 | loop fusion | flops 1310464 | bytes 657408 | tf_op jit(solution)/shard_map/reduce_sum | solution.py:23
  2.9 2.9 %fusion.23 = bf16[2,256,320]{1,2,0:T(8,128)(2,1)} fusion(bf16[3,1280,320]{1,2,0:T(8,128)(2,1)} %param.14, f32[2,320]{1,0:T(2,128)S(1)} %slice.79, bf16[256,1280]{1,0:T(8,128)(2,1)S(1)} %copy-done.1, f32[1280]{0:T(1024)S(1)} %copy-done.14, f32[1280]{0:T(1024)S(1)} %copy-done.15, f32[256]{0:T(256)S(1)} %add_rsqrt_fusion, f32[256]{0:T(256)S(1)} %broadcast_multiply_fusion), kind=kOutput, calls=%fused_computation.33 | convolution fusion | flops 421724160 | bytes 2636288 | tf_op jit(solution)/shard_map/tc,kcd->ktd/dot_general | solution.py:44
  5.8 3.8 %collective-permute-start.1 = (bf16[2,256,320]{1,2,0:T(8,128)(2,1)}, bf16[2,256,320]{1,2,0:T(8,128)(2,1)S(1)}, u32[]{:S(2)}, u32[]{:S(2)}) collective-permute-start(bf16[2,256,320]{1,2,0:T(8,128)(2,1)} %fusion.23), channel_id=1, source_target_pairs={{0,8},{4,12},{8,16},{12,20},{16,24},{20,28},{24,32},{28,36},{32,40... | collective-permute-start | bytes 983048 | tf_op jit(solution)/shard_map/ppermute | solution.py:17
  9.6 4.8 %collective-permute-start.2 = (bf16[2,256,320]{1,2,0:T(8,128)(2,1)}, bf16[2,256,320]{1,2,0:T(8,128)(2,1)S(1)}, u32[]{:S(2)}, u32[]{:S(2)}) collective-permute-start(bf16[2,256,320]{1,2,0:T(8,128)(2,1)} %fusion.23), channel_id=1, source_target_pairs={{8,0},{12,4},{16,8},{20,12},{24,16},{28,20},{32,24},{36,28},{40,32... | collective-permute-start | bytes 983048 | tf_op jit(solution)/shard_map/ppermute | solution.py:17
  14.5 1.3 %collective-permute-start.5 = (bf16[2,256,320]{1,2,0:T(8,128)(2,1)}, bf16[2,256,320]{1,2,0:T(8,128)(2,1)S(1)}, u32[]{:S(2)}, u32[]{:S(2)}) collective-permute-start(bf16[2,256,320]{1,2,0:T(8,128)(2,1)} %fusion.23), channel_id=1, source_target_pairs={{16,0},{20,4},{24,8},{28,12},{32,16},{36,20},{40,24},{44,28},{48,3... | collective-permute-start | bytes 983048 | tf_op jit(solution)/shard_map/ppermute | solution.py:17
  15.8 5.5 %collective-permute-start.4 = (bf16[2,256,320]{1,2,0:T(8,128)(2,1)}, bf16[2,256,320]{1,2,0:T(8,128)(2,1)S(1)}, u32[]{:S(2)}, u32[]{:S(2)}) collective-permute-start(bf16[2,256,320]{1,2,0:T(8,128)(2,1)} %fusion.23), channel_id=1, source_target_pairs={{0,16},{4,20},{8,24},{12,28},{16,32},{20,36},{24,40},{28,44},{32,4... | collective-permute-start | bytes 983048 | tf_op jit(solution)/shard_map/ppermute | solution.py:17
  21.2 1.9 %collective-permute-start = (bf16[2,256,320]{1,2,0:T(8,128)(2,1)}, bf16[2,256,320]{1,2,0:T(8,128)(2,1)}, u32[]{:S(2)}, u32[]{:S(2)}) collective-permute-start(bf16[2,256,320]{1,2,0:T(8,128)(2,1)} %fusion.23), channel_id=1, source_target_pairs={{0,4},{4,0},{8,12},{12,8},{16,20},{20,16},{24,28},{28,24},{32,36},... | collective-permute-start | bytes 983048 | tf_op jit(solution)/shard_map/ppermute | solution.py:101
  23.2 1.7 %fusion.109 = (bf16[1,256,320]{1,2,0:T(8,128)(2,1)S(1)}, bf16[1,256,320]{1,2,0:T(8,128)(2,1)}) fusion(bf16[2,256,320]{1,2,0:T(8,128)(2,1)} %fusion.23), kind=kLoop, calls=%fused_computation.154 | loop fusion | bytes 655360 | tf_op jit(solution)/shard_map/slice | solution.py:66
  25.3 1.7 %fusion.43 = bf16[256,320]{0,1:T(8,128)(2,1)S(1)} fusion(bf16[3,1280,320]{1,2,0:T(8,128)(2,1)} %param.14, f32[320]{0:T(512)S(1)} %slice_reduce_fusion, bf16[256,1280]{1,0:T(8,128)(2,1)S(1)} %copy-done.1, f32[1280]{0:T(1024)S(1)} %copy-done.14, f32[1280]{0:T(1024)S(1)} %copy-done.15, f32[256]{0:T(256)S(1)} %add_rsqrt_fusion, f32[256]{0:T(256)S(1)} %broadcast_multiply_fusion), kind=kOutput, calls=%fused_computation.54 | convolution fusion | flops 211845120 | bytes 1651968 | tf_op jit(solution)/shard_map/dot_general | solution.py:40
  27.2 1.1 broadcast_compare_fusion.8
  28.3 0.7 fusion.97
  29.0 1.4 %reduce_window_sum.11 = s32[64,128]{1,0:T(8,128)} reduce-window(s32[64,128]{1,0:T(8,128)} %fusion.97, s32[]{:T(128)} %constant.77.clone.1), window={size=64x1 pad=63_0x0_0}, to_apply=%region_0.0 | reduce-window | flops 516096 | bytes 65540 | tf_op jit(solution)/shard_map/jit(cumsum)/reduce_window_sum | solution.py:142
  30.4 1.2 fusion.124
  31.7 2.4 %collective-permute-start.3 = (bf16[4,256,320]{1,2,0:T(8,128)(2,1)S(1)}, bf16[4,256,320]{1,2,0:T(8,128)(2,1)S(1)}, u32[]{:S(2)}, u32[]{:S(2)}) collective-permute-start(bf16[4,256,320]{1,2,0:T(8,128)(2,1)S(1)} %pad_maximum_fusion), channel_id=1, source_target_pairs={{0,4},{4,0},{8,12},{12,8},{16,20},{20,16},{24,28},{28,24},{32,36},... | collective-permute-start | bytes 1966088 | tf_op jit(solution)/shard_map/ppermute | solution.py:101
  34.1 0.3 collective-permute-done.5
  34.5 2.1 %collective-permute-start.6 = (bf16[2,256,320]{1,2,0:T(8,128)(2,1)S(1)}, bf16[2,256,320]{1,2,0:T(8,128)(2,1)S(1)}, u32[]{:S(2)}, u32[]{:S(2)}) collective-permute-start(bf16[2,256,320]{1,2,0:T(8,128)(2,1)S(1)} %broadcast_select_fusion), channel_id=1, source_target_pairs={{0,4},{4,0},{8,12},{12,8},{16,20},{20,16},{24,28},{28,24},{32,36},... | collective-permute-start | bytes 983048 | tf_op jit(solution)/shard_map/ppermute | solution.py:101
  36.6 0.4 fusion.117
  37.0 0.4 fusion.118
  37.4 0.4 copy-done.4
  37.8 0.4 fusion.121
  38.3 0.4 fusion.122
  38.6 1.0 fusion.108
  39.7 0.4 fusion.123
  40.1 0.4 fusion.116
  40.5 0.4 fusion.119
  40.9 0.4 fusion.120
  41.3 0.3 fusion.78
  41.6 0.3 fusion.48
  41.9 0.3 fusion.76
  42.2 0.3 fusion.74
  42.5 0.3 fusion.52
  42.8 0.3 fusion.72
  43.1 0.3 fusion.70
  43.4 0.3 fusion.56
  43.8 0.3 fusion.68
  44.2 0.3 fusion.66
  44.5 0.3 fusion.44
  44.9 0.3 fusion.26
  45.2 0.4 fusion.42
  46.2 1.3 %convolution_convert_fusion.1 = bf16[4,64,1280]{2,1,0:T(8,128)(2,1)} fusion(bf16[4,64,320]{2,1,0:T(8,128)(2,1)S(1)} %convert_element_type.96, bf16[320,1280]{1,0:T(8,128)(2,1)S(1)} %copy-done), kind=kOutput, calls=%fused_computation.1 | convolution fusion | flops 210042880 | bytes 1638400 | tf_op jit(solution)/shard_map/tgc,cd->tgd/dot_general | solution.py:127
  47.6 4.3 %all-to-all-start = ((bf16[4,64,1280]{2,1,0:T(8,128)(2,1)}), bf16[4,64,1280]{2,1,0:T(8,128)(2,1)S(1)}, u32[]{:S(2)}, u32[]{:S(2)}) async-start(bf16[4,64,1280]{2,1,0:T(8,128)(2,1)} %convolution_convert_fusion.1), calls=%async_computation | async-start | bytes 1310720 | tf_op jit(solution)/shard_map/all_to_all | solution.py:130
  52.2 0.3 dynamic-slice_convert_fusion
  52.6 10.9 %all-to-all-done = bf16[4,64,1280]{2,1,0:T(8,128)(2,1)S(1)} async-done(((bf16[4,64,1280]{2,1,0:T(8,128)(2,1)}), bf16[4,64,1280]{2,1,0:T(8,128)(2,1)S(1)}, u32[]{:S(2)}, u32[]{:S(2)}) %all-to-all-start) | async-done | bytes 655392 | tf_op jit(solution)/shard_map/all_to_all | solution.py:130
  63.9 0.4 convolution_convert_fusion
  64.3 0.2 all_to_all.12
  64.6 59.3 %all_to_all.17 = bf16[128,2,1280]{2,1,0:T(2,128)(2,1)S(1)} all-to-all(bf16[128,2,1280]{2,1,0:T(2,128)(2,1)S(1)} %all_to_all.12), channel_id=1, replica_groups=mesh['seq'=128,'tp'=4] {'seq'}, dimensions={0} | all-to-all | bytes 1310720 | tf_op jit(solution)/shard_map/all_to_all | solution.py:151
  123.9 1.1 all_to_all.14
  (68 shorter events, 2.5 us)
Async XLA Ops:
  0.0 46.2 %copy-start = (bf16[320,1280]{1,0:T(8,128)(2,1)S(1)}, bf16[320,1280]{1,0:T(8,128)(2,1)}, u32[]{:S(2)}) copy-start(bf16[320,1280]{1,0:T(8,128)(2,1)} %param.16) | copy-start | bytes 2457604
  0.0 2.8 %copy-start.1 = (bf16[256,1280]{1,0:T(8,128)(2,1)S(1)}, bf16[256,1280]{1,0:T(8,128)(2,1)}, u32[]{:S(2)}) copy-start(bf16[256,1280]{1,0:T(8,128)(2,1)} %param.11) | copy-start | bytes 1966084
  0.0 2.8 %copy-start.12 = (f32[3,320]{1,0:T(4,128)S(1)}, f32[3,320]{1,0:T(4,128)}, u32[]{:S(2)}) copy-start(f32[3,320]{1,0:T(4,128)} %param.15) | copy-start | bytes 11524
  0.0 2.8 %copy-start.15 = (f32[1280]{0:T(1024)S(1)}, f32[1280]{0:T(1024)}, u32[]{:S(2)}) copy-start(f32[1280]{0:T(1024)} %param.12) | copy-start | bytes 15364
  0.0 2.8 %copy-start.14 = (f32[1280]{0:T(1024)S(1)}, f32[1280]{0:T(1024)}, u32[]{:S(2)}) copy-start(f32[1280]{0:T(1024)} %param.13) | copy-start | bytes 15364
  2.9 22.0 %copy-start.8 = (s32[8192]{0:T(1024)S(1)}, s32[8192]{0:T(1024)}, u32[]{:S(2)}) copy-start(s32[8192]{0:T(1024)} %param.20) | copy-start | bytes 98308
  5.8 25.8 %collective-permute-start.1 = (bf16[2,256,320]{1,2,0:T(8,128)(2,1)}, bf16[2,256,320]{1,2,0:T(8,128)(2,1)S(1)}, u32[]{:S(2)}, u32[]{:S(2)}) collective-permute-start(bf16[2,256,320]{1,2,0:T(8,128)(2,1)} %fusion.23), channel_id=1, source_target_pairs={{0,8},{4,12},{8,16},{12,20},{16,24},{20,28},{24,32},{28,36},{32,40... | collective-permute-start | bytes 983048 | tf_op jit(solution)/shard_map/ppermute | solution.py:17
  9.6 22.0 %collective-permute-start.2 = (bf16[2,256,320]{1,2,0:T(8,128)(2,1)}, bf16[2,256,320]{1,2,0:T(8,128)(2,1)S(1)}, u32[]{:S(2)}, u32[]{:S(2)}) collective-permute-start(bf16[2,256,320]{1,2,0:T(8,128)(2,1)} %fusion.23), channel_id=1, source_target_pairs={{8,0},{12,4},{16,8},{20,12},{24,16},{28,20},{32,24},{36,28},{40,32... | collective-permute-start | bytes 983048 | tf_op jit(solution)/shard_map/ppermute | solution.py:17
  14.5 20.0 %collective-permute-start.5 = (bf16[2,256,320]{1,2,0:T(8,128)(2,1)}, bf16[2,256,320]{1,2,0:T(8,128)(2,1)S(1)}, u32[]{:S(2)}, u32[]{:S(2)}) collective-permute-start(bf16[2,256,320]{1,2,0:T(8,128)(2,1)} %fusion.23), channel_id=1, source_target_pairs={{16,0},{20,4},{24,8},{28,12},{32,16},{36,20},{40,24},{44,28},{48,3... | collective-permute-start | bytes 983048 | tf_op jit(solution)/shard_map/ppermute | solution.py:17
  15.8 18.7 %collective-permute-start.4 = (bf16[2,256,320]{1,2,0:T(8,128)(2,1)}, bf16[2,256,320]{1,2,0:T(8,128)(2,1)S(1)}, u32[]{:S(2)}, u32[]{:S(2)}) collective-permute-start(bf16[2,256,320]{1,2,0:T(8,128)(2,1)} %fusion.23), channel_id=1, source_target_pairs={{0,16},{4,20},{8,24},{12,28},{16,32},{20,36},{24,40},{28,44},{32,4... | collective-permute-start | bytes 983048 | tf_op jit(solution)/shard_map/ppermute | solution.py:17
  21.2 17.4 %collective-permute-start = (bf16[2,256,320]{1,2,0:T(8,128)(2,1)}, bf16[2,256,320]{1,2,0:T(8,128)(2,1)}, u32[]{:S(2)}, u32[]{:S(2)}) collective-permute-start(bf16[2,256,320]{1,2,0:T(8,128)(2,1)} %fusion.23), channel_id=1, source_target_pairs={{0,4},{4,0},{8,12},{12,8},{16,20},{20,16},{24,28},{28,24},{32,36},... | collective-permute-start | bytes 983048 | tf_op jit(solution)/shard_map/ppermute | solution.py:101
  25.3 3.0 %copy-start.13 = (s32[64,1]{0,1:T(1,128)S(1)}, s32[64,1]{0,1:T(1,128)}, u32[]{:S(2)}) copy-start(s32[64,1]{0,1:T(1,128)} %param.21) | copy-start | bytes 772
  25.3 5.1 %copy-start.2 = (bf16[1,256,320]{1,2,0:T(8,128)(2,1)S(1)}, bf16[1,256,320]{1,2,0:T(8,128)(2,1)}, u32[]{:S(2)}) copy-start(bf16[1,256,320]{1,2,0:T(8,128)(2,1)} %get-tuple-element.31) | copy-start | bytes 491524
  31.6 5.0 %copy-start.6 = (pred[256,256]{0,1:T(8,128)(4,1)S(1)}, pred[256,256]{0,1:T(8,128)(4,1)}, u32[]{:S(2)}) copy-start(pred[256,256]{0,1:T(8,128)(4,1)} %get-tuple-element.59) | copy-start | bytes 196612
  31.7 8.8 %collective-permute-start.3 = (bf16[4,256,320]{1,2,0:T(8,128)(2,1)S(1)}, bf16[4,256,320]{1,2,0:T(8,128)(2,1)S(1)}, u32[]{:S(2)}, u32[]{:S(2)}) collective-permute-start(bf16[4,256,320]{1,2,0:T(8,128)(2,1)S(1)} %pad_maximum_fusion), channel_id=1, source_target_pairs={{0,4},{4,0},{8,12},{12,8},{16,20},{20,16},{24,28},{28,24},{32,36},... | collective-permute-start | bytes 1966088 | tf_op jit(solution)/shard_map/ppermute | solution.py:101
  34.5 2.5 %copy-start.5 = (pred[256,256]{0,1:T(8,128)(4,1)S(1)}, pred[256,256]{0,1:T(8,128)(4,1)}, u32[]{:S(2)}) copy-start(pred[256,256]{0,1:T(8,128)(4,1)} %get-tuple-element.58) | copy-start | bytes 196612
  34.5 5.5 %collective-permute-start.6 = (bf16[2,256,320]{1,2,0:T(8,128)(2,1)S(1)}, bf16[2,256,320]{1,2,0:T(8,128)(2,1)S(1)}, u32[]{:S(2)}, u32[]{:S(2)}) collective-permute-start(bf16[2,256,320]{1,2,0:T(8,128)(2,1)S(1)} %broadcast_select_fusion), channel_id=1, source_target_pairs={{0,4},{4,0},{8,12},{12,8},{16,20},{20,16},{24,28},{28,24},{32,36},... | collective-permute-start | bytes 983048 | tf_op jit(solution)/shard_map/ppermute | solution.py:101
  37.0 0.8 copy-start.4
  37.4 0.8 copy-start.3
  46.2 5.7 %copy-start.7 = (s32[64,128]{1,0:T(8,128)S(1)}, s32[64,128]{1,0:T(8,128)}, u32[]{:S(2)}) copy-start(s32[64,128]{1,0:T(8,128)} %reduce_window_sum.11) | copy-start | bytes 98308
  47.6 15.9 %all-to-all-start = ((bf16[4,64,1280]{2,1,0:T(8,128)(2,1)}), bf16[4,64,1280]{2,1,0:T(8,128)(2,1)S(1)}, u32[]{:S(2)}, u32[]{:S(2)}) async-start(bf16[4,64,1280]{2,1,0:T(8,128)(2,1)} %convolution_convert_fusion.1), calls=%async_computation | async-start | bytes 1310720 | tf_op jit(solution)/shard_map/all_to_all | solution.py:130
  52.1 11.5 %copy-start.9 = (f32[1280]{0:T(1024)S(1)}, f32[1280]{0:T(1024)}, u32[]{:S(2)}) copy-start(f32[1280]{0:T(1024)} %param.17) | copy-start | bytes 15364
  52.5 11.4 %copy-start.10 = (f32[1280]{0:T(1024)S(1)}, f32[1280]{0:T(1024)}, u32[]{:S(2)}) copy-start(f32[1280]{0:T(1024)} %param.19) | copy-start | bytes 15364
  52.6 11.4 %copy-start.11 = (f32[1280]{0:T(1024)S(1)}, f32[1280]{0:T(1024)}, u32[]{:S(2)}) copy-start(f32[1280]{0:T(1024)} %param.18) | copy-start | bytes 15364

commit v9 on v8

--- a/solution.py
+++ b/solution.py
@@ -107,15 +107,14 @@
     above_2 = from_behind(key_value, "seq", -2)
     below_4 = from_behind(key_value, "seq", 4)
     above_4 = from_behind(key_value, "seq", -4)
-    partner_own = swap(key_value)
     state = absorb(start_state, key_value, query_segment)
-    partner_near = swap(jnp.concatenate([below_2, above_2], axis=0))
+    partner_near = swap(jnp.concatenate([key_value, below_2, above_2], axis=0))
     partner_far = swap(jnp.where(sign > 0, above_4, below_4))
-    state = absorb_at(state, partner_own, sign)
     state = absorb_at(state, below_2, -2)
     state = absorb_at(state, above_2, 2)
-    state = absorb_at(state, partner_near[:2], sign - 2)
-    state = absorb_at(state, partner_near[2:], sign + 2)
+    state = absorb_at(state, partner_near[:2], sign)
+    state = absorb_at(state, partner_near[2:4], sign - 2)
+    state = absorb_at(state, partner_near[4:], sign + 2)
     state = absorb_at(state, below_4, -4)
     state = absorb_at(state, above_4, 4)
     state = absorb_at(state, partner_far, -3 * sign)

time: 126 us -> 126 us (level)
  waiting for transfers between devices: 11.2 us -> 14.6 us
  starting transfers between devices: 26.1 us -> 23.8 us
    ppermute x4, waiting for transfers between devices: 0.32 us -> 3.74 us  [from_behind(): lax.ppermute(value, axis, [(source, source + steps) for source in range(l...]
    ppermute x3 -> x2, starting transfers between devices: 6.39 us -> 4.1 us  [swap(): return lax.ppermute(value, 'seq', [(i, i ^ 1) for i in range(seq_count)])]
    slice x7 -> x6, local copies, waits for them, and re-layouts: 2.83 us -> 0.89 us  [block_scores(): value_heads = block[1].reshape(-1, local_heads, HEAD_DIM)]
    unnamed x32 -> x38, local copies, waits for them, and re-layouts: 0.46 us -> 2.13 us
  transfers between devices with their start and end apart: 8 -> 7, of which waited for: 2 -> 2; matrix products, arithmetic and copies ran while one was open for 10% -> 8% of each run, Pallas kernels for 0% -> 0%
where the time goes in v9:
time: 126 us; the launch traced here: 125 us
  blocking collectives  59.4 us (47%)
  starting transfers between devices  23.8 us (19%)
  waiting for transfers between devices  14.6 us (12%)
  matrix products  12.8 us (10%)
  other arithmetic  8.1 us (6%)
  local copies, waits for them, and re-layouts  5.54 us (4%)
    all_to_all x1, blocking collectives, per_device(): lax.all_to_all(outgoing, 'seq', split_axis=0, concat_axis=0, tiled=True)  59.4 us
    ppermute x4, starting transfers between devices, from_behind(): lax.ppermute(value, axis, [(source, source + steps) for source in range(l...  15.4 us
    all_to_all x1, waiting for transfers between devices, per_device(): lax.all_to_all(head_term, 'tp', split_axis=0, concat_axis=0, tiled=True)  10.9 us
    all_to_all x1, starting transfers between devices, per_device(): lax.all_to_all(head_term, 'tp', split_axis=0, concat_axis=0, tiled=True)  4.27 us
    dot_general x9, matrix products, block_scores(): jnp.einsum('qhd,khd->hqk', query_heads, key_heads, preferred_element_type...  4.24 us
    ppermute x2, starting transfers between devices, swap(): return lax.ppermute(value, 'seq', [(i, i ^ 1) for i in range(seq_count)])  4.1 us
    ppermute x4, waiting for transfers between devices, from_behind(): lax.ppermute(value, axis, [(source, source + steps) for source in range(l...  3.74 us
    dot_general x9, matrix products, absorb(): jnp.einsum('hqk,khd->hqd', weights.astype(jnp.bfloat16), value_heads, pre...  2.84 us
  transfers between devices with their start and end apart: 7, of which 2 were waited for; matrix products, arithmetic and copies ran while one was open for 8% of the time, Pallas kernels for 0%

profile of v9, /device:TPU:32, one launch (start us, length us, event | category | flops | bytes accessed | tf_op | source)
XLA Modules:
  0.0 124.8 jit_solution(15085539574690075584)
XLA Ops:
  0.0 1.4 %convert_reduce_fusion = f32[256]{0:T(256)S(1)} fusion(bf16[256,1280]{1,0:T(8,128)(2,1)} %param.11), kind=kLoop, calls=%fused_computation.5 | loop fusion | flops 655104 | bytes 656384 | tf_op jit(solution)/shard_map/reduce_sum | solution.py:21
  1.4 1.4 %fusion.13 = f32[256]{0:T(256)S(1)} fusion(bf16[256,1280]{1,0:T(8,128)(2,1)} %param.11, f32[256]{0:T(256)S(1)} %broadcast_multiply_fusion), kind=kLoop, calls=%fused_computation.26 | loop fusion | flops 1310464 | bytes 657408 | tf_op jit(solution)/shard_map/reduce_sum | solution.py:23
  2.9 2.2 %fusion.23 = bf16[2,256,320]{1,2,0:T(8,128)(2,1)S(1)} fusion(bf16[3,1280,320]{1,2,0:T(8,128)(2,1)} %param.14, f32[2,320]{1,0:T(2,128)S(1)} %slice.82, bf16[256,1280]{1,0:T(8,128)(2,1)S(1)} %copy-done.1, f32[1280]{0:T(1024)S(1)} %copy-done.17, f32[1280]{0:T(1024)S(1)} %copy-done.18, f32[256]{0:T(256)S(1)} %add_rsqrt_fusion, f32[256]{0:T(256)S(1)} %broadcast_multiply_fusion), kind=kOutput, calls=%fused_computation.33 | convolution fusion | flops 421724160 | bytes 2636288 | tf_op jit(solution)/shard_map/tc,kcd->ktd/dot_general | solution.py:44
  5.1 3.8 %collective-permute-start = (bf16[2,256,320]{1,2,0:T(8,128)(2,1)S(1)}, bf16[2,256,320]{1,2,0:T(8,128)(2,1)S(1)}, u32[]{:S(2)}, u32[]{:S(2)}) collective-permute-start(bf16[2,256,320]{1,2,0:T(8,128)(2,1)S(1)} %fusion.23), channel_id=1, source_target_pairs={{0,8},{4,12},{8,16},{12,20},{16,24},{20,28},{24,32},{28,36},{32,40... | collective-permute-start | bytes 983048 | tf_op jit(solution)/shard_map/ppermute | solution.py:17
  8.9 4.8 %collective-permute-start.1 = (bf16[2,256,320]{1,2,0:T(8,128)(2,1)S(1)}, bf16[2,256,320]{1,2,0:T(8,128)(2,1)S(1)}, u32[]{:S(2)}, u32[]{:S(2)}) collective-permute-start(bf16[2,256,320]{1,2,0:T(8,128)(2,1)S(1)} %fusion.23), channel_id=1, source_target_pairs={{8,0},{12,4},{16,8},{20,12},{24,16},{28,20},{32,24},{36,28},{40,32... | collective-permute-start | bytes 983048 | tf_op jit(solution)/shard_map/ppermute | solution.py:17
  13.8 1.3 %collective-permute-start.4 = (bf16[2,256,320]{1,2,0:T(8,128)(2,1)S(1)}, bf16[2,256,320]{1,2,0:T(8,128)(2,1)S(1)}, u32[]{:S(2)}, u32[]{:S(2)}) collective-permute-start(bf16[2,256,320]{1,2,0:T(8,128)(2,1)S(1)} %fusion.23), channel_id=1, source_target_pairs={{16,0},{20,4},{24,8},{28,12},{32,16},{36,20},{40,24},{44,28},{48,3... | collective-permute-start | bytes 983048 | tf_op jit(solution)/shard_map/ppermute | solution.py:17
  15.1 5.5 %collective-permute-start.3 = (bf16[2,256,320]{1,2,0:T(8,128)(2,1)S(1)}, bf16[2,256,320]{1,2,0:T(8,128)(2,1)S(1)}, u32[]{:S(2)}, u32[]{:S(2)}) collective-permute-start(bf16[2,256,320]{1,2,0:T(8,128)(2,1)S(1)} %fusion.23), channel_id=1, source_target_pairs={{0,16},{4,20},{8,24},{12,28},{16,32},{20,36},{24,40},{28,44},{32,4... | collective-permute-start | bytes 983048 | tf_op jit(solution)/shard_map/ppermute | solution.py:17
  20.6 0.7 fusion.109
  21.8 1.8 %fusion.43 = bf16[256,320]{0,1:T(8,128)(2,1)S(1)} fusion(bf16[3,1280,320]{1,2,0:T(8,128)(2,1)} %param.14, f32[320]{0:T(512)S(1)} %slice_reduce_fusion, bf16[256,1280]{1,0:T(8,128)(2,1)S(1)} %copy-done.1, f32[1280]{0:T(1024)} %param.13, f32[1280]{0:T(1024)} %param.12, f32[256]{0:T(256)S(1)} %add_rsqrt_fusion, f32[256]{0:T(256)S(1)} %broadcast_multiply_fusion), kind=kOutput, calls=%fused_computation.54 | convolution fusion | flops 211845120 | bytes 1658112 | tf_op jit(solution)/shard_map/dot_general | solution.py:40
  23.6 1.2 broadcast_compare_fusion.8
  24.8 0.7 fusion.97
  25.5 0.9 reduce_window_sum.11
  26.4 1.2 fusion.123
  27.7 2.1 %collective-permute-start.2 = (bf16[6,256,320]{1,2,0:T(8,128)(2,1)S(1)}, bf16[6,256,320]{1,2,0:T(8,128)(2,1)S(1)}, u32[]{:S(2)}, u32[]{:S(2)}) collective-permute-start(bf16[6,256,320]{1,2,0:T(8,128)(2,1)S(1)} %pad_maximum_fusion), channel_id=1, source_target_pairs={{0,4},{4,0},{8,12},{12,8},{16,20},{20,16},{24,28},{28,24},{32,36},... | collective-permute-start | bytes 2949128 | tf_op jit(solution)/shard_map/ppermute | solution.py:101
  29.8 3.7 %collective-permute-done.4 = bf16[2,256,320]{1,2,0:T(8,128)(2,1)S(1)} collective-permute-done((bf16[2,256,320]{1,2,0:T(8,128)(2,1)S(1)}, bf16[2,256,320]{1,2,0:T(8,128)(2,1)S(1)}, u32[]{:S(2)}, u32[]{:S(2)}) %collective-permute-start.4) | collective-permute-done | bytes 327712 | tf_op jit(solution)/shard_map/ppermute | solution.py:17
  33.6 2.1 %collective-permute-start.5 = (bf16[2,256,320]{1,2,0:T(8,128)(2,1)S(1)}, bf16[2,256,320]{1,2,0:T(8,128)(2,1)S(1)}, u32[]{:S(2)}, u32[]{:S(2)}) collective-permute-start(bf16[2,256,320]{1,2,0:T(8,128)(2,1)S(1)} %broadcast_select_fusion), channel_id=1, source_target_pairs={{0,4},{4,0},{8,12},{12,8},{16,20},{20,16},{24,28},{28,24},{32,36},... | collective-permute-start | bytes 983048 | tf_op jit(solution)/shard_map/ppermute | solution.py:101
  35.7 0.4 fusion.116
  36.1 0.4 fusion.117
  36.6 0.4 copy-done.8
  36.9 0.4 fusion.121
  37.4 0.4 fusion.122
  37.8 0.4 copy-done.6
  38.1 0.4 fusion.115
  38.6 0.7 copy-done.5
  39.4 0.4 fusion.118
  39.8 0.4 fusion.119
  40.1 0.4 fusion.120
  40.6 0.3 fusion.78
  40.9 0.3 fusion.48
  41.2 0.3 fusion.76
  41.5 0.3 fusion.74
  41.8 0.3 fusion.52
  42.1 0.3 fusion.72
  42.4 0.3 fusion.70
  42.7 0.3 fusion.56
  43.0 0.3 fusion.68
  43.5 0.3 fusion.66
  43.8 0.3 fusion.44
  44.1 0.6 copy-done.2
  44.7 0.3 fusion.26
  45.0 0.4 fusion.42
  46.0 1.3 %convolution_convert_fusion.1 = bf16[4,64,1280]{2,1,0:T(8,128)(2,1)} fusion(bf16[4,64,320]{2,1,0:T(8,128)(2,1)S(1)} %convert_element_type.96, bf16[320,1280]{1,0:T(8,128)(2,1)S(1)} %copy-done), kind=kOutput, calls=%fused_computation.1 | convolution fusion | flops 210042880 | bytes 1638400 | tf_op jit(solution)/shard_map/tgc,cd->tgd/dot_general | solution.py:126
  47.3 4.3 %all-to-all-start = ((bf16[4,64,1280]{2,1,0:T(8,128)(2,1)}), bf16[4,64,1280]{2,1,0:T(8,128)(2,1)S(1)}, u32[]{:S(2)}, u32[]{:S(2)}) async-start(bf16[4,64,1280]{2,1,0:T(8,128)(2,1)} %convolution_convert_fusion.1), calls=%async_computation | async-start | bytes 1310720 | tf_op jit(solution)/shard_map/all_to_all | solution.py:129
  52.0 0.3 dynamic-slice_convert_fusion
  52.3 10.9 %all-to-all-done = bf16[4,64,1280]{2,1,0:T(8,128)(2,1)S(1)} async-done(((bf16[4,64,1280]{2,1,0:T(8,128)(2,1)}), bf16[4,64,1280]{2,1,0:T(8,128)(2,1)S(1)}, u32[]{:S(2)}, u32[]{:S(2)}) %all-to-all-start) | async-done | bytes 655392 | tf_op jit(solution)/shard_map/all_to_all | solution.py:129
  63.7 0.4 convolution_convert_fusion
  64.3 59.4 %all_to_all.17 = bf16[128,2,1280]{2,1,0:T(2,128)(2,1)S(1)} all-to-all(bf16[128,2,1280]{2,1,0:T(2,128)(2,1)S(1)} %all_to_all.12), channel_id=1, replica_groups=mesh['seq'=128,'tp'=4] {'seq'}, dimensions={0} | all-to-all | bytes 1310720 | tf_op jit(solution)/shard_map/all_to_all | solution.py:150
  123.7 1.1 all_to_all.14
  (71 shorter events, 2.8 us)
Async XLA Ops:
  0.0 46.0 %copy-start = (bf16[320,1280]{1,0:T(8,128)(2,1)S(1)}, bf16[320,1280]{1,0:T(8,128)(2,1)}, u32[]{:S(2)}) copy-start(bf16[320,1280]{1,0:T(8,128)(2,1)} %param.16) | copy-start | bytes 2457604
  0.0 2.8 %copy-start.1 = (bf16[256,1280]{1,0:T(8,128)(2,1)S(1)}, bf16[256,1280]{1,0:T(8,128)(2,1)}, u32[]{:S(2)}) copy-start(bf16[256,1280]{1,0:T(8,128)(2,1)} %param.11) | copy-start | bytes 1966084
  0.0 2.8 %copy-start.15 = (f32[3,320]{1,0:T(4,128)S(1)}, f32[3,320]{1,0:T(4,128)}, u32[]{:S(2)}) copy-start(f32[3,320]{1,0:T(4,128)} %param.15) | copy-start | bytes 11524
  0.0 2.8 %copy-start.18 = (f32[1280]{0:T(1024)S(1)}, f32[1280]{0:T(1024)}, u32[]{:S(2)}) copy-start(f32[1280]{0:T(1024)} %param.12) | copy-start | bytes 15364
  0.0 2.8 %copy-start.17 = (f32[1280]{0:T(1024)S(1)}, f32[1280]{0:T(1024)}, u32[]{:S(2)}) copy-start(f32[1280]{0:T(1024)} %param.13) | copy-start | bytes 15364
  2.9 18.4 %copy-start.11 = (s32[8192]{0:T(1024)S(1)}, s32[8192]{0:T(1024)}, u32[]{:S(2)}) copy-start(s32[8192]{0:T(1024)} %param.20) | copy-start | bytes 98308
  5.1 22.5 %collective-permute-start = (bf16[2,256,320]{1,2,0:T(8,128)(2,1)S(1)}, bf16[2,256,320]{1,2,0:T(8,128)(2,1)S(1)}, u32[]{:S(2)}, u32[]{:S(2)}) collective-permute-start(bf16[2,256,320]{1,2,0:T(8,128)(2,1)S(1)} %fusion.23), channel_id=1, source_target_pairs={{0,8},{4,12},{8,16},{12,20},{16,24},{20,28},{24,32},{28,36},{32,40... | collective-permute-start | bytes 983048 | tf_op jit(solution)/shard_map/ppermute | solution.py:17
  8.9 18.7 %collective-permute-start.1 = (bf16[2,256,320]{1,2,0:T(8,128)(2,1)S(1)}, bf16[2,256,320]{1,2,0:T(8,128)(2,1)S(1)}, u32[]{:S(2)}, u32[]{:S(2)}) collective-permute-start(bf16[2,256,320]{1,2,0:T(8,128)(2,1)S(1)} %fusion.23), channel_id=1, source_target_pairs={{8,0},{12,4},{16,8},{20,12},{24,16},{28,20},{32,24},{36,28},{40,32... | collective-permute-start | bytes 983048 | tf_op jit(solution)/shard_map/ppermute | solution.py:17
  13.8 19.8 %collective-permute-start.4 = (bf16[2,256,320]{1,2,0:T(8,128)(2,1)S(1)}, bf16[2,256,320]{1,2,0:T(8,128)(2,1)S(1)}, u32[]{:S(2)}, u32[]{:S(2)}) collective-permute-start(bf16[2,256,320]{1,2,0:T(8,128)(2,1)S(1)} %fusion.23), channel_id=1, source_target_pairs={{16,0},{20,4},{24,8},{28,12},{32,16},{36,20},{40,24},{44,28},{48,3... | collective-permute-start | bytes 983048 | tf_op jit(solution)/shard_map/ppermute | solution.py:17
  15.1 18.5 %collective-permute-start.3 = (bf16[2,256,320]{1,2,0:T(8,128)(2,1)S(1)}, bf16[2,256,320]{1,2,0:T(8,128)(2,1)S(1)}, u32[]{:S(2)}, u32[]{:S(2)}) collective-permute-start(bf16[2,256,320]{1,2,0:T(8,128)(2,1)S(1)} %fusion.23), channel_id=1, source_target_pairs={{0,16},{4,20},{8,24},{12,28},{16,32},{20,36},{24,40},{28,44},{32,4... | collective-permute-start | bytes 983048 | tf_op jit(solution)/shard_map/ppermute | solution.py:17
  21.7 3.1 %copy-start.16 = (s32[64,1]{0,1:T(1,128)S(1)}, s32[64,1]{0,1:T(1,128)}, u32[]{:S(2)}) copy-start(s32[64,1]{0,1:T(1,128)} %param.21) | copy-start | bytes 772
  21.8 4.6 %copy-start.3 = (bf16[1,256,320]{1,2,0:T(8,128)(2,1)S(1)}, bf16[1,256,320]{1,2,0:T(8,128)(2,1)}, u32[]{:S(2)}) copy-start(bf16[1,256,320]{1,2,0:T(8,128)(2,1)} %get-tuple-element.33) | copy-start | bytes 491524
  27.7 8.0 %copy-start.10 = (pred[256,256]{0,1:T(8,128)(4,1)S(1)}, pred[256,256]{0,1:T(8,128)(4,1)}, u32[]{:S(2)}) copy-start(pred[256,256]{0,1:T(8,128)(4,1)} %get-tuple-element.59) | copy-start | bytes 196612
  27.7 10.8 %collective-permute-start.2 = (bf16[6,256,320]{1,2,0:T(8,128)(2,1)S(1)}, bf16[6,256,320]{1,2,0:T(8,128)(2,1)S(1)}, u32[]{:S(2)}, u32[]{:S(2)}) collective-permute-start(bf16[6,256,320]{1,2,0:T(8,128)(2,1)S(1)} %pad_maximum_fusion), channel_id=1, source_target_pairs={{0,4},{4,0},{8,12},{12,8},{16,20},{20,16},{24,28},{28,24},{32,36},... | collective-permute-start | bytes 2949128 | tf_op jit(solution)/shard_map/ppermute | solution.py:101
  33.6 2.5 %copy-start.9 = (pred[256,256]{0,1:T(8,128)(4,1)S(1)}, pred[256,256]{0,1:T(8,128)(4,1)}, u32[]{:S(2)}) copy-start(pred[256,256]{0,1:T(8,128)(4,1)} %get-tuple-element.58) | copy-start | bytes 196612
  33.6 4.2 %collective-permute-start.5 = (bf16[2,256,320]{1,2,0:T(8,128)(2,1)S(1)}, bf16[2,256,320]{1,2,0:T(8,128)(2,1)S(1)}, u32[]{:S(2)}, u32[]{:S(2)}) collective-permute-start(bf16[2,256,320]{1,2,0:T(8,128)(2,1)S(1)} %broadcast_select_fusion), channel_id=1, source_target_pairs={{0,4},{4,0},{8,12},{12,8},{16,20},{20,16},{24,28},{28,24},{32,36},... | collective-permute-start | bytes 983048 | tf_op jit(solution)/shard_map/ppermute | solution.py:101
  36.1 0.8 copy-start.8
  36.5 0.8 copy-start.7
  37.3 0.8 copy-start.6
  38.5 0.8 copy-start.5
  38.5 1.2 copy-start.4
  43.8 0.9 copy-start.2
  47.3 15.8 %all-to-all-start = ((bf16[4,64,1280]{2,1,0:T(8,128)(2,1)}), bf16[4,64,1280]{2,1,0:T(8,128)(2,1)S(1)}, u32[]{:S(2)}, u32[]{:S(2)}) async-start(bf16[4,64,1280]{2,1,0:T(8,128)(2,1)} %convolution_convert_fusion.1), calls=%async_computation | async-start | bytes 1310720 | tf_op jit(solution)/shard_map/all_to_all | solution.py:129
  51.8 11.5 %copy-start.12 = (f32[1280]{0:T(1024)S(1)}, f32[1280]{0:T(1024)}, u32[]{:S(2)}) copy-start(f32[1280]{0:T(1024)} %param.17) | copy-start | bytes 15364
  52.3 11.4 %copy-start.13 = (f32[1280]{0:T(1024)S(1)}, f32[1280]{0:T(1024)}, u32[]{:S(2)}) copy-start(f32[1280]{0:T(1024)} %param.19) | copy-start | bytes 15364
  52.3 11.4 %copy-start.14 = (f32[1280]{0:T(1024)S(1)}, f32[1280]{0:T(1024)}, u32[]{:S(2)}) copy-start(f32[1280]{0:T(1024)} %param.18) | copy-start | bytes 15364

commit v10 on v8

--- a/solution.py
+++ b/solution.py
@@ -36,7 +36,14 @@
     row_start = seq_index * tok_dev
     reach_rows = SPAN * tok_dev
     scale_factor = HEAD_DIM ** (-0.5)
-    normed = layer_norm(tokens.astype(jnp.float32), ln_gain, ln_bias).astype(jnp.bfloat16)
+    ones = jnp.ones((model_width, 1), jnp.float32)
+    center = jnp.dot(tokens, ones.astype(tokens.dtype), preferred_element_type=jnp.float32) / model_width
+    centered = tokens.astype(jnp.float32) - center
+    spread = (
+        jnp.dot(centered * centered, ones, precision=lax.Precision.HIGHEST, preferred_element_type=jnp.float32)
+        / model_width
+    )
+    normed = (centered * lax.rsqrt(spread + epsilon) * ln_gain + ln_bias).astype(jnp.bfloat16)
     query = (jnp.dot(normed, w_qkv[0], preferred_element_type=jnp.float32) + b_qkv[0]).astype(
         jnp.bfloat16
     )

time: 126 us -> 127 us (level)
  matrix products: 13.4 us -> 17.3 us
  other arithmetic: 8.56 us -> 5.81 us
    dot_general x0 -> x2, matrix products: none -> 3.83 us  [the longest x1 2.39 us: per_device(): jnp.dot(centered * centered, ones, precision=lax.Precision.HIGHEST, prefe...]
    reduce_sum x2 -> x1, other arithmetic: 1.6 us -> 0.2 us  [layer_norm(): spread = jnp.mean(centered * centered, axis=-1, keepdims=True)]
    reduce_sum x2 -> x1, other arithmetic: 1.51 us -> 0.14 us  [layer_norm(): center = jnp.mean(values, axis=-1, keepdims=True)]
where the time goes in v10:
time: 127 us; the launch traced here: 126 us
  blocking collectives  59.4 us (47%)
  starting transfers between devices  26 us (20%)
  matrix products  17.3 us (14%)
  waiting for transfers between devices  11.2 us (9%)
  local copies, waits for them, and re-layouts  5.82 us (5%)
  other arithmetic  5.81 us (5%)
    all_to_all x1, blocking collectives, per_device(): lax.all_to_all(outgoing, 'seq', split_axis=0, concat_axis=0, tiled=True)  59.4 us
    ppermute x4, starting transfers between devices, from_behind(): lax.ppermute(value, axis, [(source, source + steps) for source in range(l...  15.4 us
    all_to_all x1, waiting for transfers between devices, per_device(): lax.all_to_all(head_term, 'tp', split_axis=0, concat_axis=0, tiled=True)  10.9 us
    ppermute x3, starting transfers between devices, swap(): return lax.ppermute(value, 'seq', [(i, i ^ 1) for i in range(seq_count)])  6.38 us
    all_to_all x1, starting transfers between devices, per_device(): lax.all_to_all(head_term, 'tp', split_axis=0, concat_axis=0, tiled=True)  4.25 us
    dot_general x9, matrix products, block_scores(): jnp.einsum('qhd,khd->hqk', query_heads, key_heads, preferred_element_type...  4.23 us
    dot_general x1, matrix products, per_device(): jnp.einsum('tc,kcd->ktd', normed, w_qkv[1:], preferred_element_type=jnp.f...  2.91 us
    dot_general x9, matrix products, absorb(): jnp.einsum('hqk,khd->hqd', weights.astype(jnp.bfloat16), value_heads, pre...  2.85 us
  transfers between devices with their start and end apart: 8, of which 2 were waited for; matrix products, arithmetic and copies ran while one was open for 10% of the time, Pallas kernels for 0%

profile of v10, /device:TPU:32, one launch (start us, length us, event | category | flops | bytes accessed | tf_op | source)
XLA Modules:
  0.0 126.1 jit_solution(8188600846136053919)
XLA Ops:
  0.0 1.4 %fusion.98 = f32[1,256]{1,0:T(1,128)S(1)} fusion(bf16[256,1280]{1,0:T(8,128)(2,1)} %param.11), kind=kOutput, calls=%fused_computation.140 | convolution fusion | flops 655360 | bytes 656384 | tf_op jit(solution)/shard_map/dot_general | solution.py:40
  1.5 2.4 %fusion.11 = f32[1,256]{1,0:T(1,128)S(1)} fusion(bf16[256,1280]{1,0:T(8,128)(2,1)} %param.11, f32[256]{0:T(256)S(1)} %broadcast_multiply_fusion), kind=kOutput, calls=%fused_computation.24 | convolution fusion | flops 4915200 | bytes 657408 | tf_op jit(solution)/shard_map/dot_general | solution.py:43
  4.0 2.9 %fusion.19 = bf16[2,256,320]{1,2,0:T(8,128)(2,1)} fusion(bf16[3,1280,320]{1,2,0:T(8,128)(2,1)} %param.14, f32[2,320]{1,0:T(2,128)S(1)} %slice.79, bf16[256,1280]{1,0:T(8,128)(2,1)S(1)} %copy-done.1, f32[1280]{0:T(1024)S(1)} %copy-done.14, f32[1280]{0:T(1024)S(1)} %copy-done.15, f32[256]{0:T(256)S(1)} %add_rsqrt_fusion, f32[256]{0:T(256)S(1)} %broadcast_multiply_fusion), kind=kOutput, calls=%fused_computation.29 | convolution fusion | flops 421724160 | bytes 2636288 | tf_op jit(solution)/shard_map/tc,kcd->ktd/dot_general | solution.py:51
  6.9 3.8 %collective-permute-start.1 = (bf16[2,256,320]{1,2,0:T(8,128)(2,1)}, bf16[2,256,320]{1,2,0:T(8,128)(2,1)S(1)}, u32[]{:S(2)}, u32[]{:S(2)}) collective-permute-start(bf16[2,256,320]{1,2,0:T(8,128)(2,1)} %fusion.19), channel_id=1, source_target_pairs={{0,8},{4,12},{8,16},{12,20},{16,24},{20,28},{24,32},{28,36},{32,40... | collective-permute-start | bytes 983048 | tf_op jit(solution)/shard_map/ppermute | solution.py:17
  10.7 4.8 %collective-permute-start.2 = (bf16[2,256,320]{1,2,0:T(8,128)(2,1)}, bf16[2,256,320]{1,2,0:T(8,128)(2,1)S(1)}, u32[]{:S(2)}, u32[]{:S(2)}) collective-permute-start(bf16[2,256,320]{1,2,0:T(8,128)(2,1)} %fusion.19), channel_id=1, source_target_pairs={{8,0},{12,4},{16,8},{20,12},{24,16},{28,20},{32,24},{36,28},{40,32... | collective-permute-start | bytes 983048 | tf_op jit(solution)/shard_map/ppermute | solution.py:17
  15.5 1.3 %collective-permute-start.5 = (bf16[2,256,320]{1,2,0:T(8,128)(2,1)}, bf16[2,256,320]{1,2,0:T(8,128)(2,1)S(1)}, u32[]{:S(2)}, u32[]{:S(2)}) collective-permute-start(bf16[2,256,320]{1,2,0:T(8,128)(2,1)} %fusion.19), channel_id=1, source_target_pairs={{16,0},{20,4},{24,8},{28,12},{32,16},{36,20},{40,24},{44,28},{48,3... | collective-permute-start | bytes 983048 | tf_op jit(solution)/shard_map/ppermute | solution.py:17
  16.8 5.5 %collective-permute-start.4 = (bf16[2,256,320]{1,2,0:T(8,128)(2,1)}, bf16[2,256,320]{1,2,0:T(8,128)(2,1)S(1)}, u32[]{:S(2)}, u32[]{:S(2)}) collective-permute-start(bf16[2,256,320]{1,2,0:T(8,128)(2,1)} %fusion.19), channel_id=1, source_target_pairs={{0,16},{4,20},{8,24},{12,28},{16,32},{20,36},{24,40},{28,44},{32,4... | collective-permute-start | bytes 983048 | tf_op jit(solution)/shard_map/ppermute | solution.py:17
  22.3 1.9 %collective-permute-start = (bf16[2,256,320]{1,2,0:T(8,128)(2,1)}, bf16[2,256,320]{1,2,0:T(8,128)(2,1)}, u32[]{:S(2)}, u32[]{:S(2)}) collective-permute-start(bf16[2,256,320]{1,2,0:T(8,128)(2,1)} %fusion.19), channel_id=1, source_target_pairs={{0,4},{4,0},{8,12},{12,8},{16,20},{20,16},{24,28},{28,24},{32,36},... | collective-permute-start | bytes 983048 | tf_op jit(solution)/shard_map/ppermute | solution.py:108
  24.3 1.7 %fusion.109 = (bf16[1,256,320]{1,2,0:T(8,128)(2,1)S(1)}, bf16[1,256,320]{1,2,0:T(8,128)(2,1)}) fusion(bf16[2,256,320]{1,2,0:T(8,128)(2,1)} %fusion.19), kind=kLoop, calls=%fused_computation.156 | loop fusion | bytes 655360 | tf_op jit(solution)/shard_map/slice | solution.py:73
  26.4 1.7 %fusion.39 = bf16[256,320]{0,1:T(8,128)(2,1)S(1)} fusion(bf16[3,1280,320]{1,2,0:T(8,128)(2,1)} %param.14, f32[320]{0:T(512)S(1)} %slice_reduce_fusion, bf16[256,1280]{1,0:T(8,128)(2,1)S(1)} %copy-done.1, f32[1280]{0:T(1024)S(1)} %copy-done.14, f32[1280]{0:T(1024)S(1)} %copy-done.15, f32[256]{0:T(256)S(1)} %add_rsqrt_fusion, f32[256]{0:T(256)S(1)} %broadcast_multiply_fusion), kind=kOutput, calls=%fused_computation.50 | convolution fusion | flops 211845120 | bytes 1651968 | tf_op jit(solution)/shard_map/dot_general | solution.py:47
  28.2 1.1 broadcast_compare_fusion.8
  29.4 0.7 fusion.94
  30.0 1.4 %reduce_window_sum.11 = s32[64,128]{1,0:T(8,128)} reduce-window(s32[64,128]{1,0:T(8,128)} %fusion.94, s32[]{:T(128)} %constant.79.clone.1), window={size=64x1 pad=63_0x0_0}, to_apply=%region_0.1 | reduce-window | flops 516096 | bytes 65540 | tf_op jit(solution)/shard_map/jit(cumsum)/reduce_window_sum | solution.py:149
  31.5 1.2 fusion.124
  32.8 2.4 %collective-permute-start.3 = (bf16[4,256,320]{1,2,0:T(8,128)(2,1)S(1)}, bf16[4,256,320]{1,2,0:T(8,128)(2,1)S(1)}, u32[]{:S(2)}, u32[]{:S(2)}) collective-permute-start(bf16[4,256,320]{1,2,0:T(8,128)(2,1)S(1)} %pad_maximum_fusion), channel_id=1, source_target_pairs={{0,4},{4,0},{8,12},{12,8},{16,20},{20,16},{24,28},{28,24},{32,36},... | collective-permute-start | bytes 1966088 | tf_op jit(solution)/shard_map/ppermute | solution.py:108
  35.2 0.3 collective-permute-done.5
  35.6 2.1 %collective-permute-start.6 = (bf16[2,256,320]{1,2,0:T(8,128)(2,1)S(1)}, bf16[2,256,320]{1,2,0:T(8,128)(2,1)S(1)}, u32[]{:S(2)}, u32[]{:S(2)}) collective-permute-start(bf16[2,256,320]{1,2,0:T(8,128)(2,1)S(1)} %broadcast_select_fusion), channel_id=1, source_target_pairs={{0,4},{4,0},{8,12},{12,8},{16,20},{20,16},{24,28},{28,24},{32,36},... | collective-permute-start | bytes 983048 | tf_op jit(solution)/shard_map/ppermute | solution.py:108
  37.7 0.4 fusion.117
  38.1 0.4 fusion.118
  38.5 0.4 copy-done.4
  38.9 0.4 fusion.121
  39.4 0.4 fusion.122
  39.7 1.0 fusion.108
  40.8 0.4 fusion.123
  41.2 0.4 fusion.116
  41.6 0.4 fusion.119
  42.0 0.4 fusion.120
  42.4 0.3 fusion.75
  42.7 0.3 fusion.44
  43.0 0.3 fusion.73
  43.3 0.3 fusion.71
  43.6 0.3 fusion.48
  44.0 0.3 fusion.69
  44.3 0.3 fusion.67
  44.6 0.3 fusion.52
  44.9 0.3 fusion.65
  45.3 0.3 fusion.63
  45.6 0.3 fusion.40
  46.0 0.3 fusion.22
  46.3 0.4 fusion.38
  47.3 1.3 %convolution_convert_fusion.1 = bf16[4,64,1280]{2,1,0:T(8,128)(2,1)} fusion(bf16[4,64,320]{2,1,0:T(8,128)(2,1)S(1)} %convert_element_type.100, bf16[320,1280]{1,0:T(8,128)(2,1)S(1)} %copy-done), kind=kOutput, calls=%fused_computation.1 | convolution fusion | flops 210042880 | bytes 1638400 | tf_op jit(solution)/shard_map/tgc,cd->tgd/dot_general | solution.py:134
  48.7 4.3 %all-to-all-start = ((bf16[4,64,1280]{2,1,0:T(8,128)(2,1)}), bf16[4,64,1280]{2,1,0:T(8,128)(2,1)S(1)}, u32[]{:S(2)}, u32[]{:S(2)}) async-start(bf16[4,64,1280]{2,1,0:T(8,128)(2,1)} %convolution_convert_fusion.1), calls=%async_computation | async-start | bytes 1310720 | tf_op jit(solution)/shard_map/all_to_all | solution.py:137
  53.3 0.3 dynamic-slice_convert_fusion
  53.6 10.9 %all-to-all-done = bf16[4,64,1280]{2,1,0:T(8,128)(2,1)S(1)} async-done(((bf16[4,64,1280]{2,1,0:T(8,128)(2,1)}), bf16[4,64,1280]{2,1,0:T(8,128)(2,1)S(1)}, u32[]{:S(2)}, u32[]{:S(2)}) %all-to-all-start) | async-done | bytes 655392 | tf_op jit(solution)/shard_map/all_to_all | solution.py:137
  65.0 0.4 convolution_convert_fusion
  65.4 0.2 all_to_all.12
  65.6 59.4 %all_to_all.17 = bf16[128,2,1280]{2,1,0:T(2,128)(2,1)S(1)} all-to-all(bf16[128,2,1280]{2,1,0:T(2,128)(2,1)S(1)} %all_to_all.12), channel_id=1, replica_groups=mesh['seq'=128,'tp'=4] {'seq'}, dimensions={0} | all-to-all | bytes 1310720 | tf_op jit(solution)/shard_map/all_to_all | solution.py:158
  125.1 1.1 all_to_all.14
  (68 shorter events, 2.5 us)
Async XLA Ops:
  0.0 47.3 %copy-start = (bf16[320,1280]{1,0:T(8,128)(2,1)S(1)}, bf16[320,1280]{1,0:T(8,128)(2,1)}, u32[]{:S(2)}) copy-start(bf16[320,1280]{1,0:T(8,128)(2,1)} %param.16) | copy-start | bytes 2457604
  0.0 3.9 %copy-start.1 = (bf16[256,1280]{1,0:T(8,128)(2,1)S(1)}, bf16[256,1280]{1,0:T(8,128)(2,1)}, u32[]{:S(2)}) copy-start(bf16[256,1280]{1,0:T(8,128)(2,1)} %param.11) | copy-start | bytes 1966084
  0.0 3.9 %copy-start.12 = (f32[3,320]{1,0:T(4,128)S(1)}, f32[3,320]{1,0:T(4,128)}, u32[]{:S(2)}) copy-start(f32[3,320]{1,0:T(4,128)} %param.15) | copy-start | bytes 11524
  0.0 3.9 %copy-start.15 = (f32[1280]{0:T(1024)S(1)}, f32[1280]{0:T(1024)}, u32[]{:S(2)}) copy-start(f32[1280]{0:T(1024)} %param.12) | copy-start | bytes 15364
  0.0 3.9 %copy-start.14 = (f32[1280]{0:T(1024)S(1)}, f32[1280]{0:T(1024)}, u32[]{:S(2)}) copy-start(f32[1280]{0:T(1024)} %param.13) | copy-start | bytes 15364
  3.9 22.0 %copy-start.8 = (s32[8192]{0:T(1024)S(1)}, s32[8192]{0:T(1024)}, u32[]{:S(2)}) copy-start(s32[8192]{0:T(1024)} %param.20) | copy-start | bytes 98308
  6.9 25.8 %collective-permute-start.1 = (bf16[2,256,320]{1,2,0:T(8,128)(2,1)}, bf16[2,256,320]{1,2,0:T(8,128)(2,1)S(1)}, u32[]{:S(2)}, u32[]{:S(2)}) collective-permute-start(bf16[2,256,320]{1,2,0:T(8,128)(2,1)} %fusion.19), channel_id=1, source_target_pairs={{0,8},{4,12},{8,16},{12,20},{16,24},{20,28},{24,32},{28,36},{32,40... | collective-permute-start | bytes 983048 | tf_op jit(solution)/shard_map/ppermute | solution.py:17
  10.7 22.0 %collective-permute-start.2 = (bf16[2,256,320]{1,2,0:T(8,128)(2,1)}, bf16[2,256,320]{1,2,0:T(8,128)(2,1)S(1)}, u32[]{:S(2)}, u32[]{:S(2)}) collective-permute-start(bf16[2,256,320]{1,2,0:T(8,128)(2,1)} %fusion.19), channel_id=1, source_target_pairs={{8,0},{12,4},{16,8},{20,12},{24,16},{28,20},{32,24},{36,28},{40,32... | collective-permute-start | bytes 983048 | tf_op jit(solution)/shard_map/ppermute | solution.py:17
  15.5 20.0 %collective-permute-start.5 = (bf16[2,256,320]{1,2,0:T(8,128)(2,1)}, bf16[2,256,320]{1,2,0:T(8,128)(2,1)S(1)}, u32[]{:S(2)}, u32[]{:S(2)}) collective-permute-start(bf16[2,256,320]{1,2,0:T(8,128)(2,1)} %fusion.19), channel_id=1, source_target_pairs={{16,0},{20,4},{24,8},{28,12},{32,16},{36,20},{40,24},{44,28},{48,3... | collective-permute-start | bytes 983048 | tf_op jit(solution)/shard_map/ppermute | solution.py:17
  16.8 18.7 %collective-permute-start.4 = (bf16[2,256,320]{1,2,0:T(8,128)(2,1)}, bf16[2,256,320]{1,2,0:T(8,128)(2,1)S(1)}, u32[]{:S(2)}, u32[]{:S(2)}) collective-permute-start(bf16[2,256,320]{1,2,0:T(8,128)(2,1)} %fusion.19), channel_id=1, source_target_pairs={{0,16},{4,20},{8,24},{12,28},{16,32},{20,36},{24,40},{28,44},{32,4... | collective-permute-start | bytes 983048 | tf_op jit(solution)/shard_map/ppermute | solution.py:17
  22.3 17.4 %collective-permute-start = (bf16[2,256,320]{1,2,0:T(8,128)(2,1)}, bf16[2,256,320]{1,2,0:T(8,128)(2,1)}, u32[]{:S(2)}, u32[]{:S(2)}) collective-permute-start(bf16[2,256,320]{1,2,0:T(8,128)(2,1)} %fusion.19), channel_id=1, source_target_pairs={{0,4},{4,0},{8,12},{12,8},{16,20},{20,16},{24,28},{28,24},{32,36},... | collective-permute-start | bytes 983048 | tf_op jit(solution)/shard_map/ppermute | solution.py:108
  26.4 3.0 %copy-start.13 = (s32[64,1]{0,1:T(1,128)S(1)}, s32[64,1]{0,1:T(1,128)}, u32[]{:S(2)}) copy-start(s32[64,1]{0,1:T(1,128)} %param.21) | copy-start | bytes 772
  26.4 5.1 %copy-start.2 = (bf16[1,256,320]{1,2,0:T(8,128)(2,1)S(1)}, bf16[1,256,320]{1,2,0:T(8,128)(2,1)}, u32[]{:S(2)}) copy-start(bf16[1,256,320]{1,2,0:T(8,128)(2,1)} %get-tuple-element.31) | copy-start | bytes 491524
  32.7 5.0 %copy-start.6 = (pred[256,256]{0,1:T(8,128)(4,1)S(1)}, pred[256,256]{0,1:T(8,128)(4,1)}, u32[]{:S(2)}) copy-start(pred[256,256]{0,1:T(8,128)(4,1)} %get-tuple-element.59) | copy-start | bytes 196612
  32.8 8.8 %collective-permute-start.3 = (bf16[4,256,320]{1,2,0:T(8,128)(2,1)S(1)}, bf16[4,256,320]{1,2,0:T(8,128)(2,1)S(1)}, u32[]{:S(2)}, u32[]{:S(2)}) collective-permute-start(bf16[4,256,320]{1,2,0:T(8,128)(2,1)S(1)} %pad_maximum_fusion), channel_id=1, source_target_pairs={{0,4},{4,0},{8,12},{12,8},{16,20},{20,16},{24,28},{28,24},{32,36},... | collective-permute-start | bytes 1966088 | tf_op jit(solution)/shard_map/ppermute | solution.py:108
  35.6 2.5 %copy-start.5 = (pred[256,256]{0,1:T(8,128)(4,1)S(1)}, pred[256,256]{0,1:T(8,128)(4,1)}, u32[]{:S(2)}) copy-start(pred[256,256]{0,1:T(8,128)(4,1)} %get-tuple-element.58) | copy-start | bytes 196612
  35.6 5.6 %collective-permute-start.6 = (bf16[2,256,320]{1,2,0:T(8,128)(2,1)S(1)}, bf16[2,256,320]{1,2,0:T(8,128)(2,1)S(1)}, u32[]{:S(2)}, u32[]{:S(2)}) collective-permute-start(bf16[2,256,320]{1,2,0:T(8,128)(2,1)S(1)} %broadcast_select_fusion), channel_id=1, source_target_pairs={{0,4},{4,0},{8,12},{12,8},{16,20},{20,16},{24,28},{28,24},{32,36},... | collective-permute-start | bytes 983048 | tf_op jit(solution)/shard_map/ppermute | solution.py:108
  38.1 0.8 copy-start.4
  38.5 0.8 copy-start.3
  47.3 5.6 %copy-start.7 = (s32[64,128]{1,0:T(8,128)S(1)}, s32[64,128]{1,0:T(8,128)}, u32[]{:S(2)}) copy-start(s32[64,128]{1,0:T(8,128)} %reduce_window_sum.11) | copy-start | bytes 98308
  48.7 15.8 %all-to-all-start = ((bf16[4,64,1280]{2,1,0:T(8,128)(2,1)}), bf16[4,64,1280]{2,1,0:T(8,128)(2,1)S(1)}, u32[]{:S(2)}, u32[]{:S(2)}) async-start(bf16[4,64,1280]{2,1,0:T(8,128)(2,1)} %convolution_convert_fusion.1), calls=%async_computation | async-start | bytes 1310720 | tf_op jit(solution)/shard_map/all_to_all | solution.py:137
  53.1 11.5 %copy-start.9 = (f32[1280]{0:T(1024)S(1)}, f32[1280]{0:T(1024)}, u32[]{:S(2)}) copy-start(f32[1280]{0:T(1024)} %param.17) | copy-start | bytes 15364
  53.6 11.4 %copy-start.10 = (f32[1280]{0:T(1024)S(1)}, f32[1280]{0:T(1024)}, u32[]{:S(2)}) copy-start(f32[1280]{0:T(1024)} %param.19) | copy-start | bytes 15364
  53.6 11.4 %copy-start.11 = (f32[1280]{0:T(1024)S(1)}, f32[1280]{0:T(1024)}, u32[]{:S(2)}) copy-start(f32[1280]{0:T(1024)} %param.18) | copy-start | bytes 15364

commit v11 on v8

--- a/solution.py
+++ b/solution.py
@@ -110,7 +110,8 @@
     partner_own = swap(key_value)
     state = absorb(start_state, key_value, query_segment)
     partner_near = swap(jnp.concatenate([below_2, above_2], axis=0))
-    partner_far = swap(jnp.where(sign > 0, above_4, below_4))
+    partner_below = swap(below_4)
+    partner_above = swap(above_4)
     state = absorb_at(state, partner_own, sign)
     state = absorb_at(state, below_2, -2)
     state = absorb_at(state, above_2, 2)
@@ -118,7 +119,7 @@
     state = absorb_at(state, partner_near[2:], sign + 2)
     state = absorb_at(state, below_4, -4)
     state = absorb_at(state, above_4, 4)
-    state = absorb_at(state, partner_far, -3 * sign)
+    state = absorb_at(state, jnp.where(sign > 0, partner_below, partner_above), -3 * sign)
     row_top, totals, summed = state
     tp_index = lax.axis_index("tp")
     quarter = tok_dev // 4

time: 126 us -> 126 us (level)
  other arithmetic: 8.56 us -> 6.63 us
  waiting for transfers between devices: 11.2 us -> 12.9 us
  blocking collectives: 59.3 us -> 60.6 us
    ppermute x3 -> x4, starting transfers between devices: 6.39 us -> 8.78 us  [swap(): return lax.ppermute(value, 'seq', [(i, i ^ 1) for i in range(seq_count)])]
    ppermute x4, starting transfers between devices: 15.4 us -> 13.4 us  [from_behind(): lax.ppermute(value, axis, [(source, source + steps) for source in range(l...]
    ppermute x4, waiting for transfers between devices: 0.32 us -> 2.12 us  [from_behind(): lax.ppermute(value, axis, [(source, source + steps) for source in range(l...]
    another operation x1, other arithmetic: 1.43 us -> 0.1 us  [per_device(): earlier = jnp.cumsum(owner_table, axis=0) - owner_table]
  transfers between devices with their start and end apart: 8 -> 9, of which waited for: 2 -> 2; matrix products, arithmetic and copies ran while one was open for 10% -> 8% of each run, Pallas kernels for 0% -> 0%
where the time goes in v11:
time: 126 us
  blocking collectives  60.6 us (48%)
  starting transfers between devices  26.6 us (21%)
  waiting for transfers between devices  12.9 us (10%)
  matrix products  12.5 us (10%)
  other arithmetic  6.63 us (5%)
  local copies, waits for them, and re-layouts  5.75 us (5%)
    all_to_all x1, blocking collectives, per_device(): lax.all_to_all(outgoing, 'seq', split_axis=0, concat_axis=0, tiled=True)  60.6 us
    ppermute x4, starting transfers between devices, from_behind(): lax.ppermute(value, axis, [(source, source + steps) for source in range(l...  13.4 us
    all_to_all x1, waiting for transfers between devices, per_device(): lax.all_to_all(head_term, 'tp', split_axis=0, concat_axis=0, tiled=True)  10.7 us
    ppermute x4, starting transfers between devices, swap(): return lax.ppermute(value, 'seq', [(i, i ^ 1) for i in range(seq_count)])  8.78 us
    all_to_all x1, starting transfers between devices, per_device(): lax.all_to_all(head_term, 'tp', split_axis=0, concat_axis=0, tiled=True)  4.34 us
    dot_general x9, matrix products, block_scores(): jnp.einsum('qhd,khd->hqk', query_heads, key_heads, preferred_element_type...  3.39 us
    dot_general x1, matrix products, per_device(): jnp.einsum('tc,kcd->ktd', normed, w_qkv[1:], preferred_element_type=jnp.f...  2.91 us
    dot_general x9, matrix products, absorb(): jnp.einsum('hqk,khd->hqd', weights.astype(jnp.bfloat16), value_heads, pre...  2.82 us
  transfers between devices with their start and end apart: 9, of which 2 were waited for; matrix products, arithmetic and copies ran while one was open for 8% of the time, Pallas kernels for 0%

profile of v11, /device:TPU:32, one launch (start us, length us, event | category | flops | bytes accessed | tf_op | source)
XLA Modules:
  0.0 125.5 jit_solution(14916167707757255688)
XLA Ops:
  0.0 1.4 %convert_reduce_fusion = f32[256]{0:T(256)S(1)} fusion(bf16[256,1280]{1,0:T(8,128)(2,1)} %param.11), kind=kLoop, calls=%fused_computation.5 | loop fusion | flops 655104 | bytes 656384 | tf_op jit(solution)/shard_map/reduce_sum | solution.py:21
  1.4 1.4 %fusion.13 = f32[256]{0:T(256)S(1)} fusion(bf16[256,1280]{1,0:T(8,128)(2,1)} %param.11, f32[256]{0:T(256)S(1)} %broadcast_multiply_fusion), kind=kLoop, calls=%fused_computation.26 | loop fusion | flops 1310464 | bytes 657408 | tf_op jit(solution)/shard_map/reduce_sum | solution.py:23
  2.9 2.9 %fusion.23 = bf16[2,256,320]{1,2,0:T(8,128)(2,1)} fusion(bf16[3,1280,320]{1,2,0:T(8,128)(2,1)} %param.14, f32[2,320]{1,0:T(2,128)S(1)} %slice.79, bf16[256,1280]{1,0:T(8,128)(2,1)S(1)} %copy-done.1, f32[1280]{0:T(1024)S(1)} %copy-done.10, f32[1280]{0:T(1024)S(1)} %copy-done.11, f32[256]{0:T(256)S(1)} %add_rsqrt_fusion, f32[256]{0:T(256)S(1)} %broadcast_multiply_fusion), kind=kOutput, calls=%fused_computation.33 | convolution fusion | flops 421724160 | bytes 2636288 | tf_op jit(solution)/shard_map/tc,kcd->ktd/dot_general | solution.py:44
  5.8 3.8 %collective-permute-start.1 = (bf16[2,256,320]{1,2,0:T(8,128)(2,1)}, bf16[2,256,320]{1,2,0:T(8,128)(2,1)S(1)}, u32[]{:S(2)}, u32[]{:S(2)}) collective-permute-start(bf16[2,256,320]{1,2,0:T(8,128)(2,1)} %fusion.23), channel_id=1, source_target_pairs={{0,8},{4,12},{8,16},{12,20},{16,24},{20,28},{24,32},{28,36},{32,40... | collective-permute-start | bytes 983048 | tf_op jit(solution)/shard_map/ppermute | solution.py:17
  9.6 4.8 %collective-permute-start.2 = (bf16[2,256,320]{1,2,0:T(8,128)(2,1)}, bf16[2,256,320]{1,2,0:T(8,128)(2,1)S(1)}, u32[]{:S(2)}, u32[]{:S(2)}) collective-permute-start(bf16[2,256,320]{1,2,0:T(8,128)(2,1)} %fusion.23), channel_id=1, source_target_pairs={{8,0},{12,4},{16,8},{20,12},{24,16},{28,20},{32,24},{36,28},{40,32... | collective-permute-start | bytes 983048 | tf_op jit(solution)/shard_map/ppermute | solution.py:17
  14.5 3.5 %collective-permute-start.4 = (bf16[2,256,320]{1,2,0:T(8,128)(2,1)}, bf16[2,256,320]{1,2,0:T(8,128)(2,1)S(1)}, u32[]{:S(2)}, u32[]{:S(2)}) collective-permute-start(bf16[2,256,320]{1,2,0:T(8,128)(2,1)} %fusion.23), channel_id=1, source_target_pairs={{0,16},{4,20},{8,24},{12,28},{16,32},{20,36},{24,40},{28,44},{32,4... | collective-permute-start | bytes 983048 | tf_op jit(solution)/shard_map/ppermute | solution.py:17
  18.0 1.3 %collective-permute-start.5 = (bf16[2,256,320]{1,2,0:T(8,128)(2,1)}, bf16[2,256,320]{1,2,0:T(8,128)(2,1)}, u32[]{:S(2)}, u32[]{:S(2)}) collective-permute-start(bf16[2,256,320]{1,2,0:T(8,128)(2,1)} %fusion.23), channel_id=1, source_target_pairs={{16,0},{20,4},{24,8},{28,12},{32,16},{36,20},{40,24},{44,28},{48,3... | collective-permute-start | bytes 983048 | tf_op jit(solution)/shard_map/ppermute | solution.py:17
  19.3 1.9 %collective-permute-start = (bf16[2,256,320]{1,2,0:T(8,128)(2,1)}, bf16[2,256,320]{1,2,0:T(8,128)(2,1)}, u32[]{:S(2)}, u32[]{:S(2)}) collective-permute-start(bf16[2,256,320]{1,2,0:T(8,128)(2,1)} %fusion.23), channel_id=1, source_target_pairs={{0,4},{4,0},{8,12},{12,8},{16,20},{20,16},{24,28},{28,24},{32,36},... | collective-permute-start | bytes 983048 | tf_op jit(solution)/shard_map/ppermute | solution.py:101
  21.2 1.0 fusion.108
  22.7 1.7 %fusion.42 = bf16[256,320]{0,1:T(8,128)(2,1)S(1)} fusion(bf16[3,1280,320]{1,2,0:T(8,128)(2,1)} %param.14, f32[320]{0:T(512)S(1)} %slice_reduce_fusion, bf16[256,1280]{1,0:T(8,128)(2,1)S(1)} %copy-done.1, f32[1280]{0:T(1024)S(1)} %copy-done.10, f32[1280]{0:T(1024)S(1)} %copy-done.11, f32[256]{0:T(256)S(1)} %add_rsqrt_fusion, f32[256]{0:T(256)S(1)} %broadcast_multiply_fusion), kind=kOutput, calls=%fused_computation.54 | convolution fusion | flops 211845120 | bytes 1651968 | tf_op jit(solution)/shard_map/dot_general | solution.py:40
  24.5 1.1 broadcast_compare_fusion.8
  25.8 0.4 fusion.122
  26.3 2.5 %collective-permute-start.3 = (bf16[4,256,320]{1,2,0:T(8,128)(2,1)S(1)}, bf16[4,256,320]{1,2,0:T(8,128)(2,1)S(1)}, u32[]{:S(2)}, u32[]{:S(2)}) collective-permute-start(bf16[4,256,320]{1,2,0:T(8,128)(2,1)S(1)} %pad_maximum_fusion), channel_id=1, source_target_pairs={{0,4},{4,0},{8,12},{12,8},{16,20},{20,16},{24,28},{28,24},{32,36},... | collective-permute-start | bytes 1966088 | tf_op jit(solution)/shard_map/ppermute | solution.py:101
  28.8 2.1 %collective-permute-done.4 = bf16[2,256,320]{1,2,0:T(8,128)(2,1)S(1)} collective-permute-done((bf16[2,256,320]{1,2,0:T(8,128)(2,1)}, bf16[2,256,320]{1,2,0:T(8,128)(2,1)S(1)}, u32[]{:S(2)}, u32[]{:S(2)}) %collective-permute-start.4) | collective-permute-done | bytes 327712 | tf_op jit(solution)/shard_map/ppermute | solution.py:17
  31.0 0.4 fusion.116
  31.4 0.4 fusion.119
  31.8 1.9 %collective-permute-start.6 = (bf16[2,256,320]{1,2,0:T(8,128)(2,1)S(1)}, bf16[2,256,320]{1,2,0:T(8,128)(2,1)S(1)}, u32[]{:S(2)}, u32[]{:S(2)}) collective-permute-start(bf16[2,256,320]{1,2,0:T(8,128)(2,1)S(1)} %collective-permute-done.4), channel_id=1, source_target_pairs={{0,4},{4,0},{8,12},{12,8},{16,20},{20,16},{24,28},{28,24},{32,36},... | collective-permute-start | bytes 983048 | tf_op jit(solution)/shard_map/ppermute | solution.py:101
  33.8 0.4 fusion.120
  34.1 1.0 fusion.107
  35.2 0.4 fusion.121
  35.6 2.4 %collective-permute-start.7 = (bf16[2,256,320]{1,2,0:T(8,128)(2,1)}, bf16[2,256,320]{1,2,0:T(8,128)(2,1)S(1)}, u32[]{:S(2)}, u32[]{:S(2)}) collective-permute-start(bf16[2,256,320]{1,2,0:T(8,128)(2,1)} %collective-permute-done.5), channel_id=1, source_target_pairs={{0,4},{4,0},{8,12},{12,8},{16,20},{20,16},{24,28},{28,24},{32,36},... | collective-permute-start | bytes 983048 | tf_op jit(solution)/shard_map/ppermute | solution.py:101
  37.9 1.0 fusion.112
  39.0 0.4 fusion.115
  39.4 0.4 fusion.114
  39.9 0.4 fusion.117
  40.3 0.4 fusion.118
  40.7 0.3 fusion.76
  41.0 0.3 fusion.47
  41.3 0.3 fusion.74
  41.6 0.3 fusion.72
  41.9 0.3 fusion.51
  42.2 0.3 fusion.70
  42.5 0.3 fusion.68
  42.8 0.3 fusion.55
  43.2 0.3 fusion.66
  43.6 0.3 fusion.43
  44.0 0.3 fusion.26
  44.3 0.4 fusion.39
  44.7 0.3 fusion.41
  45.2 0.2 copy.42
  45.6 1.3 %convolution_convert_fusion.1 = bf16[4,64,1280]{2,1,0:T(8,128)(2,1)} fusion(bf16[4,64,320]{2,1,0:T(8,128)(2,1)S(1)} %convert_element_type.96, bf16[320,1280]{1,0:T(8,128)(2,1)S(1)} %copy-done), kind=kOutput, calls=%fused_computation.1 | convolution fusion | flops 210042880 | bytes 1638400 | tf_op jit(solution)/shard_map/tgc,cd->tgd/dot_general | solution.py:128
  46.9 4.3 %all-to-all-start = ((bf16[4,64,1280]{2,1,0:T(8,128)(2,1)}), bf16[4,64,1280]{2,1,0:T(8,128)(2,1)S(1)}, u32[]{:S(2)}, u32[]{:S(2)}) async-start(bf16[4,64,1280]{2,1,0:T(8,128)(2,1)} %convolution_convert_fusion.1), calls=%async_computation | async-start | bytes 1310720 | tf_op jit(solution)/shard_map/all_to_all | solution.py:131
  51.6 0.3 dynamic-slice_convert_fusion
  52.0 10.7 %all-to-all-done = bf16[4,64,1280]{2,1,0:T(8,128)(2,1)S(1)} async-done(((bf16[4,64,1280]{2,1,0:T(8,128)(2,1)}), bf16[4,64,1280]{2,1,0:T(8,128)(2,1)S(1)}, u32[]{:S(2)}, u32[]{:S(2)}) %all-to-all-start) | async-done | bytes 655392 | tf_op jit(solution)/shard_map/all_to_all | solution.py:131
  63.2 0.4 convolution_convert_fusion
  63.6 0.2 all_to_all.12
  63.9 60.6 %all_to_all.17 = bf16[128,2,1280]{2,1,0:T(2,128)(2,1)S(1)} all-to-all(bf16[128,2,1280]{2,1,0:T(2,128)(2,1)S(1)} %all_to_all.12), channel_id=1, replica_groups=mesh['seq'=128,'tp'=4] {'seq'}, dimensions={0} | all-to-all | bytes 1310720 | tf_op jit(solution)/shard_map/all_to_all | solution.py:152
  124.4 1.1 all_to_all.14
  (62 shorter events, 2.4 us)
Async XLA Ops:
  0.0 45.6 %copy-start = (bf16[320,1280]{1,0:T(8,128)(2,1)S(1)}, bf16[320,1280]{1,0:T(8,128)(2,1)}, u32[]{:S(2)}) copy-start(bf16[320,1280]{1,0:T(8,128)(2,1)} %param.16) | copy-start | bytes 2457604
  0.0 2.8 %copy-start.1 = (bf16[256,1280]{1,0:T(8,128)(2,1)S(1)}, bf16[256,1280]{1,0:T(8,128)(2,1)}, u32[]{:S(2)}) copy-start(bf16[256,1280]{1,0:T(8,128)(2,1)} %param.11) | copy-start | bytes 1966084
  0.0 2.8 %copy-start.8 = (f32[3,320]{1,0:T(4,128)S(1)}, f32[3,320]{1,0:T(4,128)}, u32[]{:S(2)}) copy-start(f32[3,320]{1,0:T(4,128)} %param.15) | copy-start | bytes 11524
  0.0 2.8 %copy-start.11 = (f32[1280]{0:T(1024)S(1)}, f32[1280]{0:T(1024)}, u32[]{:S(2)}) copy-start(f32[1280]{0:T(1024)} %param.12) | copy-start | bytes 15364
  0.0 2.8 %copy-start.10 = (f32[1280]{0:T(1024)S(1)}, f32[1280]{0:T(1024)}, u32[]{:S(2)}) copy-start(f32[1280]{0:T(1024)} %param.13) | copy-start | bytes 15364
  2.9 19.4 %copy-start.4 = (s32[8192]{0:T(1024)S(1)}, s32[8192]{0:T(1024)}, u32[]{:S(2)}) copy-start(s32[8192]{0:T(1024)} %param.20) | copy-start | bytes 98308
  5.8 20.4 %collective-permute-start.1 = (bf16[2,256,320]{1,2,0:T(8,128)(2,1)}, bf16[2,256,320]{1,2,0:T(8,128)(2,1)S(1)}, u32[]{:S(2)}, u32[]{:S(2)}) collective-permute-start(bf16[2,256,320]{1,2,0:T(8,128)(2,1)} %fusion.23), channel_id=1, source_target_pairs={{0,8},{4,12},{8,16},{12,20},{16,24},{20,28},{24,32},{28,36},{32,40... | collective-permute-start | bytes 983048 | tf_op jit(solution)/shard_map/ppermute | solution.py:17
  9.6 16.6 %collective-permute-start.2 = (bf16[2,256,320]{1,2,0:T(8,128)(2,1)}, bf16[2,256,320]{1,2,0:T(8,128)(2,1)S(1)}, u32[]{:S(2)}, u32[]{:S(2)}) collective-permute-start(bf16[2,256,320]{1,2,0:T(8,128)(2,1)} %fusion.23), channel_id=1, source_target_pairs={{8,0},{12,4},{16,8},{20,12},{24,16},{28,20},{32,24},{36,28},{40,32... | collective-permute-start | bytes 983048 | tf_op jit(solution)/shard_map/ppermute | solution.py:17
  14.5 16.5 %collective-permute-start.4 = (bf16[2,256,320]{1,2,0:T(8,128)(2,1)}, bf16[2,256,320]{1,2,0:T(8,128)(2,1)S(1)}, u32[]{:S(2)}, u32[]{:S(2)}) collective-permute-start(bf16[2,256,320]{1,2,0:T(8,128)(2,1)} %fusion.23), channel_id=1, source_target_pairs={{0,16},{4,20},{8,24},{12,28},{16,32},{20,36},{24,40},{28,44},{32,4... | collective-permute-start | bytes 983048 | tf_op jit(solution)/shard_map/ppermute | solution.py:17
  18.0 17.6 %collective-permute-start.5 = (bf16[2,256,320]{1,2,0:T(8,128)(2,1)}, bf16[2,256,320]{1,2,0:T(8,128)(2,1)}, u32[]{:S(2)}, u32[]{:S(2)}) collective-permute-start(bf16[2,256,320]{1,2,0:T(8,128)(2,1)} %fusion.23), channel_id=1, source_target_pairs={{16,0},{20,4},{24,8},{28,12},{32,16},{36,20},{40,24},{44,28},{48,3... | collective-permute-start | bytes 983048 | tf_op jit(solution)/shard_map/ppermute | solution.py:17
  19.3 14.9 %collective-permute-start = (bf16[2,256,320]{1,2,0:T(8,128)(2,1)}, bf16[2,256,320]{1,2,0:T(8,128)(2,1)}, u32[]{:S(2)}, u32[]{:S(2)}) collective-permute-start(bf16[2,256,320]{1,2,0:T(8,128)(2,1)} %fusion.23), channel_id=1, source_target_pairs={{0,4},{4,0},{8,12},{12,8},{16,20},{20,16},{24,28},{28,24},{32,36},... | collective-permute-start | bytes 983048 | tf_op jit(solution)/shard_map/ppermute | solution.py:101
  22.7 2.9 %copy-start.9 = (s32[64,1]{0,1:T(1,128)S(1)}, s32[64,1]{0,1:T(1,128)}, u32[]{:S(2)}) copy-start(s32[64,1]{0,1:T(1,128)} %param.21) | copy-start | bytes 772
  26.1 4.8 %copy-start.3 = (pred[256,256]{0,1:T(8,128)(4,1)S(1)}, pred[256,256]{0,1:T(8,128)(4,1)}, u32[]{:S(2)}) copy-start(pred[256,256]{0,1:T(8,128)(4,1)} %get-tuple-element.58) | copy-start | bytes 196612
  26.2 5.1 %copy-start.2 = (pred[256,256]{0,1:T(8,128)(4,1)S(1)}, pred[256,256]{0,1:T(8,128)(4,1)}, u32[]{:S(2)}) copy-start(pred[256,256]{0,1:T(8,128)(4,1)} %get-tuple-element.55) | copy-start | bytes 196612
  26.3 13.6 %collective-permute-start.3 = (bf16[4,256,320]{1,2,0:T(8,128)(2,1)S(1)}, bf16[4,256,320]{1,2,0:T(8,128)(2,1)S(1)}, u32[]{:S(2)}, u32[]{:S(2)}) collective-permute-start(bf16[4,256,320]{1,2,0:T(8,128)(2,1)S(1)} %pad_maximum_fusion), channel_id=1, source_target_pairs={{0,4},{4,0},{8,12},{12,8},{16,20},{20,16},{24,28},{28,24},{32,36},... | collective-permute-start | bytes 1966088 | tf_op jit(solution)/shard_map/ppermute | solution.py:101
  31.8 7.6 %collective-permute-start.6 = (bf16[2,256,320]{1,2,0:T(8,128)(2,1)S(1)}, bf16[2,256,320]{1,2,0:T(8,128)(2,1)S(1)}, u32[]{:S(2)}, u32[]{:S(2)}) collective-permute-start(bf16[2,256,320]{1,2,0:T(8,128)(2,1)S(1)} %collective-permute-done.4), channel_id=1, source_target_pairs={{0,4},{4,0},{8,12},{12,8},{16,20},{20,16},{24,28},{28,24},{32,36},... | collective-permute-start | bytes 983048 | tf_op jit(solution)/shard_map/ppermute | solution.py:101
  35.6 3.8 %collective-permute-start.7 = (bf16[2,256,320]{1,2,0:T(8,128)(2,1)}, bf16[2,256,320]{1,2,0:T(8,128)(2,1)S(1)}, u32[]{:S(2)}, u32[]{:S(2)}) collective-permute-start(bf16[2,256,320]{1,2,0:T(8,128)(2,1)} %collective-permute-done.5), channel_id=1, source_target_pairs={{0,4},{4,0},{8,12},{12,8},{16,20},{20,16},{24,28},{28,24},{32,36},... | collective-permute-start | bytes 983048 | tf_op jit(solution)/shard_map/ppermute | solution.py:101
  46.9 15.8 %all-to-all-start = ((bf16[4,64,1280]{2,1,0:T(8,128)(2,1)}), bf16[4,64,1280]{2,1,0:T(8,128)(2,1)S(1)}, u32[]{:S(2)}, u32[]{:S(2)}) async-start(bf16[4,64,1280]{2,1,0:T(8,128)(2,1)} %convolution_convert_fusion.1), calls=%async_computation | async-start | bytes 1310720 | tf_op jit(solution)/shard_map/all_to_all | solution.py:131
  51.4 11.4 %copy-start.5 = (f32[1280]{0:T(1024)S(1)}, f32[1280]{0:T(1024)}, u32[]{:S(2)}) copy-start(f32[1280]{0:T(1024)} %param.17) | copy-start | bytes 15364
  51.9 11.2 %copy-start.6 = (f32[1280]{0:T(1024)S(1)}, f32[1280]{0:T(1024)}, u32[]{:S(2)}) copy-start(f32[1280]{0:T(1024)} %param.19) | copy-start | bytes 15364
  52.0 11.2 %copy-start.7 = (f32[1280]{0:T(1024)S(1)}, f32[1280]{0:T(1024)}, u32[]{:S(2)}) copy-start(f32[1280]{0:T(1024)} %param.18) | copy-start | bytes 15364

commit v12 on v8

--- a/solution.py
+++ b/solution.py
@@ -109,13 +109,14 @@
     above_4 = from_behind(key_value, "seq", -4)
     partner_own = swap(key_value)
     state = absorb(start_state, key_value, query_segment)
-    partner_near = swap(jnp.concatenate([below_2, above_2], axis=0))
+    partner_below_2 = swap(below_2)
+    partner_above_2 = swap(above_2)
     partner_far = swap(jnp.where(sign > 0, above_4, below_4))
     state = absorb_at(state, partner_own, sign)
     state = absorb_at(state, below_2, -2)
     state = absorb_at(state, above_2, 2)
-    state = absorb_at(state, partner_near[:2], sign - 2)
-    state = absorb_at(state, partner_near[2:], sign + 2)
+    state = absorb_at(state, partner_below_2, sign - 2)
+    state = absorb_at(state, partner_above_2, sign + 2)
     state = absorb_at(state, below_4, -4)
     state = absorb_at(state, above_4, 4)
     state = absorb_at(state, partner_far, -3 * sign)

time: 126 us -> 130 us (1.032)
  waiting for transfers between devices: 11.2 us -> 16.4 us
  other arithmetic: 8.56 us -> 6.52 us
  starting transfers between devices: 26.1 us -> 27.8 us
    ppermute x4, waiting for transfers between devices: 0.32 us -> 5.31 us  [from_behind(): lax.ppermute(value, axis, [(source, source + steps) for source in range(l...]
    ppermute x3 -> x4, starting transfers between devices: 6.39 us -> 8.3 us  [swap(): return lax.ppermute(value, 'seq', [(i, i ^ 1) for i in range(seq_count)])]
    another operation x1, other arithmetic: 1.43 us -> 0.1 us  [per_device(): earlier = jnp.cumsum(owner_table, axis=0) - owner_table]
    slice x7 -> x8, local copies, waits for them, and re-layouts: 2.83 us -> 3.18 us  [block_scores(): value_heads = block[1].reshape(-1, local_heads, HEAD_DIM)]
  transfers between devices with their start and end apart: 8 -> 9, of which waited for: 2 -> 3; matrix products, arithmetic and copies ran while one was open for 10% -> 8% of each run, Pallas kernels for 0% -> 0%
where the time goes in v12:
time: 130 us
  blocking collectives  60.2 us (46%)
  starting transfers between devices  27.8 us (21%)
  waiting for transfers between devices  16.4 us (13%)
  matrix products  12.5 us (10%)
  other arithmetic  6.52 us (5%)
  local copies, waits for them, and re-layouts  5.76 us (4%)
    all_to_all x1, blocking collectives, per_device(): lax.all_to_all(outgoing, 'seq', split_axis=0, concat_axis=0, tiled=True)  60.2 us
    ppermute x4, starting transfers between devices, from_behind(): lax.ppermute(value, axis, [(source, source + steps) for source in range(l...  16 us
    all_to_all x1, waiting for transfers between devices, per_device(): lax.all_to_all(head_term, 'tp', split_axis=0, concat_axis=0, tiled=True)  11.1 us
    ppermute x4, starting transfers between devices, swap(): return lax.ppermute(value, 'seq', [(i, i ^ 1) for i in range(seq_count)])  8.3 us
    ppermute x4, waiting for transfers between devices, from_behind(): lax.ppermute(value, axis, [(source, source + steps) for source in range(l...  5.31 us
    all_to_all x1, starting transfers between devices, per_device(): lax.all_to_all(head_term, 'tp', split_axis=0, concat_axis=0, tiled=True)  3.48 us
    dot_general x9, matrix products, block_scores(): jnp.einsum('qhd,khd->hqk', query_heads, key_heads, preferred_element_type...  3.4 us
    slice x8, local copies, waits for them, and re-layouts, block_scores(): value_heads = block[1].reshape(-1, local_heads, HEAD_DIM)  3.18 us
  transfers between devices with their start and end apart: 9, of which 3 were waited for; matrix products, arithmetic and copies ran while one was open for 8% of the time, Pallas kernels for 0%

profile of v12, /device:TPU:32, one launch (start us, length us, event | category | flops | bytes accessed | tf_op | source)
XLA Modules:
  0.0 129.7 jit_solution(1595765497005378309)
XLA Ops:
  0.0 1.4 %convert_reduce_fusion = f32[256]{0:T(256)S(1)} fusion(bf16[256,1280]{1,0:T(8,128)(2,1)} %param.11), kind=kLoop, calls=%fused_computation.5 | loop fusion | flops 655104 | bytes 656384 | tf_op jit(solution)/shard_map/reduce_sum | solution.py:21
  1.4 1.4 %fusion.13 = f32[256]{0:T(256)S(1)} fusion(bf16[256,1280]{1,0:T(8,128)(2,1)} %param.11, f32[256]{0:T(256)S(1)} %broadcast_multiply_fusion), kind=kLoop, calls=%fused_computation.26 | loop fusion | flops 1310464 | bytes 657408 | tf_op jit(solution)/shard_map/reduce_sum | solution.py:23
  2.9 2.9 %fusion.23 = bf16[2,256,320]{1,2,0:T(8,128)(2,1)} fusion(bf16[3,1280,320]{1,2,0:T(8,128)(2,1)} %param.14, f32[2,320]{1,0:T(2,128)S(1)} %slice.73, bf16[256,1280]{1,0:T(8,128)(2,1)S(1)} %copy-done.1, f32[1280]{0:T(1024)S(1)} %copy-done.10, f32[1280]{0:T(1024)S(1)} %copy-done.11, f32[256]{0:T(256)S(1)} %add_rsqrt_fusion, f32[256]{0:T(256)S(1)} %broadcast_multiply_fusion), kind=kOutput, calls=%fused_computation.33 | convolution fusion | flops 421724160 | bytes 2636288 | tf_op jit(solution)/shard_map/tc,kcd->ktd/dot_general | solution.py:44
  5.8 7.3 %collective-permute-start.2 = (bf16[2,256,320]{1,2,0:T(8,128)(2,1)}, bf16[2,256,320]{1,2,0:T(8,128)(2,1)}, u32[]{:S(2)}, u32[]{:S(2)}) collective-permute-start(bf16[2,256,320]{1,2,0:T(8,128)(2,1)} %fusion.23), channel_id=1, source_target_pairs={{8,0},{12,4},{16,8},{20,12},{24,16},{28,20},{32,24},{36,28},{40,32... | collective-permute-start | bytes 983048 | tf_op jit(solution)/shard_map/ppermute | solution.py:17
  13.2 1.9 %collective-permute-start.1 = (bf16[2,256,320]{1,2,0:T(8,128)(2,1)}, bf16[2,256,320]{1,2,0:T(8,128)(2,1)S(1)}, u32[]{:S(2)}, u32[]{:S(2)}) collective-permute-start(bf16[2,256,320]{1,2,0:T(8,128)(2,1)} %fusion.23), channel_id=1, source_target_pairs={{0,8},{4,12},{8,16},{12,20},{16,24},{20,28},{24,32},{28,36},{32,40... | collective-permute-start | bytes 983048 | tf_op jit(solution)/shard_map/ppermute | solution.py:17
  15.1 1.3 collective-permute-start.6
  16.4 5.5 %collective-permute-start.5 = (bf16[2,256,320]{1,2,0:T(8,128)(2,1)}, bf16[2,256,320]{1,2,0:T(8,128)(2,1)S(1)}, u32[]{:S(2)}, u32[]{:S(2)}) collective-permute-start(bf16[2,256,320]{1,2,0:T(8,128)(2,1)} %fusion.23), channel_id=1, source_target_pairs={{0,16},{4,20},{8,24},{12,28},{16,32},{20,36},{24,40},{28,44},{32,4... | collective-permute-start | bytes 983048 | tf_op jit(solution)/shard_map/ppermute | solution.py:17
  21.9 1.9 %collective-permute-start = (bf16[2,256,320]{1,2,0:T(8,128)(2,1)}, bf16[2,256,320]{1,2,0:T(8,128)(2,1)}, u32[]{:S(2)}, u32[]{:S(2)}) collective-permute-start(bf16[2,256,320]{1,2,0:T(8,128)(2,1)} %fusion.23), channel_id=1, source_target_pairs={{0,4},{4,0},{8,12},{12,8},{16,20},{20,16},{24,28},{28,24},{32,36},... | collective-permute-start | bytes 983048 | tf_op jit(solution)/shard_map/ppermute | solution.py:101
  23.8 1.0 fusion.107
  25.3 1.7 %fusion.42 = bf16[256,320]{0,1:T(8,128)(2,1)S(1)} fusion(bf16[3,1280,320]{1,2,0:T(8,128)(2,1)} %param.14, f32[320]{0:T(512)S(1)} %slice_reduce_fusion, bf16[256,1280]{1,0:T(8,128)(2,1)S(1)} %copy-done.1, f32[1280]{0:T(1024)S(1)} %copy-done.10, f32[1280]{0:T(1024)S(1)} %copy-done.11, f32[256]{0:T(256)S(1)} %add_rsqrt_fusion, f32[256]{0:T(256)S(1)} %broadcast_multiply_fusion), kind=kOutput, calls=%fused_computation.54 | convolution fusion | flops 211845120 | bytes 1651968 | tf_op jit(solution)/shard_map/dot_general | solution.py:40
  27.1 1.1 broadcast_compare_fusion.8
  28.4 0.4 fusion.123
  28.7 1.5 %collective-permute-done.6 = bf16[2,256,320]{1,2,0:T(8,128)(2,1)S(1)} collective-permute-done((bf16[2,256,320]{1,2,0:T(8,128)(2,1)}, bf16[2,256,320]{1,2,0:T(8,128)(2,1)S(1)}, u32[]{:S(2)}, u32[]{:S(2)}) %collective-permute-start.6) | collective-permute-done | bytes 327712 | tf_op jit(solution)/shard_map/ppermute | solution.py:17
  30.2 3.8 %collective-permute-done.5 = bf16[2,256,320]{1,2,0:T(8,128)(2,1)S(1)} collective-permute-done((bf16[2,256,320]{1,2,0:T(8,128)(2,1)}, bf16[2,256,320]{1,2,0:T(8,128)(2,1)S(1)}, u32[]{:S(2)}, u32[]{:S(2)}) %collective-permute-start.5) | collective-permute-done | bytes 327712 | tf_op jit(solution)/shard_map/ppermute | solution.py:17
  34.1 2.1 %collective-permute-start.7 = (bf16[2,256,320]{1,2,0:T(8,128)(2,1)S(1)}, bf16[2,256,320]{1,2,0:T(8,128)(2,1)S(1)}, u32[]{:S(2)}, u32[]{:S(2)}) collective-permute-start(bf16[2,256,320]{1,2,0:T(8,128)(2,1)S(1)} %broadcast_select_fusion), channel_id=1, source_target_pairs={{0,4},{4,0},{8,12},{12,8},{16,20},{20,16},{24,28},{28,24},{32,36},... | collective-permute-start | bytes 983048 | tf_op jit(solution)/shard_map/ppermute | solution.py:101
  36.2 0.4 fusion.116
  36.6 0.4 fusion.117
  37.0 2.4 %collective-permute-start.4 = (bf16[2,256,320]{1,2,0:T(8,128)(2,1)}, bf16[2,256,320]{1,2,0:T(8,128)(2,1)S(1)}, u32[]{:S(2)}, u32[]{:S(2)}) collective-permute-start(bf16[2,256,320]{1,2,0:T(8,128)(2,1)} %collective-permute-done.2), channel_id=1, source_target_pairs={{0,4},{4,0},{8,12},{12,8},{16,20},{20,16},{24,28},{28,24},{32,36},... | collective-permute-start | bytes 983048 | tf_op jit(solution)/shard_map/ppermute | solution.py:101
  39.4 1.0 fusion.109
  40.5 0.4 fusion.120
  40.8 1.9 %collective-permute-start.3 = (bf16[2,256,320]{1,2,0:T(8,128)(2,1)S(1)}, bf16[2,256,320]{1,2,0:T(8,128)(2,1)S(1)}, u32[]{:S(2)}, u32[]{:S(2)}) collective-permute-start(bf16[2,256,320]{1,2,0:T(8,128)(2,1)S(1)} %collective-permute-done.1), channel_id=1, source_target_pairs={{0,4},{4,0},{8,12},{12,8},{16,20},{20,16},{24,28},{28,24},{32,36},... | collective-permute-start | bytes 983048 | tf_op jit(solution)/shard_map/ppermute | solution.py:101
  42.8 0.4 fusion.121
  43.2 1.0 fusion.106
  44.2 0.4 fusion.122
  44.6 0.4 fusion.118
  45.1 0.4 fusion.119
  45.5 0.4 fusion.115
  45.9 0.3 fusion.76
  46.2 0.3 fusion.47
  46.5 0.3 fusion.74
  46.8 0.3 fusion.69
  47.1 0.3 fusion.55
  47.4 0.3 fusion.67
  47.9 0.3 fusion.65
  48.2 0.3 fusion.71
  48.5 0.3 fusion.51
  48.8 0.3 fusion.43
  49.1 0.3 fusion.26
  49.5 0.3 fusion.31
  49.8 0.4 fusion.41
  50.7 1.3 %convolution_convert_fusion.1 = bf16[4,64,1280]{2,1,0:T(8,128)(2,1)} fusion(bf16[4,64,320]{2,1,0:T(8,128)(2,1)S(1)} %convert_element_type.96, bf16[320,1280]{1,0:T(8,128)(2,1)S(1)} %copy-done), kind=kOutput, calls=%fused_computation.1 | convolution fusion | flops 210042880 | bytes 1638400 | tf_op jit(solution)/shard_map/tgc,cd->tgd/dot_general | solution.py:128
  52.1 3.5 %all-to-all-start = ((bf16[4,64,1280]{2,1,0:T(8,128)(2,1)}), bf16[4,64,1280]{2,1,0:T(8,128)(2,1)S(1)}, u32[]{:S(2)}, u32[]{:S(2)}) async-start(bf16[4,64,1280]{2,1,0:T(8,128)(2,1)} %convolution_convert_fusion.1), calls=%async_computation | async-start | bytes 1310720 | tf_op jit(solution)/shard_map/all_to_all | solution.py:131
  55.9 0.3 dynamic-slice_convert_fusion
  56.3 11.1 %all-to-all-done = bf16[4,64,1280]{2,1,0:T(8,128)(2,1)S(1)} async-done(((bf16[4,64,1280]{2,1,0:T(8,128)(2,1)}), bf16[4,64,1280]{2,1,0:T(8,128)(2,1)S(1)}, u32[]{:S(2)}, u32[]{:S(2)}) %all-to-all-start) | async-done | bytes 655392 | tf_op jit(solution)/shard_map/all_to_all | solution.py:131
  67.8 0.4 convolution_convert_fusion
  68.2 0.2 all_to_all.12
  68.5 60.2 %all_to_all.17 = bf16[128,2,1280]{2,1,0:T(2,128)(2,1)S(1)} all-to-all(bf16[128,2,1280]{2,1,0:T(2,128)(2,1)S(1)} %all_to_all.12), channel_id=1, replica_groups=mesh['seq'=128,'tp'=4] {'seq'}, dimensions={0} | all-to-all | bytes 1310720 | tf_op jit(solution)/shard_map/all_to_all | solution.py:152
  128.6 1.1 all_to_all.14
  (62 shorter events, 2.5 us)
Async XLA Ops:
  0.0 50.7 %copy-start = (bf16[320,1280]{1,0:T(8,128)(2,1)S(1)}, bf16[320,1280]{1,0:T(8,128)(2,1)}, u32[]{:S(2)}) copy-start(bf16[320,1280]{1,0:T(8,128)(2,1)} %param.16) | copy-start | bytes 2457604
  0.0 2.8 %copy-start.1 = (bf16[256,1280]{1,0:T(8,128)(2,1)S(1)}, bf16[256,1280]{1,0:T(8,128)(2,1)}, u32[]{:S(2)}) copy-start(bf16[256,1280]{1,0:T(8,128)(2,1)} %param.11) | copy-start | bytes 1966084
  0.0 2.8 %copy-start.8 = (f32[3,320]{1,0:T(4,128)S(1)}, f32[3,320]{1,0:T(4,128)}, u32[]{:S(2)}) copy-start(f32[3,320]{1,0:T(4,128)} %param.15) | copy-start | bytes 11524
  0.0 2.8 %copy-start.11 = (f32[1280]{0:T(1024)S(1)}, f32[1280]{0:T(1024)}, u32[]{:S(2)}) copy-start(f32[1280]{0:T(1024)} %param.12) | copy-start | bytes 15364
  0.0 2.8 %copy-start.10 = (f32[1280]{0:T(1024)S(1)}, f32[1280]{0:T(1024)}, u32[]{:S(2)}) copy-start(f32[1280]{0:T(1024)} %param.13) | copy-start | bytes 15364
  2.9 22.0 %copy-start.4 = (s32[8192]{0:T(1024)S(1)}, s32[8192]{0:T(1024)}, u32[]{:S(2)}) copy-start(s32[8192]{0:T(1024)} %param.20) | copy-start | bytes 98308
  5.8 31.2 %collective-permute-start.2 = (bf16[2,256,320]{1,2,0:T(8,128)(2,1)}, bf16[2,256,320]{1,2,0:T(8,128)(2,1)}, u32[]{:S(2)}, u32[]{:S(2)}) collective-permute-start(bf16[2,256,320]{1,2,0:T(8,128)(2,1)} %fusion.23), channel_id=1, source_target_pairs={{8,0},{12,4},{16,8},{20,12},{24,16},{28,20},{32,24},{36,28},{40,32... | collective-permute-start | bytes 983048 | tf_op jit(solution)/shard_map/ppermute | solution.py:17
  13.2 27.7 %collective-permute-start.1 = (bf16[2,256,320]{1,2,0:T(8,128)(2,1)}, bf16[2,256,320]{1,2,0:T(8,128)(2,1)S(1)}, u32[]{:S(2)}, u32[]{:S(2)}) collective-permute-start(bf16[2,256,320]{1,2,0:T(8,128)(2,1)} %fusion.23), channel_id=1, source_target_pairs={{0,8},{4,12},{8,16},{12,20},{16,24},{20,28},{24,32},{28,36},{32,40... | collective-permute-start | bytes 983048 | tf_op jit(solution)/shard_map/ppermute | solution.py:17
  15.1 15.2 %collective-permute-start.6 = (bf16[2,256,320]{1,2,0:T(8,128)(2,1)}, bf16[2,256,320]{1,2,0:T(8,128)(2,1)S(1)}, u32[]{:S(2)}, u32[]{:S(2)}) collective-permute-start(bf16[2,256,320]{1,2,0:T(8,128)(2,1)} %fusion.23), channel_id=1, source_target_pairs={{16,0},{20,4},{24,8},{28,12},{32,16},{36,20},{40,24},{44,28},{48,3... | collective-permute-start | bytes 983048 | tf_op jit(solution)/shard_map/ppermute | solution.py:17
  16.4 17.7 %collective-permute-start.5 = (bf16[2,256,320]{1,2,0:T(8,128)(2,1)}, bf16[2,256,320]{1,2,0:T(8,128)(2,1)S(1)}, u32[]{:S(2)}, u32[]{:S(2)}) collective-permute-start(bf16[2,256,320]{1,2,0:T(8,128)(2,1)} %fusion.23), channel_id=1, source_target_pairs={{0,16},{4,20},{8,24},{12,28},{16,32},{20,36},{24,40},{28,44},{32,4... | collective-permute-start | bytes 983048 | tf_op jit(solution)/shard_map/ppermute | solution.py:17
  21.9 21.3 %collective-permute-start = (bf16[2,256,320]{1,2,0:T(8,128)(2,1)}, bf16[2,256,320]{1,2,0:T(8,128)(2,1)}, u32[]{:S(2)}, u32[]{:S(2)}) collective-permute-start(bf16[2,256,320]{1,2,0:T(8,128)(2,1)} %fusion.23), channel_id=1, source_target_pairs={{0,4},{4,0},{8,12},{12,8},{16,20},{20,16},{24,28},{28,24},{32,36},... | collective-permute-start | bytes 983048 | tf_op jit(solution)/shard_map/ppermute | solution.py:101
  25.3 2.9 %copy-start.9 = (s32[64,1]{0,1:T(1,128)S(1)}, s32[64,1]{0,1:T(1,128)}, u32[]{:S(2)}) copy-start(s32[64,1]{0,1:T(1,128)} %param.21) | copy-start | bytes 772
  28.4 7.8 %copy-start.3 = (pred[256,256]{0,1:T(8,128)(4,1)S(1)}, pred[256,256]{0,1:T(8,128)(4,1)}, u32[]{:S(2)}) copy-start(pred[256,256]{0,1:T(8,128)(4,1)} %get-tuple-element.59) | copy-start | bytes 196612
  34.1 2.5 %copy-start.2 = (pred[256,256]{0,1:T(8,128)(4,1)S(1)}, pred[256,256]{0,1:T(8,128)(4,1)}, u32[]{:S(2)}) copy-start(pred[256,256]{0,1:T(8,128)(4,1)} %get-tuple-element.58) | copy-start | bytes 196612
  34.1 11.3 %collective-permute-start.7 = (bf16[2,256,320]{1,2,0:T(8,128)(2,1)S(1)}, bf16[2,256,320]{1,2,0:T(8,128)(2,1)S(1)}, u32[]{:S(2)}, u32[]{:S(2)}) collective-permute-start(bf16[2,256,320]{1,2,0:T(8,128)(2,1)S(1)} %broadcast_select_fusion), channel_id=1, source_target_pairs={{0,4},{4,0},{8,12},{12,8},{16,20},{20,16},{24,28},{28,24},{32,36},... | collective-permute-start | bytes 983048 | tf_op jit(solution)/shard_map/ppermute | solution.py:101
  37.0 7.6 %collective-permute-start.4 = (bf16[2,256,320]{1,2,0:T(8,128)(2,1)}, bf16[2,256,320]{1,2,0:T(8,128)(2,1)S(1)}, u32[]{:S(2)}, u32[]{:S(2)}) collective-permute-start(bf16[2,256,320]{1,2,0:T(8,128)(2,1)} %collective-permute-done.2), channel_id=1, source_target_pairs={{0,4},{4,0},{8,12},{12,8},{16,20},{20,16},{24,28},{28,24},{32,36},... | collective-permute-start | bytes 983048 | tf_op jit(solution)/shard_map/ppermute | solution.py:101
  40.8 4.2 %collective-permute-start.3 = (bf16[2,256,320]{1,2,0:T(8,128)(2,1)S(1)}, bf16[2,256,320]{1,2,0:T(8,128)(2,1)S(1)}, u32[]{:S(2)}, u32[]{:S(2)}) collective-permute-start(bf16[2,256,320]{1,2,0:T(8,128)(2,1)S(1)} %collective-permute-done.1), channel_id=1, source_target_pairs={{0,4},{4,0},{8,12},{12,8},{16,20},{20,16},{24,28},{28,24},{32,36},... | collective-permute-start | bytes 983048 | tf_op jit(solution)/shard_map/ppermute | solution.py:101
  52.1 15.3 %all-to-all-start = ((bf16[4,64,1280]{2,1,0:T(8,128)(2,1)}), bf16[4,64,1280]{2,1,0:T(8,128)(2,1)S(1)}, u32[]{:S(2)}, u32[]{:S(2)}) async-start(bf16[4,64,1280]{2,1,0:T(8,128)(2,1)} %convolution_convert_fusion.1), calls=%async_computation | async-start | bytes 1310720 | tf_op jit(solution)/shard_map/all_to_all | solution.py:131
  55.7 11.7 %copy-start.5 = (f32[1280]{0:T(1024)S(1)}, f32[1280]{0:T(1024)}, u32[]{:S(2)}) copy-start(f32[1280]{0:T(1024)} %param.17) | copy-start | bytes 15364
  56.2 11.6 %copy-start.6 = (f32[1280]{0:T(1024)S(1)}, f32[1280]{0:T(1024)}, u32[]{:S(2)}) copy-start(f32[1280]{0:T(1024)} %param.19) | copy-start | bytes 15364
  56.2 11.6 %copy-start.7 = (f32[1280]{0:T(1024)S(1)}, f32[1280]{0:T(1024)}, u32[]{:S(2)}) copy-start(f32[1280]{0:T(1024)} %param.18) | copy-start | bytes 15364
